TPU v7x, 512 devices: a whole 4x8x8 slice. The times are simulated.
512 devices in a mesh: blk: 32 (over z_hi, x, core), head: 16 (over y, z_lo).
Axes of the slice: x: 4, y: 8, z: 8 (z_hi: 4, z_lo: 2; z = z_hi * 2 + z_lo), core: 2. Of those that a mesh axis runs over, the one named last changes fastest.
Arguments:
- query_rows: bfloat16 [65536, 1024], P(('blk', 'head')), may hold values from -6 to 6
- key_rows: bfloat16 [65536, 1024], P(('blk', 'head')), may hold values from -6 to 6
- value_rows: bfloat16 [65536, 1024], P(('blk', 'head')), may hold values from -6 to 6
- out_grad: bfloat16 [65536, 1024], P(('blk', 'head')), may hold values from -6 to 6
- neighbour_blocks: int32 [128, 2], replicated, may hold values from 0 to 3
Outputs:
- attended: bfloat16 [65536, 1024], P(('blk', 'head'))
- query_grad: bfloat16 [65536, 1024], P(('blk', 'head'))
- key_grad: bfloat16 [65536, 1024], P(('blk', 'head'))
- value_grad: bfloat16 [65536, 1024], P(('blk', 'head'))
Inputs may be any that keep to these rules, and one draw needn't show every extreme that they name: neighbour_blocks[g, 0] and neighbour_blocks[g, 1] number a block within the previous and the next segment, counted from that segment's first block.
All inputs are finite; a program needn't handle non-finite values.
Results may differ from a plain program's by a relative error of at most 0.012.
The roundings to bfloat16 on the way count: a program that leaves them out, or rounds other values in their place, can miss the bound.
Values may be sent and summed in bfloat16 or wider, within the bound.
No kernel may reach another device: no remote copies, remote signals or barrier semaphores. Data moves between devices by JAX's collectives and lax.ppermute only.
A program may use at most 64 MiB of HBM per device.

v0:
```python
import jax
import jax.numpy as jnp
from jax import lax
from jax.sharding import PartitionSpec as P

HEAD_DIM = 64
BLOCK = 512


def extended(x, sides, width):
    for axis, dim in sides:
        count, length = (lax.axis_size(axis), x.shape[dim])
        up = [(i, (i + 1) % count) for i in range(count)]
        down = [(j, i) for i, j in up]
        last = lax.slice_in_dim(x, length - width, length, axis=dim)
        leading = lax.slice_in_dim(x, 0, width, axis=dim)
        before = lax.ppermute(last, axis, up)
        after = lax.ppermute(leading, axis, down)
        x = jnp.concatenate([before, x, after], axis=dim)
    return x


def shortened(x):
    return jax.tree.map(lambda a: a.astype(jnp.bfloat16) if a.dtype == jnp.float32 else a, x)


def from_behind(value, axis, steps):
    count = lax.axis_size(axis)
    pairs = [(source, (source + steps) % count) for source in range(count)]
    return lax.ppermute(value, axis, pairs)


def scaled_scores(query_block, key_block):
    product = jnp.einsum("qgd,kgd->gqk", query_block, key_block, preferred_element_type=jnp.float32)
    return product * HEAD_DIM ** (-0.5)


def forward_block(query_block, key_block, value_block, allowed):
    scores = jnp.where(allowed[None], scaled_scores(query_block, key_block), -jnp.inf)
    highest = jnp.max(scores, axis=2, keepdims=True)
    log_total = highest + jnp.log(jnp.sum(jnp.exp(scores - highest), axis=2, keepdims=True))
    weights = jnp.exp(scores - log_total).astype(jnp.bfloat16)
    attended = jnp.einsum("gqk,kgd->qgd", weights, value_block, preferred_element_type=jnp.float32)
    return (attended.astype(jnp.bfloat16), log_total[:, :, 0])


def gradient_block(query_block, grad_block, log_total, row_delta, key_block, value_block, allowed):
    weights = jnp.exp(scaled_scores(query_block, key_block) - log_total[:, :, None])
    weights = jnp.where(allowed[None], weights, 0.0)
    weight_grad = jnp.einsum(
        "qgd,kgd->gqk", grad_block, value_block, preferred_element_type=jnp.float32
    )
    score_grad = (weights * (weight_grad - row_delta[:, :, None])).astype(jnp.bfloat16)
    factor = HEAD_DIM ** (-0.5)
    results = []
    results.append(
        jnp.einsum("gqk,kgd->qgd", score_grad, key_block, preferred_element_type=jnp.float32)
        * factor
    )
    key_part = (
        jnp.einsum("gqk,qgd->kgd", score_grad, query_block, preferred_element_type=jnp.float32)
        * factor
    )
    value_part = jnp.einsum(
        "gqk,qgd->kgd", weights.astype(jnp.bfloat16), grad_block, preferred_element_type=jnp.float32
    )
    results.append(jnp.stack([key_part, value_part], axis=1))
    return tuple(results)


def shards(query_rows, key_rows, value_rows, out_grad, neighbour_blocks):
    query_heads, key_heads, value_heads, grad_heads = (
        lax.all_to_all(query_rows, "head", split_axis=1, concat_axis=0, tiled=True),
        lax.all_to_all(key_rows, "head", split_axis=1, concat_axis=0, tiled=True),
        lax.all_to_all(value_rows, "head", split_axis=1, concat_axis=0, tiled=True),
        lax.all_to_all(out_grad, "head", split_axis=1, concat_axis=0, tiled=True),
    )
    row_count = query_heads.shape[0]
    feature_count = query_heads.shape[1]
    head_count = feature_count // HEAD_DIM
    block_count = row_count // BLOCK
    cycle_size = lax.axis_size("blk")
    cycle_place = lax.axis_index("blk")
    block_range = jnp.arange(block_count, dtype=jnp.int32)

    def split_blocks(source):
        return source.reshape(block_count, BLOCK, head_count, HEAD_DIM)

    def split_pairs(source):
        return source.reshape(block_count, BLOCK, 2, head_count, HEAD_DIM)

    def picks_of(column):
        first_row = cycle_place % cycle_size * block_count
        return lax.dynamic_slice_in_dim(neighbour_blocks[:, column], first_row, block_count, 0)

    def route(picked, pieces):
        onehot = (picked[None, :] == block_range[:, None]).astype(jnp.float32)
        summed = jnp.dot(onehot, pieces.reshape(block_count, -1), precision=lax.Precision.HIGHEST)
        return summed.reshape(row_count, -1)

    paired = jnp.concatenate([key_heads, value_heads], axis=1)
    key_window = extended(paired, (("blk", 0),), row_count)
    own_pairs = split_pairs(paired)
    left_pairs = split_pairs(key_window[:row_count])
    right_pairs = split_pairs(key_window[2 * row_count :])
    left_picks = picks_of(0)
    right_picks = picks_of(1)
    positions = jnp.arange(BLOCK, dtype=jnp.int32)
    causal = positions[None, :] <= positions[:, None]
    allowed = jnp.concatenate([causal, jnp.ones((BLOCK, 2 * BLOCK), dtype=bool)], axis=1)
    query_blocks = split_blocks(query_heads)
    grad_blocks = split_blocks(grad_heads)

    def key_set(number):
        stacked = jnp.concatenate(
            [own_pairs[number], left_pairs[left_picks[number]], right_pairs[right_picks[number]]],
            axis=0,
        )
        return (stacked[:, 0], stacked[:, 1])

    def forward_one(number):
        key_block, value_block = key_set(number)
        return forward_block(query_blocks[number], key_block, value_block, allowed)

    out_blocks, log_totals = lax.map(forward_one, block_range)
    attended_heads = out_blocks.reshape(row_count, feature_count)
    row_deltas = jnp.sum(
        grad_blocks.astype(jnp.float32) * out_blocks.astype(jnp.float32), axis=3
    ).transpose(0, 2, 1)

    def backward_one(number):
        key_block, value_block = key_set(number)
        return gradient_block(
            query_blocks[number],
            grad_blocks[number],
            log_totals[number],
            row_deltas[number],
            key_block,
            value_block,
            allowed,
        )

    query_parts, key_parts = lax.map(backward_one, block_range)
    own_grads = key_parts[:, :BLOCK].reshape(row_count, -1)
    to_left = route(left_picks, key_parts[:, BLOCK : 2 * BLOCK])
    to_right = route(right_picks, key_parts[:, 2 * BLOCK :])
    from_right = from_behind(shortened(to_left), "blk", -1).astype(to_left.dtype)
    from_left = from_behind(shortened(to_right), "blk", 1).astype(to_right.dtype)
    key_total = own_grads + from_right + from_left
    query_grad_heads = query_parts.reshape(row_count, feature_count).astype(jnp.bfloat16)
    split_total = key_total.reshape(row_count, 2, feature_count)
    key_grad_heads = split_total[:, 0].astype(jnp.bfloat16)
    value_grad_heads = split_total[:, 1].astype(jnp.bfloat16)
    attended, query_grad, key_grad, value_grad = (
        lax.all_to_all(
            shortened(attended_heads), "head", split_axis=0, concat_axis=1, tiled=True
        ).astype(attended_heads.dtype),
        lax.all_to_all(query_grad_heads, "head", split_axis=0, concat_axis=1, tiled=True),
        lax.all_to_all(key_grad_heads, "head", split_axis=0, concat_axis=1, tiled=True),
        lax.all_to_all(value_grad_heads, "head", split_axis=0, concat_axis=1, tiled=True),
    )
    return (attended, query_grad, key_grad, value_grad)


def solution(mesh):
    in_specs = (
        P(("blk", "head"), None),
        P(("blk", "head"), None),
        P(("blk", "head"), None),
        P(("blk", "head"), None),
        P(),
    )
    out_specs = (
        P(("blk", "head"), None),
        P(("blk", "head"), None),
        P(("blk", "head"), None),
        P(("blk", "head"), None),
    )
    return jax.shard_map(shards, mesh=mesh, in_specs=in_specs, out_specs=out_specs, check_vma=False)
```

profile of v0, /device:TPU:134, one launch (start us, length us, event | category | flops | bytes accessed | tf_op | source)
XLA Modules:
  0.0 251.5 jit_solution(17740148639971149953)
XLA Ops:
  0.6 1.8 copy.78
  2.5 9.1 %all-to-all-start = ((bf16[128,16,64]{0,2,1:T(8,128)(2,1)}), bf16[128,16,64]{0,2,1:T(8,128)(2,1)S(1)}, u32[]{:S(2)}, u32[]{:S(2)}) async-start(bf16[128,16,64]{0,2,1:T(8,128)(2,1)} %bitcast.35), calls=%async_computation | async-start | bytes 524288 | tf_op jit(solution)/shard_map/all_to_all | solution.py:74
  11.6 1.8 copy.80
  13.4 10.2 %all-to-all-done = bf16[128,16,64]{0,2,1:T(8,128)(2,1)S(1)} async-done(((bf16[128,16,64]{0,2,1:T(8,128)(2,1)}), bf16[128,16,64]{0,2,1:T(8,128)(2,1)S(1)}, u32[]{:S(2)}, u32[]{:S(2)}) %all-to-all-start) | async-done | bytes 262176 | tf_op jit(solution)/shard_map/all_to_all | solution.py:74
  23.7 3.5 %all-to-all-start.1 = ((bf16[128,16,64]{0,2,1:T(8,128)(2,1)}), bf16[128,16,64]{0,2,1:T(8,128)(2,1)S(1)}, u32[]{:S(2)}, u32[]{:S(2)}) async-start(bf16[128,16,64]{0,2,1:T(8,128)(2,1)} %bitcast.37), calls=%async_computation.1 | async-start | bytes 524288 | tf_op jit(solution)/shard_map/all_to_all | solution.py:75
  27.2 1.8 copy.82
  29.0 0.7 bitcast_dynamic-update-slice_fusion.1
  29.7 8.3 %all-to-all-done.1 = bf16[128,16,64]{0,2,1:T(8,128)(2,1)S(1)} async-done(((bf16[128,16,64]{0,2,1:T(8,128)(2,1)}), bf16[128,16,64]{0,2,1:T(8,128)(2,1)S(1)}, u32[]{:S(2)}, u32[]{:S(2)}) %all-to-all-start.1) | async-done | bytes 262176 | tf_op jit(solution)/shard_map/all_to_all | solution.py:75
  38.1 3.5 %all-to-all-start.2 = ((bf16[128,16,64]{0,2,1:T(8,128)(2,1)}), bf16[128,16,64]{0,2,1:T(8,128)(2,1)S(1)}, u32[]{:S(2)}, u32[]{:S(2)}) async-start(bf16[128,16,64]{0,2,1:T(8,128)(2,1)} %bitcast.41), calls=%async_computation.2 | async-start | bytes 524288 | tf_op jit(solution)/shard_map/all_to_all | solution.py:73
  41.6 0.7 bitcast_dynamic-update-slice_fusion
  42.4 1.9 collective-permute-start
  44.3 3.6 %collective-permute-start.1 = (bf16[2048,128]{0,1:T(8,128)(2,1)}, bf16[2048,128]{0,1:T(8,128)(2,1)}, u32[]{:S(2)}, u32[]{:S(2)}) collective-permute-start(bf16[2048,128]{0,1:T(8,128)(2,1)} %bitcast_dynamic-update-slice_fusion), channel_id=1, source_target_pairs={{16,0},{32,16},{48,32},{64,48},{80,64},{96,80},{112,96},{128,112},... | collective-permute-start | bytes 1572872 | tf_op jit(solution)/shard_map/ppermute | solution.py:18
  47.9 0.8 copy.90
  48.8 3.5 %all-to-all-done.2 = bf16[128,16,64]{0,2,1:T(8,128)(2,1)S(1)} async-done(((bf16[128,16,64]{0,2,1:T(8,128)(2,1)}), bf16[128,16,64]{0,2,1:T(8,128)(2,1)S(1)}, u32[]{:S(2)}, u32[]{:S(2)}) %all-to-all-start.2) | async-done | bytes 262176 | tf_op jit(solution)/shard_map/all_to_all | solution.py:73
  52.3 4.5 %all-to-all-start.4 = ((bf16[128,16,64]{0,2,1:T(8,128)(2,1)}), bf16[128,16,64]{0,2,1:T(8,128)(2,1)S(1)}, u32[]{:S(2)}, u32[]{:S(2)}) async-start(bf16[128,16,64]{0,2,1:T(8,128)(2,1)} %bitcast.45), calls=%async_computation.4 | async-start | bytes 524288 | tf_op jit(solution)/shard_map/all_to_all | solution.py:76
  57.6 1.4 reshape.208
  59.5 8.6 %all-to-all-done.4 = bf16[128,16,64]{0,2,1:T(8,128)(2,1)S(1)} async-done(((bf16[128,16,64]{0,2,1:T(8,128)(2,1)}), bf16[128,16,64]{0,2,1:T(8,128)(2,1)S(1)}, u32[]{:S(2)}, u32[]{:S(2)}) %all-to-all-start.4) | async-done | bytes 262176 | tf_op jit(solution)/shard_map/all_to_all | solution.py:76
  68.5 1.4 reshape.209
  70.0 2.2 reshape.210
  72.2 1.1 copy.86
  73.4 39.2 %while.24 = (s32[]{:T(128)}, bf16[4,512,1,64]{1,3,2,0:T(8,128)(2,1)S(1)}, f32[4,1,512]{2,1,0:T(1,128)S(1)}, s32[4]{0:T(128)S(1)}, bf16[4,512,2,1,64]{1,4,3,2,0:T...) while((s32[]{:T(128)}, ...), condition=%wide.region_3.4_spmd, body=%wide.region_0.3_spmd.sunk | while | flops 208043520 | bytes 12339503 | solution.py:125
  81.1 0.8 fusion.56
  82.5 0.7 fusion.57
  90.9 0.8 fusion.56
  92.3 0.7 fusion.57
  100.7 0.8 fusion.56
  102.1 0.7 fusion.57
  110.5 0.8 fusion.56
  112.9 48.0 %while.25 = (s32[]{:T(128)}, bf16[4,512,1,64]{1,3,2,0:T(8,128)(2,1)}, f32[4,1536,2,1,64]{1,4,2,3,0:T(8,128)}, s32[4]{0:T(128)S(1)}, bf16[4,512,2,1,64]{1,4,3,2,0...) while((s32[]{:T(128)}, ...), condition=%wide.region_6.7_spmd, body=%wide.region_5.6_spmd.sunk | while | flops 510328832 | bytes 21967248 | solution.py:143
  120.6 0.9 fusion.65
  123.9 0.9 fusion.69
  132.6 1.0 fusion.65
  135.9 1.0 fusion.69
  144.6 1.0 fusion.65
  147.9 1.0 fusion.69
  156.6 0.9 fusion.65
  159.9 1.0 fusion.69
  160.9 3.7 %fusion.34 = (f32[4,512,2,1,64]{1,4,2,3,0:T(8,128)}, f32[4,512,2,1,64]{1,4,2,3,0:T(8,128)S(1)}, f32[4,512,2,1,64]{1,4,2,3,0:T(8,128)}) fusion(f32[4,1536,2,1,64]{1,4,2,3,0:T(8,128)} %get-tuple-element.138), kind=kLoop, calls=%fused_computation.72 | loop fusion | bytes 6291456 | tf_op jit(solution)/shard_map/slice | solution.py:145
  164.6 1.1 copy.103
  165.6 1.7 reshape.215
  167.3 1.1 convolution_convert_fusion
  169.0 1.0 copy.104
  170.0 4.2 %collective-permute-start.3 = (bf16[2048,128]{0,1:T(8,128)(2,1)}, bf16[2048,128]{0,1:T(8,128)(2,1)}, u32[]{:S(2)}, u32[]{:S(2)}) collective-permute-start(bf16[2048,128]{0,1:T(8,128)(2,1)} %copy.104), channel_id=1, source_target_pairs={{0,16},{16,32},{32,48},{48,64},{64,80},{80,96},{96,112},{112,128},... | collective-permute-start | bytes 1572872 | tf_op jit(solution)/shard_map/ppermute | solution.py:30
  174.2 2.7 %copy.101 = f32[4,512,2,1,64]{4,2,1,0,3:T(2,128)S(1)} copy(f32[4,512,2,1,64]{1,4,2,3,0:T(8,128)} %get-tuple-element.284) | data formatting | bytes 2097152 | tf_op jit(solution)/shard_map/slice | solution.py:145
  176.9 1.7 reshape.214
  178.6 1.1 convolution_convert_fusion.1
  180.5 1.9 collective-permute-start.2
  182.7 0.8 copy.89
  183.5 7.7 %all-to-all-start.3 = ((bf16[16,128,64]{1,2,0:T(8,128)(2,1)}), bf16[16,128,64]{1,2,0:T(8,128)(2,1)S(1)}, u32[]{:S(2)}, u32[]{:S(2)}) async-start(bf16[16,128,64]{1,2,0:T(8,128)(2,1)} %copy.89), calls=%async_computation.3 | async-start | bytes 524288 | tf_op jit(solution)/shard_map/all_to_all | solution.py:155
  191.5 0.8 copy.99
  193.3 9.1 %all-to-all-done.3 = bf16[16,128,64]{1,2,0:T(8,128)(2,1)S(1)} async-done(((bf16[16,128,64]{1,2,0:T(8,128)(2,1)}), bf16[16,128,64]{1,2,0:T(8,128)(2,1)S(1)}, u32[]{:S(2)}, u32[]{:S(2)}) %all-to-all-start.3) | async-done | bytes 262176 | tf_op jit(solution)/shard_map/all_to_all | solution.py:155
  202.5 3.7 %all-to-all-start.5 = ((bf16[16,128,64]{1,2,0:T(8,128)(2,1)}), bf16[16,128,64]{1,2,0:T(8,128)(2,1)S(1)}, u32[]{:S(2)}, u32[]{:S(2)}) async-start(bf16[16,128,64]{1,2,0:T(8,128)(2,1)} %copy.99), calls=%async_computation.5 | async-start | bytes 524288 | tf_op jit(solution)/shard_map/all_to_all | solution.py:158
  206.1 1.2 add_convert_fusion
  207.5 0.8 copy.105
  208.3 10.3 %all-to-all-done.5 = bf16[16,128,64]{1,2,0:T(8,128)(2,1)S(1)} async-done(((bf16[16,128,64]{1,2,0:T(8,128)(2,1)}), bf16[16,128,64]{1,2,0:T(8,128)(2,1)S(1)}, u32[]{:S(2)}, u32[]{:S(2)}) %all-to-all-start.5) | async-done | bytes 262176 | tf_op jit(solution)/shard_map/all_to_all | solution.py:158
  218.6 3.5 %all-to-all-start.6 = ((bf16[16,128,64]{1,2,0:T(8,128)(2,1)}), bf16[16,128,64]{1,2,0:T(8,128)(2,1)S(1)}, u32[]{:S(2)}, u32[]{:S(2)}) async-start(bf16[16,128,64]{1,2,0:T(8,128)(2,1)} %copy.105), calls=%async_computation.6 | async-start | bytes 524288 | tf_op jit(solution)/shard_map/all_to_all | solution.py:159
  222.2 0.8 copy.106
  222.9 12.8 %all-to-all-done.6 = bf16[16,128,64]{1,2,0:T(8,128)(2,1)S(1)} async-done(((bf16[16,128,64]{1,2,0:T(8,128)(2,1)}), bf16[16,128,64]{1,2,0:T(8,128)(2,1)S(1)}, u32[]{:S(2)}, u32[]{:S(2)}) %all-to-all-start.6) | async-done | bytes 262176 | tf_op jit(solution)/shard_map/all_to_all | solution.py:159
  235.8 3.5 %all-to-all-start.7 = ((bf16[16,128,64]{1,2,0:T(8,128)(2,1)}), bf16[16,128,64]{1,2,0:T(8,128)(2,1)S(1)}, u32[]{:S(2)}, u32[]{:S(2)}) async-start(bf16[16,128,64]{1,2,0:T(8,128)(2,1)} %copy.106), calls=%async_computation.7 | async-start | bytes 524288 | tf_op jit(solution)/shard_map/all_to_all | solution.py:160
  239.3 0.9 copy.107
  240.2 0.8 copy.108
  241.0 0.8 copy.109
  241.9 8.8 %all-to-all-done.7 = bf16[16,128,64]{1,2,0:T(8,128)(2,1)S(1)} async-done(((bf16[16,128,64]{1,2,0:T(8,128)(2,1)}), bf16[16,128,64]{1,2,0:T(8,128)(2,1)S(1)}, u32[]{:S(2)}, u32[]{:S(2)}) %all-to-all-start.7) | async-done | bytes 262176 | tf_op jit(solution)/shard_map/all_to_all | solution.py:160
  250.6 0.8 copy.110
  (141 shorter events, 32.0 us)
Async XLA Ops:
  0.6 47.3 %copy-start.1 = (bf16[128,1024]{1,0:T(8,128)(2,1)S(1)}, bf16[128,1024]{1,0:T(8,128)(2,1)}, u32[]{:S(2)}) copy-start(bf16[128,1024]{1,0:T(8,128)(2,1)} %param.12) | copy-start | bytes 786436
  2.5 55.0 %copy-start.5 = (s32[128,2]{0,1:T(2,128)S(1)}, s32[128,2]{0,1:T(2,128)}, u32[]{:S(2)}) copy-start(s32[128,2]{0,1:T(2,128)} %param.13) | copy-start | bytes 3076
  2.5 21.2 %all-to-all-start = ((bf16[128,16,64]{0,2,1:T(8,128)(2,1)}), bf16[128,16,64]{0,2,1:T(8,128)(2,1)S(1)}, u32[]{:S(2)}, u32[]{:S(2)}) async-start(bf16[128,16,64]{0,2,1:T(8,128)(2,1)} %bitcast.35), calls=%async_computation | async-start | bytes 524288 | tf_op jit(solution)/shard_map/all_to_all | solution.py:74
  23.7 14.4 %all-to-all-start.1 = ((bf16[128,16,64]{0,2,1:T(8,128)(2,1)}), bf16[128,16,64]{0,2,1:T(8,128)(2,1)S(1)}, u32[]{:S(2)}, u32[]{:S(2)}) async-start(bf16[128,16,64]{0,2,1:T(8,128)(2,1)} %bitcast.37), calls=%async_computation.1 | async-start | bytes 524288 | tf_op jit(solution)/shard_map/all_to_all | solution.py:75
  38.1 14.3 %all-to-all-start.2 = ((bf16[128,16,64]{0,2,1:T(8,128)(2,1)}), bf16[128,16,64]{0,2,1:T(8,128)(2,1)S(1)}, u32[]{:S(2)}, u32[]{:S(2)}) async-start(bf16[128,16,64]{0,2,1:T(8,128)(2,1)} %bitcast.41), calls=%async_computation.2 | async-start | bytes 524288 | tf_op jit(solution)/shard_map/all_to_all | solution.py:73
  42.4 26.1 %collective-permute-start = (bf16[2048,128]{0,1:T(8,128)(2,1)}, bf16[2048,128]{0,1:T(8,128)(2,1)}, u32[]{:S(2)}, u32[]{:S(2)}) collective-permute-start(bf16[2048,128]{0,1:T(8,128)(2,1)} %bitcast_dynamic-update-slice_fusion), channel_id=1, source_target_pairs={{0,16},{16,32},{32,48},{48,64},{64,80},{80,96},{96,112},{112,128},... | collective-permute-start | bytes 1572872 | tf_op jit(solution)/shard_map/ppermute | solution.py:17
  44.3 25.7 %collective-permute-start.1 = (bf16[2048,128]{0,1:T(8,128)(2,1)}, bf16[2048,128]{0,1:T(8,128)(2,1)}, u32[]{:S(2)}, u32[]{:S(2)}) collective-permute-start(bf16[2048,128]{0,1:T(8,128)(2,1)} %bitcast_dynamic-update-slice_fusion), channel_id=1, source_target_pairs={{16,0},{32,16},{48,32},{64,48},{80,64},{96,80},{112,96},{128,112},... | collective-permute-start | bytes 1572872 | tf_op jit(solution)/shard_map/ppermute | solution.py:18
  52.3 15.8 %all-to-all-start.4 = ((bf16[128,16,64]{0,2,1:T(8,128)(2,1)}), bf16[128,16,64]{0,2,1:T(8,128)(2,1)S(1)}, u32[]{:S(2)}, u32[]{:S(2)}) async-start(bf16[128,16,64]{0,2,1:T(8,128)(2,1)} %bitcast.45), calls=%async_computation.4 | async-start | bytes 524288 | tf_op jit(solution)/shard_map/all_to_all | solution.py:76
  121.6 1.0 copy-start.2
  123.1 1.8 copy-start.3
  133.5 1.0 copy-start.2
  135.1 1.8 copy-start.3
  145.5 1.0 copy-start.2
  147.1 1.8 copy-start.3
  157.5 1.0 copy-start.2
  159.1 1.8 copy-start.3
  170.0 36.1 %collective-permute-start.3 = (bf16[2048,128]{0,1:T(8,128)(2,1)}, bf16[2048,128]{0,1:T(8,128)(2,1)}, u32[]{:S(2)}, u32[]{:S(2)}) collective-permute-start(bf16[2048,128]{0,1:T(8,128)(2,1)} %copy.104), channel_id=1, source_target_pairs={{0,16},{16,32},{32,48},{48,64},{64,80},{80,96},{96,112},{112,128},... | collective-permute-start | bytes 1572872 | tf_op jit(solution)/shard_map/ppermute | solution.py:30
  179.7 11.5 %copy-start.4 = (bf16[4,512,1,64]{1,3,2,0:T(8,128)(2,1)S(1)}, bf16[4,512,1,64]{1,3,2,0:T(8,128)(2,1)}, u32[]{:S(2)}) copy-start(bf16[4,512,1,64]{1,3,2,0:T(8,128)(2,1)} %get-tuple-element.137) | copy-start | bytes 786436
  179.7 12.6 %copy-start = (f32[4,512,2,1,64]{1,4,2,3,0:T(8,128)S(1)}, f32[4,512,2,1,64]{1,4,2,3,0:T(8,128)}, u32[]{:S(2)}) copy-start(f32[4,512,2,1,64]{1,4,2,3,0:T(8,128)} %get-tuple-element.286) | copy-start | bytes 3145732
  180.5 25.7 %collective-permute-start.2 = (bf16[2048,128]{0,1:T(8,128)(2,1)S(1)}, bf16[2048,128]{0,1:T(8,128)(2,1)S(1)}, u32[]{:S(2)}, u32[]{:S(2)}) collective-permute-start(bf16[2048,128]{0,1:T(8,128)(2,1)S(1)} %copy.102), channel_id=1, source_target_pairs={{0,496},{16,0},{32,16},{48,32},{64,48},{80,64},{96,80},{112,96},{1... | collective-permute-start | bytes 1572872 | tf_op jit(solution)/shard_map/ppermute | solution.py:30
  183.5 19.0 %all-to-all-start.3 = ((bf16[16,128,64]{1,2,0:T(8,128)(2,1)}), bf16[16,128,64]{1,2,0:T(8,128)(2,1)S(1)}, u32[]{:S(2)}, u32[]{:S(2)}) async-start(bf16[16,128,64]{1,2,0:T(8,128)(2,1)} %copy.89), calls=%async_computation.3 | async-start | bytes 524288 | tf_op jit(solution)/shard_map/all_to_all | solution.py:155
  202.5 16.1 %all-to-all-start.5 = ((bf16[16,128,64]{1,2,0:T(8,128)(2,1)}), bf16[16,128,64]{1,2,0:T(8,128)(2,1)S(1)}, u32[]{:S(2)}, u32[]{:S(2)}) async-start(bf16[16,128,64]{1,2,0:T(8,128)(2,1)} %copy.99), calls=%async_computation.5 | async-start | bytes 524288 | tf_op jit(solution)/shard_map/all_to_all | solution.py:158
  218.6 17.2 %all-to-all-start.6 = ((bf16[16,128,64]{1,2,0:T(8,128)(2,1)}), bf16[16,128,64]{1,2,0:T(8,128)(2,1)S(1)}, u32[]{:S(2)}, u32[]{:S(2)}) async-start(bf16[16,128,64]{1,2,0:T(8,128)(2,1)} %copy.105), calls=%async_computation.6 | async-start | bytes 524288 | tf_op jit(solution)/shard_map/all_to_all | solution.py:159
  235.8 14.9 %all-to-all-start.7 = ((bf16[16,128,64]{1,2,0:T(8,128)(2,1)}), bf16[16,128,64]{1,2,0:T(8,128)(2,1)S(1)}, u32[]{:S(2)}, u32[]{:S(2)}) async-start(bf16[16,128,64]{1,2,0:T(8,128)(2,1)} %copy.106), calls=%async_computation.7 | async-start | bytes 524288 | tf_op jit(solution)/shard_map/all_to_all | solution.py:160
where the time goes:
time: 254 us; the launch traced here: 251 us
  waiting for transfers between devices  71.8 us (28%)
  local copies, waits for them, and re-layouts  52.7 us (21%)
  starting transfers between devices  50.8 us (20%)
  loops' own time  47.1 us (19%)
  matrix products  19.9 us (8%)
  other arithmetic  7.98 us (3%)
    another operation x1, loops' own time, shards(): query_parts, key_parts = lax.map(backward_one, block_range)  23.6 us
    another operation x1, loops' own time, shards(): out_blocks, log_totals = lax.map(forward_one, block_range)  23.5 us
    all_to_all x1, waiting for transfers between devices, shards(): lax.all_to_all(key_grad_heads, 'head', split_axis=0, concat_axis=1, tiled...  12.8 us
    unnamed x21, local copies, waits for them, and re-layouts  10.9 us
    all_to_all x1, waiting for transfers between devices, shards(): lax.all_to_all(query_grad_heads, 'head', split_axis=0, concat_axis=1, til...  10.3 us
    all_to_all x1, waiting for transfers between devices, shards(): lax.all_to_all(key_rows, 'head', split_axis=1, concat_axis=0, tiled=True)  10.2 us
    all_to_all x1, starting transfers between devices, shards(): lax.all_to_all(key_rows, 'head', split_axis=1, concat_axis=0, tiled=True)  9.15 us
    all_to_all x1, waiting for transfers between devices, shards(): lax.all_to_all(shortened(attended_heads), 'head', split_axis=0, concat_ax...  9.13 us
  transfers between devices with their start and end apart: 12, of which 8 were waited for; matrix products, arithmetic and copies ran while one was open for 10% of the time, Pallas kernels for 0%

commit v1 on v0

--- a/solution.py
+++ b/solution.py
@@ -68,12 +68,29 @@
     return tuple(results)
 
 
+def to_heads(arrays):
+    count = lax.axis_size("head")
+    rows, width = arrays[0].shape
+    stacked = jnp.stack(arrays).reshape(len(arrays), rows, count, width // count)
+    stacked = stacked.transpose(2, 0, 1, 3)
+    moved = lax.all_to_all(stacked, "head", split_axis=0, concat_axis=0, tiled=True)
+    moved = moved.transpose(1, 0, 2, 3).reshape(len(arrays), count * rows, width // count)
+    return [moved[i] for i in range(len(arrays))]
+
+
+def to_rows(arrays):
+    count = lax.axis_size("head")
+    rows, width = arrays[0].shape
+    stacked = jnp.stack(arrays).reshape(len(arrays), count, rows // count, width)
+    stacked = stacked.transpose(1, 0, 2, 3)
+    moved = lax.all_to_all(stacked, "head", split_axis=0, concat_axis=0, tiled=True)
+    moved = moved.transpose(1, 2, 0, 3).reshape(len(arrays), rows // count, count * width)
+    return [moved[i] for i in range(len(arrays))]
+
+
 def shards(query_rows, key_rows, value_rows, out_grad, neighbour_blocks):
-    query_heads, key_heads, value_heads, grad_heads = (
-        lax.all_to_all(query_rows, "head", split_axis=1, concat_axis=0, tiled=True),
-        lax.all_to_all(key_rows, "head", split_axis=1, concat_axis=0, tiled=True),
-        lax.all_to_all(value_rows, "head", split_axis=1, concat_axis=0, tiled=True),
-        lax.all_to_all(out_grad, "head", split_axis=1, concat_axis=0, tiled=True),
+    query_heads, key_heads, value_heads, grad_heads = to_heads(
+        [query_rows, key_rows, value_rows, out_grad]
     )
     row_count = query_heads.shape[0]
     feature_count = query_heads.shape[1]
@@ -151,13 +168,8 @@
     split_total = key_total.reshape(row_count, 2, feature_count)
     key_grad_heads = split_total[:, 0].astype(jnp.bfloat16)
     value_grad_heads = split_total[:, 1].astype(jnp.bfloat16)
-    attended, query_grad, key_grad, value_grad = (
-        lax.all_to_all(
-            shortened(attended_heads), "head", split_axis=0, concat_axis=1, tiled=True
-        ).astype(attended_heads.dtype),
-        lax.all_to_all(query_grad_heads, "head", split_axis=0, concat_axis=1, tiled=True),
-        lax.all_to_all(key_grad_heads, "head", split_axis=0, concat_axis=1, tiled=True),
-        lax.all_to_all(value_grad_heads, "head", split_axis=0, concat_axis=1, tiled=True),
+    attended, query_grad, key_grad, value_grad = to_rows(
+        [attended_heads.astype(jnp.bfloat16), query_grad_heads, key_grad_heads, value_grad_heads]
     )
     return (attended, query_grad, key_grad, value_grad)
 

time: 254 us -> 233 us (0.917)
  the two profiles are of different devices: /device:TPU:134 before, /device:TPU:135 now
where the time goes in v1:
time: 233 us; the launch traced here: 231 us
  blocking collectives  62.5 us (27%)
  local copies, waits for them, and re-layouts  48.8 us (21%)
  loops' own time  47.2 us (20%)
  waiting for transfers between devices  28.8 us (12%)
  matrix products  19.9 us (9%)
  starting transfers between devices  14.8 us (6%)
  other arithmetic  8.23 us (4%)
    all_to_all x1, blocking collectives, to_heads(): lax.all_to_all(stacked, 'head', split_axis=0, concat_axis=0, tiled=True)  35.4 us
    all_to_all x1, blocking collectives, to_rows(): lax.all_to_all(stacked, 'head', split_axis=0, concat_axis=0, tiled=True)  27.1 us
    another operation x1, loops' own time, shards(): query_parts, key_parts = lax.map(backward_one, block_range)  23.6 us
    another operation x1, loops' own time, shards(): out_blocks, log_totals = lax.map(forward_one, block_range)  23.5 us
    ppermute x2, waiting for transfers between devices, from_behind(): return lax.ppermute(value, axis, pairs)  15.4 us
    unnamed x19, local copies, waits for them, and re-layouts  9.1 us
    ppermute x1, waiting for transfers between devices, extended(): after = lax.ppermute(leading, axis, down)  8.94 us
    ppermute x1, starting transfers between devices, extended(): before = lax.ppermute(last, axis, up)  8.43 us
  transfers between devices with their start and end apart: 4, of which 3 were waited for; matrix products, arithmetic and copies ran while one was open for 5% of the time, Pallas kernels for 0%

profile of v1, /device:TPU:135, one launch (start us, length us, event | category | flops | bytes accessed | tf_op | source)
XLA Modules:
  0.0 231.2 jit_solution(10286459736111195257)
XLA Ops:
  0.6 1.1 copy.81
  1.8 1.1 copy.80
  2.9 1.1 copy.79
  4.0 1.1 copy.78
  5.4 35.4 %all_to_all.10 = bf16[16,4,128,64]{2,3,1,0:T(8,128)(2,1)S(1)} all-to-all(bf16[16,4,128,64]{2,3,1,0:T(8,128)(2,1)S(1)} %copy.82), channel_id=1, replica_groups=mesh['blk'=32,'head'=16] {'head'}, dimensions={0} | all-to-all | bytes 2097152 | tf_op jit(solution)/shard_map/all_to_all | solution.py:76
  41.0 0.8 bitcast_dynamic-update-slice_fusion.1
  41.9 0.8 bitcast_dynamic-update-slice_fusion
  42.7 8.4 %collective-permute-start = (bf16[2048,128]{0,1:T(8,128)(2,1)}, bf16[2048,128]{0,1:T(8,128)(2,1)}, u32[]{:S(2)}, u32[]{:S(2)}) collective-permute-start(bf16[2048,128]{0,1:T(8,128)(2,1)} %bitcast_dynamic-update-slice_fusion), channel_id=1, source_target_pairs={{0,16},{16,32},{32,48},{48,64},{64,80},{80,96},{96,112},{112,128},... | collective-permute-start | bytes 1572872 | tf_op jit(solution)/shard_map/ppermute | solution.py:17
  51.1 1.9 collective-permute-start.1
  53.8 1.4 reshape.237
  56.1 4.4 %collective-permute-done = bf16[2048,128]{0,1:T(8,128)(2,1)} collective-permute-done((bf16[2048,128]{0,1:T(8,128)(2,1)}, bf16[2048,128]{0,1:T(8,128)(2,1)}, u32[]{:S(2)}, u32[]{:S(2)}) %collective-permute-start) | collective-permute-done | bytes 524320 | tf_op jit(solution)/shard_map/ppermute | solution.py:17
  60.5 1.4 reshape.238
  62.0 8.9 %collective-permute-done.1 = bf16[2048,128]{0,1:T(8,128)(2,1)} collective-permute-done((bf16[2048,128]{0,1:T(8,128)(2,1)}, bf16[2048,128]{0,1:T(8,128)(2,1)}, u32[]{:S(2)}, u32[]{:S(2)}) %collective-permute-start.1) | collective-permute-done | bytes 524320 | tf_op jit(solution)/shard_map/ppermute | solution.py:18
  71.0 2.2 reshape.239
  73.2 1.1 copy.88
  74.3 39.2 %while.24 = (s32[]{:T(128)}, bf16[4,512,1,64]{1,3,2,0:T(8,128)(2,1)S(1)}, f32[4,1,512]{2,1,0:T(1,128)S(1)}, s32[4]{0:T(128)S(1)}, bf16[4,512,2,1,64]{1,4,3,2,0:T...) while((s32[]{:T(128)}, ...), condition=%wide.region_3.4_spmd, body=%wide.region_0.3_spmd.sunk | while | flops 208043520 | bytes 12339503 | solution.py:142
  79.4 0.6 dynamic_slice.119
  82.0 0.8 fusion.56
  83.4 0.7 fusion.57
  89.2 0.6 dynamic_slice.119
  91.8 0.8 fusion.56
  93.2 0.7 fusion.57
  99.0 0.6 dynamic_slice.119
  101.6 0.8 fusion.56
  103.0 0.7 fusion.57
  108.8 0.6 dynamic_slice.119
  111.4 0.8 fusion.56
  112.8 0.7 fusion.57
  113.8 47.9 %while.25 = (s32[]{:T(128)}, bf16[4,512,1,64]{1,3,2,0:T(8,128)(2,1)}, f32[4,1536,2,1,64]{1,4,2,3,0:T(8,128)}, s32[4]{0:T(128)S(1)}, bf16[4,512,2,1,64]{1,4,3,2,0...) while((s32[]{:T(128)}, ...), condition=%wide.region_6.7_spmd, body=%wide.region_5.6_spmd.sunk | while | flops 510328832 | bytes 21967248 | solution.py:160
  116.4 0.6 dynamic_slice.128
  118.9 0.6 dynamic_slice.129
  121.5 0.9 fusion.65
  122.5 0.6 fusion.66
  123.5 0.6 fusion.67
  124.9 1.0 fusion.69
  128.4 0.6 dynamic_slice.128
  133.5 0.9 fusion.65
  134.5 0.6 fusion.66
  135.4 0.6 fusion.67
  136.8 1.0 fusion.69
  145.5 0.9 fusion.65
  146.5 0.6 fusion.66
  148.8 1.0 fusion.69
  157.5 0.9 fusion.65
  158.4 0.6 fusion.66
  160.8 1.0 fusion.69
  161.8 3.7 %fusion.34 = (f32[4,512,2,1,64]{1,4,2,3,0:T(8,128)}, f32[4,512,2,1,64]{1,4,2,3,0:T(8,128)S(1)}, f32[4,512,2,1,64]{1,4,2,3,0:T(8,128)}) fusion(f32[4,1536,2,1,64]{1,4,2,3,0:T(8,128)} %get-tuple-element.138), kind=kLoop, calls=%fused_computation.75 | loop fusion | bytes 6291456 | tf_op jit(solution)/shard_map/slice | solution.py:162
  165.4 1.1 copy.102
  166.5 1.7 reshape.242
  168.2 1.1 convolution_convert_fusion
  169.9 1.0 copy.103
  170.9 2.1 collective-permute-start.3
  173.0 2.7 %copy.100 = f32[4,512,2,1,64]{4,2,1,0,3:T(2,128)S(1)} copy(f32[4,512,2,1,64]{1,4,2,3,0:T(8,128)} %get-tuple-element.284) | data formatting | bytes 2097152 | tf_op jit(solution)/shard_map/slice | solution.py:162
  175.7 1.7 reshape.241
  177.4 1.1 convolution_convert_fusion.1
  179.2 2.4 %collective-permute-start.2 = (bf16[2048,128]{0,1:T(8,128)(2,1)S(1)}, bf16[2048,128]{0,1:T(8,128)(2,1)S(1)}, u32[]{:S(2)}, u32[]{:S(2)}) collective-permute-start(bf16[2048,128]{0,1:T(8,128)(2,1)S(1)} %copy.101), channel_id=1, source_target_pairs={{0,496},{16,0},{32,16},{48,32},{64,48},{80,64},{96,80},{112,96},{1... | collective-permute-start | bytes 1572872 | tf_op jit(solution)/shard_map/ppermute | solution.py:30
  181.9 0.7 copy.99
  183.4 15.4 %collective-permute-done.2 = bf16[2048,128]{0,1:T(8,128)(2,1)S(1)} collective-permute-done((bf16[2048,128]{0,1:T(8,128)(2,1)S(1)}, bf16[2048,128]{0,1:T(8,128)(2,1)S(1)}, u32[]{:S(2)}, u32[]{:S(2)}) %collective-permute-start.2) | collective-permute-done | bytes 524320 | tf_op jit(solution)/shard_map/ppermute | solution.py:30
  198.8 1.2 add_convert_fusion
  200.5 27.1 %all_to_all.11 = bf16[16,4,128,64]{2,3,1,0:T(8,128)(2,1)S(1)} all-to-all(bf16[16,4,128,64]{2,3,1,0:T(8,128)(2,1)S(1)} %copy.104), channel_id=1, replica_groups=mesh['blk'=32,'head'=16] {'head'}, dimensions={0} | all-to-all | bytes 2097152 | tf_op jit(solution)/shard_map/all_to_all | solution.py:86
  227.8 0.9 copy.106
  228.7 0.8 copy.107
  229.5 0.8 copy.108
  230.4 0.8 copy.109
  (130 shorter events, 24.0 us)
Async XLA Ops:
  40.7 13.0 %copy-start.4 = (s32[128,2]{0,1:T(2,128)S(1)}, s32[128,2]{0,1:T(2,128)}, u32[]{:S(2)}) copy-start(s32[128,2]{0,1:T(2,128)} %param.13) | copy-start | bytes 3076
  42.7 17.8 %collective-permute-start = (bf16[2048,128]{0,1:T(8,128)(2,1)}, bf16[2048,128]{0,1:T(8,128)(2,1)}, u32[]{:S(2)}, u32[]{:S(2)}) collective-permute-start(bf16[2048,128]{0,1:T(8,128)(2,1)} %bitcast_dynamic-update-slice_fusion), channel_id=1, source_target_pairs={{0,16},{16,32},{32,48},{48,64},{64,80},{80,96},{96,112},{112,128},... | collective-permute-start | bytes 1572872 | tf_op jit(solution)/shard_map/ppermute | solution.py:17
  51.1 19.8 %collective-permute-start.1 = (bf16[2048,128]{0,1:T(8,128)(2,1)}, bf16[2048,128]{0,1:T(8,128)(2,1)}, u32[]{:S(2)}, u32[]{:S(2)}) collective-permute-start(bf16[2048,128]{0,1:T(8,128)(2,1)} %bitcast_dynamic-update-slice_fusion), channel_id=1, source_target_pairs={{16,0},{32,16},{48,32},{64,48},{80,64},{96,80},{112,96},{128,112},... | collective-permute-start | bytes 1572872 | tf_op jit(solution)/shard_map/ppermute | solution.py:18
  122.5 1.0 copy-start.1
  124.0 1.8 copy-start.2
  134.5 1.0 copy-start.1
  136.0 1.8 copy-start.2
  146.5 1.0 copy-start.1
  148.0 1.8 copy-start.2
  158.4 1.0 copy-start.1
  160.0 1.8 copy-start.2
  170.9 12.5 %collective-permute-start.3 = (bf16[2048,128]{0,1:T(8,128)(2,1)}, bf16[2048,128]{0,1:T(8,128)(2,1)}, u32[]{:S(2)}, u32[]{:S(2)}) collective-permute-start(bf16[2048,128]{0,1:T(8,128)(2,1)} %copy.103), channel_id=1, source_target_pairs={{0,16},{16,32},{32,48},{48,64},{64,80},{80,96},{96,112},{112,128},... | collective-permute-start | bytes 1572872 | tf_op jit(solution)/shard_map/ppermute | solution.py:30
  177.4 4.5 %copy-start = (f32[4,512,2,1,64]{1,4,2,3,0:T(8,128)S(1)}, f32[4,512,2,1,64]{1,4,2,3,0:T(8,128)}, u32[]{:S(2)}) copy-start(f32[4,512,2,1,64]{1,4,2,3,0:T(8,128)} %get-tuple-element.286) | copy-start | bytes 3145732
  179.0 3.9 %copy-start.3 = (bf16[4,512,1,64]{1,3,2,0:T(8,128)(2,1)S(1)}, bf16[4,512,1,64]{1,3,2,0:T(8,128)(2,1)}, u32[]{:S(2)}) copy-start(bf16[4,512,1,64]{1,3,2,0:T(8,128)(2,1)} %get-tuple-element.137) | copy-start | bytes 786436
  179.2 19.5 %collective-permute-start.2 = (bf16[2048,128]{0,1:T(8,128)(2,1)S(1)}, bf16[2048,128]{0,1:T(8,128)(2,1)S(1)}, u32[]{:S(2)}, u32[]{:S(2)}) collective-permute-start(bf16[2048,128]{0,1:T(8,128)(2,1)S(1)} %copy.101), channel_id=1, source_target_pairs={{0,496},{16,0},{32,16},{48,32},{64,48},{80,64},{96,80},{112,96},{1... | collective-permute-start | bytes 1572872 | tf_op jit(solution)/shard_map/ppermute | solution.py:30

commit v2 on v0

v2 whole, which is shorter than its diff:
```python
import jax
import jax.numpy as jnp
from jax import lax
from jax.experimental import pallas as pl
from jax.experimental.pallas import tpu as pltpu
from jax.sharding import PartitionSpec as P

HEAD_DIM = 64
BLOCK = 512
INTERPRET = False


def to_heads(arrays):
    count = lax.axis_size("head")
    rows, width = arrays[0].shape
    stacked = jnp.stack(arrays).reshape(len(arrays), rows, count, width // count)
    stacked = stacked.transpose(2, 0, 1, 3)
    moved = lax.all_to_all(stacked, "head", split_axis=0, concat_axis=0, tiled=True)
    return moved.transpose(1, 0, 2, 3).reshape(len(arrays), count * rows, width // count)


def to_rows(stacked):
    count = lax.axis_size("head")
    parts, rows, width = stacked.shape
    stacked = stacked.reshape(parts, count, rows // count, width).transpose(1, 0, 2, 3)
    moved = lax.all_to_all(stacked, "head", split_axis=0, concat_axis=0, tiled=True)
    moved = moved.transpose(1, 2, 0, 3).reshape(parts, rows // count, count * width)
    return [moved[i] for i in range(parts)]


def from_behind(value, axis, steps):
    count = lax.axis_size(axis)
    pairs = [(source, (source + steps) % count) for source in range(count)]
    return lax.ppermute(value, axis, pairs)


def attention_kernel(picks_ref, own_ref, left_ref, right_ref, out_ref, own_grad_ref, left_ref_acc, right_ref_acc):
    number = pl.program_id(0)
    scale = HEAD_DIM ** (-0.5)
    f32 = jnp.float32

    @pl.when(number == 0)
    def _():
        left_ref_acc[...] = jnp.zeros(left_ref_acc.shape, f32)
        right_ref_acc[...] = jnp.zeros(right_ref_acc.shape, f32)

    query = own_ref[0, 0]
    grad = own_ref[3, 0]
    keys = (own_ref[1, 0], left_ref[0, 0], right_ref[0, 0])
    values = (own_ref[2, 0], left_ref[1, 0], right_ref[1, 0])

    def nt(a, b):
        return lax.dot_general(a, b, (((1,), (1,)), ((), ())), preferred_element_type=f32)

    def nn(a, b):
        return lax.dot_general(a, b, (((1,), (0,)), ((), ())), preferred_element_type=f32)

    def tn(a, b):
        return lax.dot_general(a, b, (((0,), (0,)), ((), ())), preferred_element_type=f32)

    scores = [nt(query, key) * scale for key in keys]
    row = lax.broadcasted_iota(jnp.int32, scores[0].shape, 0)
    col = lax.broadcasted_iota(jnp.int32, scores[0].shape, 1)
    scores[0] = jnp.where(col <= row, scores[0], -jnp.inf)
    highest = jnp.max(scores[0], axis=1, keepdims=True)
    for part in scores[1:]:
        highest = jnp.maximum(highest, jnp.max(part, axis=1, keepdims=True))
    total = sum(jnp.sum(jnp.exp(part - highest), axis=1, keepdims=True) for part in scores)
    log_total = highest + jnp.log(total)
    weights = [jnp.exp(part - log_total) for part in scores]
    weights_bf = [w.astype(jnp.bfloat16) for w in weights]
    attended = sum(nn(w, v) for w, v in zip(weights_bf, values)).astype(jnp.bfloat16)
    row_delta = jnp.sum(grad.astype(f32) * attended.astype(f32), axis=1, keepdims=True)
    score_grads = [
        (w * (nt(grad, v) - row_delta)).astype(jnp.bfloat16) for w, v in zip(weights, values)
    ]
    query_grad = sum(nn(d, k) for d, k in zip(score_grads, keys)) * scale
    out_ref[0, 0] = attended
    out_ref[1, 0] = query_grad.astype(jnp.bfloat16)
    key_parts = [tn(d, query) * scale for d in score_grads]
    value_parts = [tn(w, grad) for w in weights_bf]
    own_grad_ref[0, 0] = key_parts[0]
    own_grad_ref[1, 0] = value_parts[0]
    left_pick = picks_ref[0, number]
    right_pick = picks_ref[1, number]
    left_ref_acc[0, left_pick] += key_parts[1]
    left_ref_acc[1, left_pick] += value_parts[1]
    right_ref_acc[0, right_pick] += key_parts[2]
    right_ref_acc[1, right_pick] += value_parts[2]


def attention(picks, own, left, right):
    arrays, block_count, block, dim = own.shape
    own_spec = pl.BlockSpec((arrays, 1, block, dim), lambda n, p: (0, n, 0, 0))
    left_spec = pl.BlockSpec((2, 1, block, dim), lambda n, p: (0, p[0, n], 0, 0))
    right_spec = pl.BlockSpec((2, 1, block, dim), lambda n, p: (0, p[1, n], 0, 0))
    pair_spec = pl.BlockSpec((2, 1, block, dim), lambda n, p: (0, n, 0, 0))
    whole_spec = pl.BlockSpec((2, block_count, block, dim), lambda n, p: (0, 0, 0, 0))
    pair_shape = (2, block_count, block, dim)
    return pl.pallas_call(
        attention_kernel,
        grid_spec=pltpu.PrefetchScalarGridSpec(
            num_scalar_prefetch=1,
            grid=(block_count,),
            in_specs=[own_spec, left_spec, right_spec],
            out_specs=[pair_spec, pair_spec, whole_spec, whole_spec],
        ),
        out_shape=[
            jax.ShapeDtypeStruct(pair_shape, jnp.bfloat16),
            jax.ShapeDtypeStruct(pair_shape, jnp.float32),
            jax.ShapeDtypeStruct(pair_shape, jnp.float32),
            jax.ShapeDtypeStruct(pair_shape, jnp.float32),
        ],
        compiler_params=pltpu.CompilerParams(dimension_semantics=("arbitrary",)),
        interpret=INTERPRET,
    )(picks, own, left, right)


def shards(query_rows, key_rows, value_rows, out_grad, neighbour_blocks):
    heads = to_heads([query_rows, key_rows, value_rows, out_grad])
    arrays, row_count, dim = heads.shape
    block_count = row_count // BLOCK
    own = heads.reshape(arrays, block_count, BLOCK, dim)
    cycle_place = lax.axis_index("blk")
    first_row = cycle_place * block_count
    picks = jnp.stack(
        [lax.dynamic_slice_in_dim(neighbour_blocks[:, c], first_row, block_count, 0) for c in range(2)]
    )
    picks = jnp.clip(picks, 0, block_count - 1).astype(jnp.int32)
    pairs = own[1:3]
    left = from_behind(pairs, "blk", 1)
    right = from_behind(pairs, "blk", -1)
    out_pair, own_grads, to_left, to_right = attention(picks, own, left, right)
    from_right = from_behind(to_left.astype(jnp.bfloat16), "blk", -1).astype(jnp.float32)
    from_left = from_behind(to_right.astype(jnp.bfloat16), "blk", 1).astype(jnp.float32)
    kv_grads = (own_grads + from_right + from_left).astype(jnp.bfloat16)
    stacked = jnp.concatenate([out_pair, kv_grads], axis=0).reshape(4, row_count, dim)
    attended, query_grad, key_grad, value_grad = to_rows(stacked)
    return (attended, query_grad, key_grad, value_grad)


def solution(mesh):
    in_specs = (
        P(("blk", "head"), None),
        P(("blk", "head"), None),
        P(("blk", "head"), None),
        P(("blk", "head"), None),
        P(),
    )
    out_specs = (
        P(("blk", "head"), None),
        P(("blk", "head"), None),
        P(("blk", "head"), None),
        P(("blk", "head"), None),
    )
    return jax.shard_map(shards, mesh=mesh, in_specs=in_specs, out_specs=out_specs, check_vma=False)
```

time: 254 us -> 150 us (0.59)
  the two profiles are of different devices: /device:TPU:134 before, /device:TPU:8 now
where the time goes in v2:
time: 150 us
  blocking collectives  61.5 us (41%)
  waiting for transfers between devices  28.7 us (19%)
  Pallas kernels  18.4 us (12%)
  local copies, waits for them, and re-layouts  17.7 us (12%)
  starting transfers between devices  17.2 us (11%)
  other arithmetic  5.21 us (3%)
    all_to_all x1, blocking collectives, to_heads(): lax.all_to_all(stacked, 'head', split_axis=0, concat_axis=0, tiled=True)  35.4 us
    ppermute x4, waiting for transfers between devices, from_behind(): return lax.ppermute(value, axis, pairs)  28.7 us
    all_to_all x1, blocking collectives, to_rows(): lax.all_to_all(stacked, 'head', split_axis=0, concat_axis=0, tiled=True)  26 us
    pallas_call x1, Pallas kernels, attention(): pl.pallas_call(attention_kernel, grid_spec=pltpu.PrefetchScalarGridSpec(n...  18.4 us
    ppermute x4, starting transfers between devices, from_behind(): return lax.ppermute(value, axis, pairs)  17.2 us
    unnamed x14, local copies, waits for them, and re-layouts  7.89 us
    ppermute x4, local copies, waits for them, and re-layouts, from_behind(): return lax.ppermute(value, axis, pairs)  4.62 us
  transfers between devices with their start and end apart: 4, of which 4 were waited for; matrix products, arithmetic and copies ran while one was open for 4% of the time, Pallas kernels for 0%

profile of v2, /device:TPU:8, one launch (start us, length us, event | category | flops | bytes accessed | tf_op | source)
XLA Modules:
  0.0 149.5 jit_solution(11083014917656061180)
XLA Ops:
  0.6 1.1 copy.46
  1.8 1.1 copy.47
  2.9 1.1 copy.48
  4.0 1.1 copy.49
  5.1 0.1 maximum_bitcast_fusion
  5.3 0.1 copy.50
  5.4 35.4 %all_to_all.10 = bf16[16,4,128,64]{2,3,1,0:T(8,128)(2,1)S(1)} all-to-all(bf16[16,4,128,64]{2,3,1,0:T(8,128)(2,1)S(1)} %copy.50), channel_id=1, replica_groups=mesh['blk'=32,'head'=16] {'head'}, dimensions={0} | all-to-all | bytes 2097152 | tf_op jit(solution)/shard_map/all_to_all | solution.py:18
  40.8 0.0 copy-start.2
  40.9 0.3 copy.52
  41.2 0.2 slice.31
  41.4 0.1 copy.53
  41.5 10.7 %collective-permute-start.1 = (bf16[2,4,512,64]{2,3,1,0:T(8,128)(2,1)S(1)}, bf16[2,4,512,64]{2,3,1,0:T(8,128)(2,1)S(1)}, u32[]{:S(2)}, u32[]{:S(2)}) collective-permute-start(bf16[2,4,512,64]{2,3,1,0:T(8,128)(2,1)S(1)} %copy.53), channel_id=1, source_target_pairs={{0,496},{16,0},{32,16},{48,32},{64,48},{80,64},{96,80},{112,96},{1... | collective-permute-start | bytes 1572872 | tf_op jit(solution)/shard_map/ppermute | solution.py:34
  52.2 1.9 %collective-permute-start = (bf16[2,4,512,64]{2,3,1,0:T(8,128)(2,1)S(1)}, bf16[2,4,512,64]{2,3,1,0:T(8,128)(2,1)S(1)}, u32[]{:S(2)}, u32[]{:S(2)}) collective-permute-start(bf16[2,4,512,64]{2,3,1,0:T(8,128)(2,1)S(1)} %copy.53), channel_id=1, source_target_pairs={{0,16},{16,32},{32,48},{48,64},{64,80},{80,96},{96,112},{112,128},... | collective-permute-start | bytes 1572872 | tf_op jit(solution)/shard_map/ppermute | solution.py:34
  54.2 0.0 copy-done.2
  54.2 0.1 dynamic-slice_bitcast_fusion
  54.3 0.6 add_clamp_fusion.picks_ref
  54.9 1.8 %copy.51 = bf16[4,16,128,64]{3,2,1,0:T(8,128)(2,1)} copy(bf16[4,16,128,64]{2,3,0,1:T(8,128)(2,1)S(1)} %bitcast.28) | data formatting | bytes 2097152 | tf_op jit(solution)/shard_map/transpose | solution.py:19
  56.6 7.9 %collective-permute-done.1 = bf16[2,4,512,64]{2,3,1,0:T(8,128)(2,1)S(1)} collective-permute-done((bf16[2,4,512,64]{2,3,1,0:T(8,128)(2,1)S(1)}, bf16[2,4,512,64]{2,3,1,0:T(8,128)(2,1)S(1)}, u32[]{:S(2)}, u32[]{:S(2)}) %collective-permute-start.1) | collective-permute-done | bytes 524320 | tf_op jit(solution)/shard_map/ppermute | solution.py:34
  64.6 1.3 copy.56.right_ref
  65.9 5.4 %collective-permute-done = bf16[2,4,512,64]{2,3,1,0:T(8,128)(2,1)S(1)} collective-permute-done((bf16[2,4,512,64]{2,3,1,0:T(8,128)(2,1)S(1)}, bf16[2,4,512,64]{2,3,1,0:T(8,128)(2,1)S(1)}, u32[]{:S(2)}, u32[]{:S(2)}) %collective-permute-start) | collective-permute-done | bytes 524320 | tf_op jit(solution)/shard_map/ppermute | solution.py:34
  71.3 1.3 copy.55.left_ref
  72.6 18.4 %shard_map.84 = (bf16[2,4,512,64]{3,2,1,0:T(8,128)(2,1)}, f32[2,4,512,64]{3,2,1,0:T(8,128)}, f32[2,4,512,64]{3,2,1,0:T(8,128)}, f32[2,4,512,64]{3,2,1,0:T(8,128)}) custom-call(s32[2,4]{1,0:T(2,128)} %add_clamp_fusion.picks_ref, bf16[4,4,512,64]{3,2,1,0:T(8,128)(2,1)} %bitcast.25, bf16[2,4,512,64]{3,2,1,0:T(8,128)(2,1)} %copy.55.left_ref, ...), custom_call_target="tpu_custom_call" | custom-call | tf_op jit(solution)/shard_map/pallas_call | solution.py:100
  91.0 0.0 copy-start
  91.0 1.9 %convert_element_type.15 = bf16[2,4,512,64]{3,2,1,0:T(8,128)(2,1)S(1)} convert(f32[2,4,512,64]{3,2,1,0:T(8,128)} %get-tuple-element.10) | non-fusion elementwise | flops 262144 | bytes 1572864 | tf_op jit(solution)/shard_map/convert_element_type | solution.py:134
  92.9 1.1 copy.57
  94.1 2.6 %collective-permute-start.2 = (bf16[2,4,512,64]{2,3,1,0:T(8,128)(2,1)}, bf16[2,4,512,64]{2,3,1,0:T(8,128)(2,1)}, u32[]{:S(2)}, u32[]{:S(2)}) collective-permute-start(bf16[2,4,512,64]{2,3,1,0:T(8,128)(2,1)} %copy.57), channel_id=1, source_target_pairs={{0,496},{16,0},{32,16},{48,32},{64,48},{80,64},{96,80},{112,96},{1... | collective-permute-start | bytes 1572872 | tf_op jit(solution)/shard_map/ppermute | solution.py:34
  96.7 0.0 copy-done
  96.7 0.2 convert_element_type.17
  96.8 0.3 copy.59
  97.2 1.9 %collective-permute-start.3 = (bf16[2,4,512,64]{2,3,1,0:T(8,128)(2,1)S(1)}, bf16[2,4,512,64]{2,3,1,0:T(8,128)(2,1)S(1)}, u32[]{:S(2)}, u32[]{:S(2)}) collective-permute-start(bf16[2,4,512,64]{2,3,1,0:T(8,128)(2,1)S(1)} %copy.59), channel_id=1, source_target_pairs={{0,16},{16,32},{32,48},{48,64},{64,80},{80,96},{96,112},{112,128},... | collective-permute-start | bytes 1572872 | tf_op jit(solution)/shard_map/ppermute | solution.py:34
  99.1 10.2 %collective-permute-done.2 = bf16[2,4,512,64]{2,3,1,0:T(8,128)(2,1)} collective-permute-done((bf16[2,4,512,64]{2,3,1,0:T(8,128)(2,1)}, bf16[2,4,512,64]{2,3,1,0:T(8,128)(2,1)}, u32[]{:S(2)}, u32[]{:S(2)}) %collective-permute-start.2) | collective-permute-done | bytes 524320 | tf_op jit(solution)/shard_map/ppermute | solution.py:34
  109.3 1.5 %copy.58 = bf16[2,4,512,64]{3,2,1,0:T(8,128)(2,1)S(1)} copy(bf16[2,4,512,64]{2,3,1,0:T(8,128)(2,1)} %collective-permute-done.2) | data formatting | bytes 1048576 | tf_op jit(solution)/shard_map/ppermute | solution.py:34
  110.8 5.2 %collective-permute-done.3 = bf16[2,4,512,64]{2,3,1,0:T(8,128)(2,1)S(1)} collective-permute-done((bf16[2,4,512,64]{2,3,1,0:T(8,128)(2,1)S(1)}, bf16[2,4,512,64]{2,3,1,0:T(8,128)(2,1)S(1)}, u32[]{:S(2)}, u32[]{:S(2)}) %collective-permute-start.3) | collective-permute-done | bytes 524320 | tf_op jit(solution)/shard_map/ppermute | solution.py:34
  116.0 0.5 copy.60
  116.5 0.0 copy-start.1
  116.5 2.0 %add_convert_fusion = bf16[2,4,512,64]{3,2,1,0:T(8,128)(2,1)S(1)} fusion(bf16[2,4,512,64]{3,2,1,0:T(8,128)(2,1)S(1)} %copy.60, f32[2,4,512,64]{3,2,1,0:T(8,128)} %get-tuple-element.9, bf16[2,4,512,64]{3,2,1,0:T(8,128)(2,1)S(1)} %copy.58), kind=kLoop, calls=%fused_computation.1 | loop fusion | flops 1310720 | bytes 2621440 | tf_op jit(solution)/shard_map/convert_element_type | solution.py:136
  118.5 0.0 copy-done.1
  118.5 0.4 pad_maximum_fusion
  119.0 0.9 copy.61
  119.9 26.0 %all_to_all.11 = bf16[16,4,128,64]{2,3,1,0:T(8,128)(2,1)S(1)} all-to-all(bf16[16,4,128,64]{2,3,1,0:T(8,128)(2,1)S(1)} %bitcast.29), channel_id=1, replica_groups=mesh['blk'=32,'head'=16] {'head'}, dimensions={0} | all-to-all | bytes 2097152 | tf_op jit(solution)/shard_map/all_to_all | solution.py:26
  145.9 0.1 copy.68
  146.0 0.1 fusion
  146.1 0.9 copy.66
  147.0 0.8 copy.65
  147.8 0.8 copy.64
  148.7 0.8 copy.63
  (2 shorter events, 0.0 us)
Async XLA Ops:
  40.8 13.4 %copy-start.2 = (s32[128,2]{0,1:T(2,128)S(1)}, s32[128,2]{0,1:T(2,128)}, u32[]{:S(2)}) copy-start(s32[128,2]{0,1:T(2,128)} %param.9) | copy-start | bytes 3076
  41.5 23.0 %collective-permute-start.1 = (bf16[2,4,512,64]{2,3,1,0:T(8,128)(2,1)S(1)}, bf16[2,4,512,64]{2,3,1,0:T(8,128)(2,1)S(1)}, u32[]{:S(2)}, u32[]{:S(2)}) collective-permute-start(bf16[2,4,512,64]{2,3,1,0:T(8,128)(2,1)S(1)} %copy.53), channel_id=1, source_target_pairs={{0,496},{16,0},{32,16},{48,32},{64,48},{80,64},{96,80},{112,96},{1... | collective-permute-start | bytes 1572872 | tf_op jit(solution)/shard_map/ppermute | solution.py:34
  52.2 19.0 %collective-permute-start = (bf16[2,4,512,64]{2,3,1,0:T(8,128)(2,1)S(1)}, bf16[2,4,512,64]{2,3,1,0:T(8,128)(2,1)S(1)}, u32[]{:S(2)}, u32[]{:S(2)}) collective-permute-start(bf16[2,4,512,64]{2,3,1,0:T(8,128)(2,1)S(1)} %copy.53), channel_id=1, source_target_pairs={{0,16},{16,32},{32,48},{48,64},{64,80},{80,96},{96,112},{112,128},... | collective-permute-start | bytes 1572872 | tf_op jit(solution)/shard_map/ppermute | solution.py:34
  91.0 5.7 %copy-start = (f32[2,4,512,64]{3,2,1,0:T(8,128)S(1)}, f32[2,4,512,64]{3,2,1,0:T(8,128)}, u32[]{:S(2)}) copy-start(f32[2,4,512,64]{3,2,1,0:T(8,128)} %get-tuple-element.11) | copy-start | bytes 3145732
  94.1 15.3 %collective-permute-start.2 = (bf16[2,4,512,64]{2,3,1,0:T(8,128)(2,1)}, bf16[2,4,512,64]{2,3,1,0:T(8,128)(2,1)}, u32[]{:S(2)}, u32[]{:S(2)}) collective-permute-start(bf16[2,4,512,64]{2,3,1,0:T(8,128)(2,1)} %copy.57), channel_id=1, source_target_pairs={{0,496},{16,0},{32,16},{48,32},{64,48},{80,64},{96,80},{112,96},{1... | collective-permute-start | bytes 1572872 | tf_op jit(solution)/shard_map/ppermute | solution.py:34
  97.2 18.8 %collective-permute-start.3 = (bf16[2,4,512,64]{2,3,1,0:T(8,128)(2,1)S(1)}, bf16[2,4,512,64]{2,3,1,0:T(8,128)(2,1)S(1)}, u32[]{:S(2)}, u32[]{:S(2)}) collective-permute-start(bf16[2,4,512,64]{2,3,1,0:T(8,128)(2,1)S(1)} %copy.59), channel_id=1, source_target_pairs={{0,16},{16,32},{32,48},{48,64},{64,80},{80,96},{96,112},{112,128},... | collective-permute-start | bytes 1572872 | tf_op jit(solution)/shard_map/ppermute | solution.py:34
  116.5 2.0 %copy-start.1 = (bf16[2,4,512,64]{3,2,1,0:T(8,128)(2,1)S(1)}, bf16[2,4,512,64]{3,2,1,0:T(8,128)(2,1)}, u32[]{:S(2)}) copy-start(bf16[2,4,512,64]{3,2,1,0:T(8,128)(2,1)} %get-tuple-element.8) | copy-start | bytes 1572868

commit v3 on v2

--- a/solution.py
+++ b/solution.py
@@ -34,7 +34,7 @@
     return lax.ppermute(value, axis, pairs)
 
 
-def attention_kernel(picks_ref, own_ref, left_ref, right_ref, out_ref, own_grad_ref, left_ref_acc, right_ref_acc):
+def attention_kernel(picks_ref, qd_ref, kv_ref, left_ref, right_ref, out_ref, own_grad_ref, left_ref_acc, right_ref_acc):
     number = pl.program_id(0)
     scale = HEAD_DIM ** (-0.5)
     f32 = jnp.float32
@@ -44,10 +44,10 @@
         left_ref_acc[...] = jnp.zeros(left_ref_acc.shape, f32)
         right_ref_acc[...] = jnp.zeros(right_ref_acc.shape, f32)
 
-    query = own_ref[0, 0]
-    grad = own_ref[3, 0]
-    keys = (own_ref[1, 0], left_ref[0, 0], right_ref[0, 0])
-    values = (own_ref[2, 0], left_ref[1, 0], right_ref[1, 0])
+    query = qd_ref[0, 0]
+    grad = qd_ref[1, 0]
+    keys = (kv_ref[0, 0], left_ref[0, 0], right_ref[0, 0])
+    values = (kv_ref[1, 0], left_ref[1, 0], right_ref[1, 0])
 
     def nt(a, b):
         return lax.dot_general(a, b, (((1,), (1,)), ((), ())), preferred_element_type=f32)
@@ -89,9 +89,8 @@
     right_ref_acc[1, right_pick] += value_parts[2]
 
 
-def attention(picks, own, left, right):
-    arrays, block_count, block, dim = own.shape
-    own_spec = pl.BlockSpec((arrays, 1, block, dim), lambda n, p: (0, n, 0, 0))
+def attention(picks, qd, kv, left, right):
+    arrays, block_count, block, dim = kv.shape
     left_spec = pl.BlockSpec((2, 1, block, dim), lambda n, p: (0, p[0, n], 0, 0))
     right_spec = pl.BlockSpec((2, 1, block, dim), lambda n, p: (0, p[1, n], 0, 0))
     pair_spec = pl.BlockSpec((2, 1, block, dim), lambda n, p: (0, n, 0, 0))
@@ -102,7 +101,7 @@
         grid_spec=pltpu.PrefetchScalarGridSpec(
             num_scalar_prefetch=1,
             grid=(block_count,),
-            in_specs=[own_spec, left_spec, right_spec],
+            in_specs=[pair_spec, pair_spec, left_spec, right_spec],
             out_specs=[pair_spec, pair_spec, whole_spec, whole_spec],
         ),
         out_shape=[
@@ -113,29 +112,29 @@
         ],
         compiler_params=pltpu.CompilerParams(dimension_semantics=("arbitrary",)),
         interpret=INTERPRET,
-    )(picks, own, left, right)
+    )(picks, qd, kv, left, right)
 
 
 def shards(query_rows, key_rows, value_rows, out_grad, neighbour_blocks):
-    heads = to_heads([query_rows, key_rows, value_rows, out_grad])
-    arrays, row_count, dim = heads.shape
+    kv_heads = to_heads([key_rows, value_rows])
+    arrays, row_count, dim = kv_heads.shape
     block_count = row_count // BLOCK
-    own = heads.reshape(arrays, block_count, BLOCK, dim)
+    pairs = kv_heads.reshape(arrays, block_count, BLOCK, dim)
+    left = from_behind(pairs, "blk", 1)
+    right = from_behind(pairs, "blk", -1)
+    qd = to_heads([query_rows, out_grad]).reshape(arrays, block_count, BLOCK, dim)
     cycle_place = lax.axis_index("blk")
     first_row = cycle_place * block_count
     picks = jnp.stack(
         [lax.dynamic_slice_in_dim(neighbour_blocks[:, c], first_row, block_count, 0) for c in range(2)]
     )
     picks = jnp.clip(picks, 0, block_count - 1).astype(jnp.int32)
-    pairs = own[1:3]
-    left = from_behind(pairs, "blk", 1)
-    right = from_behind(pairs, "blk", -1)
-    out_pair, own_grads, to_left, to_right = attention(picks, own, left, right)
+    out_pair, own_grads, to_left, to_right = attention(picks, qd, pairs, left, right)
     from_right = from_behind(to_left.astype(jnp.bfloat16), "blk", -1).astype(jnp.float32)
     from_left = from_behind(to_right.astype(jnp.bfloat16), "blk", 1).astype(jnp.float32)
+    attended, query_grad = to_rows(out_pair.reshape(2, row_count, dim))
     kv_grads = (own_grads + from_right + from_left).astype(jnp.bfloat16)
-    stacked = jnp.concatenate([out_pair, kv_grads], axis=0).reshape(4, row_count, dim)
-    attended, query_grad, key_grad, value_grad = to_rows(stacked)
+    key_grad, value_grad = to_rows(kv_grads.reshape(2, row_count, dim))
     return (attended, query_grad, key_grad, value_grad)
 
 

time: 150 us -> 149 us (level)
  blocking collectives: 61.5 us -> 0 us
  starting transfers between devices: 17.2 us -> 47.3 us
  waiting for transfers between devices: 28.7 us -> 56 us
  local copies, waits for them, and re-layouts: 17.7 us -> 20.8 us
    all_to_all x2 -> x0, blocking collectives: 61.5 us -> none  [the longest x1 35.4 us: to_heads(): lax.all_to_all(stacked, 'head', split_axis=0, concat_axis=0, tiled=True)]
    all_to_all x0 -> x4, starting transfers between devices: none -> 30.2 us  [the longest x2 15.2 us: to_rows(): lax.all_to_all(stacked, 'head', split_axis=0, concat_axis=0, tiled=True)]
    all_to_all x0 -> x4, waiting for transfers between devices: none -> 23.9 us  [the longest x2 15.2 us: to_heads(): lax.all_to_all(stacked, 'head', split_axis=0, concat_axis=0, tiled=True)]
    ppermute x4, waiting for transfers between devices: 28.7 us -> 32.1 us  [from_behind(): return lax.ppermute(value, axis, pairs)]
    another operation x1 -> x2, local copies, waits for them, and re-layouts: 0.94 us -> 3.48 us  [to_rows(): stacked.reshape(parts, count, rows // count, width).transpose(1, 0, 2, 3)]
    unnamed x14 -> x18, local copies, waits for them, and re-layouts: 7.89 us -> 6.08 us
    transpose x1 -> x2, local copies, waits for them, and re-layouts: 0.09 us -> 1.68 us  [to_heads(): stacked = stacked.transpose(2, 0, 1, 3)]
  transfers between devices with their start and end apart: 4 -> 8, of which waited for: 4 -> 7; matrix products, arithmetic and copies ran while one was open for 4% -> 11% of each run, Pallas kernels for 0% -> 0%
where the time goes in v3:
time: 149 us; the launch traced here: 148 us
  waiting for transfers between devices  56 us (38%)
  starting transfers between devices  47.3 us (32%)
  local copies, waits for them, and re-layouts  20.8 us (14%)
  Pallas kernels  18.5 us (12%)
  other arithmetic  4.68 us (3%)
    ppermute x4, waiting for transfers between devices, from_behind(): return lax.ppermute(value, axis, pairs)  32.1 us
    pallas_call x1, Pallas kernels, attention(): pl.pallas_call(attention_kernel, grid_spec=pltpu.PrefetchScalarGridSpec(n...  18.5 us
    ppermute x4, starting transfers between devices, from_behind(): return lax.ppermute(value, axis, pairs)  17.2 us
    all_to_all x2, waiting for transfers between devices, to_heads(): lax.all_to_all(stacked, 'head', split_axis=0, concat_axis=0, tiled=True)  15.2 us
    all_to_all x2, starting transfers between devices, to_rows(): lax.all_to_all(stacked, 'head', split_axis=0, concat_axis=0, tiled=True)  15.2 us
    all_to_all x2, starting transfers between devices, to_heads(): lax.all_to_all(stacked, 'head', split_axis=0, concat_axis=0, tiled=True)  14.9 us
    all_to_all x2, waiting for transfers between devices, to_rows(): lax.all_to_all(stacked, 'head', split_axis=0, concat_axis=0, tiled=True)  8.67 us
    unnamed x18, local copies, waits for them, and re-layouts  6.08 us
  transfers between devices with their start and end apart: 8, of which 7 were waited for; matrix products, arithmetic and copies ran while one was open for 11% of the time, Pallas kernels for 0%

profile of v3, /device:TPU:8, one launch (start us, length us, event | category | flops | bytes accessed | tf_op | source)
XLA Modules:
  0.0 148.2 jit_solution(12370805245133809796)
XLA Ops:
  0.6 0.0 copy-start.2
  0.6 1.2 copy.33
  1.8 0.0 copy-start.3
  1.8 1.2 copy.34
  3.0 0.1 maximum_bitcast_fusion.1
  3.0 0.8 copy.35
  3.9 9.4 %all-to-all-start.1 = ((bf16[16,2,128,64]{2,3,1,0:T(8,128)(2,1)}), bf16[16,2,128,64]{2,3,1,0:T(8,128)(2,1)S(1)}, u32[]{:S(2)}, u32[]{:S(2)}) async-start(bf16[16,2,128,64]{2,3,1,0:T(8,128)(2,1)} %copy.35), calls=%async_computation.1 | async-start | bytes 1048576 | tf_op jit(solution)/shard_map/all_to_all | solution.py:18
  13.2 0.0 copy-done.2
  13.3 0.2 copy.29
  13.4 0.0 copy-done.3
  13.4 0.2 copy.30
  13.6 0.1 maximum_bitcast_fusion
  13.7 0.8 copy.31
  14.5 0.0 copy-start.4
  14.5 13.8 %all-to-all-done.1 = bf16[16,2,128,64]{2,3,1,0:T(8,128)(2,1)S(1)} async-done(((bf16[16,2,128,64]{2,3,1,0:T(8,128)(2,1)}), bf16[16,2,128,64]{2,3,1,0:T(8,128)(2,1)S(1)}, u32[]{:S(2)}, u32[]{:S(2)}) %all-to-all-start.1) | async-done | bytes 524320 | tf_op jit(solution)/shard_map/all_to_all | solution.py:18
  28.3 5.6 %all-to-all-start = ((bf16[16,2,128,64]{2,3,1,0:T(8,128)(2,1)}), bf16[16,2,128,64]{2,3,1,0:T(8,128)(2,1)S(1)}, u32[]{:S(2)}, u32[]{:S(2)}) async-start(bf16[16,2,128,64]{2,3,1,0:T(8,128)(2,1)} %copy.31), calls=%async_computation | async-start | bytes 1048576 | tf_op jit(solution)/shard_map/all_to_all | solution.py:18
  33.9 0.5 copy.36
  34.4 0.0 copy-start
  34.4 0.3 copy.37
  34.7 10.9 %collective-permute-start.1 = (bf16[2,4,512,64]{2,3,1,0:T(8,128)(2,1)S(1)}, bf16[2,4,512,64]{2,3,1,0:T(8,128)(2,1)S(1)}, u32[]{:S(2)}, u32[]{:S(2)}) collective-permute-start(bf16[2,4,512,64]{2,3,1,0:T(8,128)(2,1)S(1)} %copy.37), channel_id=1, source_target_pairs={{0,496},{16,0},{32,16},{48,32},{64,48},{80,64},{96,80},{112,96},{1... | collective-permute-start | bytes 1572872 | tf_op jit(solution)/shard_map/ppermute | solution.py:34
  45.6 1.9 %collective-permute-start = (bf16[2,4,512,64]{2,3,1,0:T(8,128)(2,1)S(1)}, bf16[2,4,512,64]{2,3,1,0:T(8,128)(2,1)S(1)}, u32[]{:S(2)}, u32[]{:S(2)}) collective-permute-start(bf16[2,4,512,64]{2,3,1,0:T(8,128)(2,1)S(1)} %copy.37), channel_id=1, source_target_pairs={{0,16},{16,32},{32,48},{48,64},{64,80},{80,96},{96,112},{112,128},... | collective-permute-start | bytes 1572872 | tf_op jit(solution)/shard_map/ppermute | solution.py:34
  47.6 0.0 copy-done.4
  47.6 0.1 dynamic-slice_bitcast_fusion
  47.7 0.6 add_clamp_fusion.picks_ref
  48.2 1.5 all-to-all-done
  49.7 1.4 copy.32
  51.1 7.6 %collective-permute-done.1 = bf16[2,4,512,64]{2,3,1,0:T(8,128)(2,1)S(1)} collective-permute-done((bf16[2,4,512,64]{2,3,1,0:T(8,128)(2,1)S(1)}, bf16[2,4,512,64]{2,3,1,0:T(8,128)(2,1)S(1)}, u32[]{:S(2)}, u32[]{:S(2)}) %collective-permute-start.1) | collective-permute-done | bytes 524320 | tf_op jit(solution)/shard_map/ppermute | solution.py:34
  58.7 1.3 copy.40.right_ref
  60.0 0.0 copy-done
  60.0 7.5 %collective-permute-done = bf16[2,4,512,64]{2,3,1,0:T(8,128)(2,1)S(1)} collective-permute-done((bf16[2,4,512,64]{2,3,1,0:T(8,128)(2,1)S(1)}, bf16[2,4,512,64]{2,3,1,0:T(8,128)(2,1)S(1)}, u32[]{:S(2)}, u32[]{:S(2)}) %collective-permute-start) | collective-permute-done | bytes 524320 | tf_op jit(solution)/shard_map/ppermute | solution.py:34
  67.5 1.3 copy.39.left_ref
  68.8 18.5 %shard_map.84 = (bf16[2,4,512,64]{3,2,1,0:T(8,128)(2,1)}, f32[2,4,512,64]{3,2,1,0:T(8,128)}, f32[2,4,512,64]{3,2,1,0:T(8,128)}, f32[2,4,512,64]{3,2,1,0:T(8,128)}) custom-call(s32[2,4]{1,0:T(2,128)} %add_clamp_fusion.picks_ref, bf16[2,4,512,64]{3,2,1,0:T(8,128)(2,1)} %bitcast.32, bf16[2,4,512,64]{3,2,1,0:T(8,128)(2,1)} %bitcast.31, ...), custom_call_target="tpu_custom_call" | custom-call | tf_op jit(solution)/shard_map/pallas_call | solution.py:99
  87.3 2.3 %copy.41 = bf16[2,16,128,64]{2,3,0,1:T(8,128)(2,1)} copy(bf16[2,16,128,64]{3,2,1,0:T(8,128)(2,1)} %bitcast.38) | data formatting | bytes 1048576 | tf_op jit(solution)/shard_map/reshape;reshape | solution.py:25
  89.6 6.1 %all-to-all-start.2 = ((bf16[16,2,128,64]{2,3,1,0:T(8,128)(2,1)}), bf16[16,2,128,64]{2,3,1,0:T(8,128)(2,1)}, u32[]{:S(2)}, u32[]{:S(2)}) async-start(bf16[16,2,128,64]{2,3,1,0:T(8,128)(2,1)} %bitcast.13), calls=%async_computation.2 | async-start | bytes 1048576 | tf_op jit(solution)/shard_map/all_to_all | solution.py:26
  95.7 0.0 copy-start.1
  95.7 1.9 %convert_element_type.15 = bf16[2,4,512,64]{3,2,1,0:T(8,128)(2,1)S(1)} convert(f32[2,4,512,64]{3,2,1,0:T(8,128)} %get-tuple-element.10) | non-fusion elementwise | flops 262144 | bytes 1572864 | tf_op jit(solution)/shard_map/convert_element_type | solution.py:133
  97.7 1.1 copy.43
  98.8 1.9 %collective-permute-start.2 = (bf16[2,4,512,64]{2,3,1,0:T(8,128)(2,1)}, bf16[2,4,512,64]{2,3,1,0:T(8,128)(2,1)}, u32[]{:S(2)}, u32[]{:S(2)}) collective-permute-start(bf16[2,4,512,64]{2,3,1,0:T(8,128)(2,1)} %copy.43), channel_id=1, source_target_pairs={{0,496},{16,0},{32,16},{48,32},{64,48},{80,64},{96,80},{112,96},{1... | collective-permute-start | bytes 1572872 | tf_op jit(solution)/shard_map/ppermute | solution.py:34
  100.7 0.0 copy-done.1
  100.7 0.2 convert_element_type.17
  100.9 0.3 copy.45
  101.2 2.4 %collective-permute-start.3 = (bf16[2,4,512,64]{2,3,1,0:T(8,128)(2,1)S(1)}, bf16[2,4,512,64]{2,3,1,0:T(8,128)(2,1)S(1)}, u32[]{:S(2)}, u32[]{:S(2)}) collective-permute-start(bf16[2,4,512,64]{2,3,1,0:T(8,128)(2,1)S(1)} %copy.45), channel_id=1, source_target_pairs={{0,16},{16,32},{32,48},{48,64},{64,80},{80,96},{96,112},{112,128},... | collective-permute-start | bytes 1572872 | tf_op jit(solution)/shard_map/ppermute | solution.py:34
  103.6 5.4 %collective-permute-done.2 = bf16[2,4,512,64]{2,3,1,0:T(8,128)(2,1)} collective-permute-done((bf16[2,4,512,64]{2,3,1,0:T(8,128)(2,1)}, bf16[2,4,512,64]{2,3,1,0:T(8,128)(2,1)}, u32[]{:S(2)}, u32[]{:S(2)}) %collective-permute-start.2) | collective-permute-done | bytes 524320 | tf_op jit(solution)/shard_map/ppermute | solution.py:34
  109.1 1.5 %copy.44 = bf16[2,4,512,64]{3,2,1,0:T(8,128)(2,1)S(1)} copy(bf16[2,4,512,64]{2,3,1,0:T(8,128)(2,1)} %collective-permute-done.2) | data formatting | bytes 1048576 | tf_op jit(solution)/shard_map/ppermute | solution.py:34
  110.6 11.7 %collective-permute-done.3 = bf16[2,4,512,64]{2,3,1,0:T(8,128)(2,1)S(1)} collective-permute-done((bf16[2,4,512,64]{2,3,1,0:T(8,128)(2,1)S(1)}, bf16[2,4,512,64]{2,3,1,0:T(8,128)(2,1)S(1)}, u32[]{:S(2)}, u32[]{:S(2)}) %collective-permute-start.3) | collective-permute-done | bytes 524320 | tf_op jit(solution)/shard_map/ppermute | solution.py:34
  122.3 0.5 copy.46
  122.7 1.9 %add_convert_fusion = bf16[2,4,512,64]{3,2,1,0:T(8,128)(2,1)S(1)} fusion(bf16[2,4,512,64]{3,2,1,0:T(8,128)(2,1)S(1)} %copy.46, f32[2,4,512,64]{3,2,1,0:T(8,128)} %get-tuple-element.9, bf16[2,4,512,64]{3,2,1,0:T(8,128)(2,1)S(1)} %copy.44), kind=kLoop, calls=%fused_computation | loop fusion | flops 1310720 | bytes 2621440 | tf_op jit(solution)/shard_map/convert_element_type | solution.py:136
  124.7 1.1 copy.47
  125.8 0.0 all-to-all-done.2
  125.8 9.1 %all-to-all-start.3 = ((bf16[16,2,128,64]{2,3,1,0:T(8,128)(2,1)}), bf16[16,2,128,64]{2,3,1,0:T(8,128)(2,1)S(1)}, u32[]{:S(2)}, u32[]{:S(2)}) async-start(bf16[16,2,128,64]{2,3,1,0:T(8,128)(2,1)} %bitcast.18), calls=%async_computation.3 | async-start | bytes 1048576 | tf_op jit(solution)/shard_map/all_to_all | solution.py:26
  135.0 1.1 copy.56
  136.1 0.9 copy.50
  136.9 0.8 copy.49
  137.8 8.7 %all-to-all-done.3 = bf16[16,2,128,64]{2,3,1,0:T(8,128)(2,1)S(1)} async-done(((bf16[16,2,128,64]{2,3,1,0:T(8,128)(2,1)}), bf16[16,2,128,64]{2,3,1,0:T(8,128)(2,1)S(1)}, u32[]{:S(2)}, u32[]{:S(2)}) %all-to-all-start.3) | async-done | bytes 524320 | tf_op jit(solution)/shard_map/all_to_all | solution.py:26
  146.5 0.9 copy.52
  147.4 0.8 copy.51
  (4 shorter events, 0.1 us)
Async XLA Ops:
  0.6 12.6 %copy-start.2 = (bf16[128,1024]{1,0:T(8,128)(2,1)S(1)}, bf16[128,1024]{1,0:T(8,128)(2,1)}, u32[]{:S(2)}) copy-start(bf16[128,1024]{1,0:T(8,128)(2,1)} %param.5) | copy-start | bytes 786436
  1.8 11.6 %copy-start.3 = (bf16[128,1024]{1,0:T(8,128)(2,1)S(1)}, bf16[128,1024]{1,0:T(8,128)(2,1)}, u32[]{:S(2)}) copy-start(bf16[128,1024]{1,0:T(8,128)(2,1)} %param.8) | copy-start | bytes 786436
  3.9 24.4 %all-to-all-start.1 = ((bf16[16,2,128,64]{2,3,1,0:T(8,128)(2,1)}), bf16[16,2,128,64]{2,3,1,0:T(8,128)(2,1)S(1)}, u32[]{:S(2)}, u32[]{:S(2)}) async-start(bf16[16,2,128,64]{2,3,1,0:T(8,128)(2,1)} %copy.35), calls=%async_computation.1 | async-start | bytes 1048576 | tf_op jit(solution)/shard_map/all_to_all | solution.py:18
  14.5 33.0 %copy-start.4 = (s32[128,2]{0,1:T(2,128)S(1)}, s32[128,2]{0,1:T(2,128)}, u32[]{:S(2)}) copy-start(s32[128,2]{0,1:T(2,128)} %param.9) | copy-start | bytes 3076
  28.3 21.4 %all-to-all-start = ((bf16[16,2,128,64]{2,3,1,0:T(8,128)(2,1)}), bf16[16,2,128,64]{2,3,1,0:T(8,128)(2,1)S(1)}, u32[]{:S(2)}, u32[]{:S(2)}) async-start(bf16[16,2,128,64]{2,3,1,0:T(8,128)(2,1)} %copy.31), calls=%async_computation | async-start | bytes 1048576 | tf_op jit(solution)/shard_map/all_to_all | solution.py:18
  34.4 25.7 %copy-start = (bf16[2,16,128,64]{3,2,1,0:T(8,128)(2,1)}, bf16[2,16,128,64]{3,2,1,0:T(8,128)(2,1)S(1)}, u32[]{:S(2)}) copy-start(bf16[2,16,128,64]{3,2,1,0:T(8,128)(2,1)S(1)} %copy.36) | copy-start | bytes 1572868
  34.7 24.0 %collective-permute-start.1 = (bf16[2,4,512,64]{2,3,1,0:T(8,128)(2,1)S(1)}, bf16[2,4,512,64]{2,3,1,0:T(8,128)(2,1)S(1)}, u32[]{:S(2)}, u32[]{:S(2)}) collective-permute-start(bf16[2,4,512,64]{2,3,1,0:T(8,128)(2,1)S(1)} %copy.37), channel_id=1, source_target_pairs={{0,496},{16,0},{32,16},{48,32},{64,48},{80,64},{96,80},{112,96},{1... | collective-permute-start | bytes 1572872 | tf_op jit(solution)/shard_map/ppermute | solution.py:34
  45.6 21.9 %collective-permute-start = (bf16[2,4,512,64]{2,3,1,0:T(8,128)(2,1)S(1)}, bf16[2,4,512,64]{2,3,1,0:T(8,128)(2,1)S(1)}, u32[]{:S(2)}, u32[]{:S(2)}) collective-permute-start(bf16[2,4,512,64]{2,3,1,0:T(8,128)(2,1)S(1)} %copy.37), channel_id=1, source_target_pairs={{0,16},{16,32},{32,48},{48,64},{64,80},{80,96},{96,112},{112,128},... | collective-permute-start | bytes 1572872 | tf_op jit(solution)/shard_map/ppermute | solution.py:34
  89.6 36.2 %all-to-all-start.2 = ((bf16[16,2,128,64]{2,3,1,0:T(8,128)(2,1)}), bf16[16,2,128,64]{2,3,1,0:T(8,128)(2,1)}, u32[]{:S(2)}, u32[]{:S(2)}) async-start(bf16[16,2,128,64]{2,3,1,0:T(8,128)(2,1)} %bitcast.13), calls=%async_computation.2 | async-start | bytes 1048576 | tf_op jit(solution)/shard_map/all_to_all | solution.py:26
  95.7 5.0 %copy-start.1 = (f32[2,4,512,64]{3,2,1,0:T(8,128)S(1)}, f32[2,4,512,64]{3,2,1,0:T(8,128)}, u32[]{:S(2)}) copy-start(f32[2,4,512,64]{3,2,1,0:T(8,128)} %get-tuple-element.11) | copy-start | bytes 3145732
  98.8 10.3 %collective-permute-start.2 = (bf16[2,4,512,64]{2,3,1,0:T(8,128)(2,1)}, bf16[2,4,512,64]{2,3,1,0:T(8,128)(2,1)}, u32[]{:S(2)}, u32[]{:S(2)}) collective-permute-start(bf16[2,4,512,64]{2,3,1,0:T(8,128)(2,1)} %copy.43), channel_id=1, source_target_pairs={{0,496},{16,0},{32,16},{48,32},{64,48},{80,64},{96,80},{112,96},{1... | collective-permute-start | bytes 1572872 | tf_op jit(solution)/shard_map/ppermute | solution.py:34
  101.2 21.0 %collective-permute-start.3 = (bf16[2,4,512,64]{2,3,1,0:T(8,128)(2,1)S(1)}, bf16[2,4,512,64]{2,3,1,0:T(8,128)(2,1)S(1)}, u32[]{:S(2)}, u32[]{:S(2)}) collective-permute-start(bf16[2,4,512,64]{2,3,1,0:T(8,128)(2,1)S(1)} %copy.45), channel_id=1, source_target_pairs={{0,16},{16,32},{32,48},{48,64},{64,80},{80,96},{96,112},{112,128},... | collective-permute-start | bytes 1572872 | tf_op jit(solution)/shard_map/ppermute | solution.py:34
  125.8 20.6 %all-to-all-start.3 = ((bf16[16,2,128,64]{2,3,1,0:T(8,128)(2,1)}), bf16[16,2,128,64]{2,3,1,0:T(8,128)(2,1)S(1)}, u32[]{:S(2)}, u32[]{:S(2)}) async-start(bf16[16,2,128,64]{2,3,1,0:T(8,128)(2,1)} %bitcast.18), calls=%async_computation.3 | async-start | bytes 1048576 | tf_op jit(solution)/shard_map/all_to_all | solution.py:26

commit v4 on v3

v4 whole, which is shorter than its diff:
```python
import jax
import jax.numpy as jnp
from jax import lax
from jax.experimental import pallas as pl
from jax.experimental.pallas import tpu as pltpu
from jax.sharding import PartitionSpec as P

HEAD_DIM = 64
BLOCK = 512
INTERPRET = False


def to_heads(first, second):
    count = lax.axis_size("head")
    rows, width = first.shape
    split = [a.reshape(rows, count, width // count) for a in (first, second)]
    packed = jnp.concatenate(split, axis=2)
    moved = lax.all_to_all(packed, "head", split_axis=1, concat_axis=0, tiled=True)
    return moved.reshape(count * rows, 2 * width // count)


def to_rows(packed):
    count = lax.axis_size("head")
    rows, width = packed.shape
    moved = lax.all_to_all(packed, "head", split_axis=0, concat_axis=1, tiled=True)
    moved = moved.reshape(rows // count, count, 2, width // 2)
    return [moved[:, :, i].reshape(rows // count, count * width // 2) for i in range(2)]


def from_behind(value, axis, steps):
    count = lax.axis_size(axis)
    pairs = [(source, (source + steps) % count) for source in range(count)]
    return lax.ppermute(value, axis, pairs)


def attention_kernel(
    picks_ref, qd_ref, kv_ref, left_ref, right_ref,
    out_ref, own_grad_ref, to_left_ref, to_right_ref, left_acc, right_acc,
):
    number = pl.program_id(0)
    scale = HEAD_DIM ** (-0.5)
    f32 = jnp.float32

    @pl.when(number == 0)
    def _():
        left_acc[...] = jnp.zeros(left_acc.shape, f32)
        right_acc[...] = jnp.zeros(right_acc.shape, f32)

    packed = qd_ref[0]
    lane = lax.broadcasted_iota(jnp.int32, packed.shape, 1)
    low = lane < HEAD_DIM
    zero = jnp.zeros_like(packed)
    query_ext = jnp.where(low, packed, zero)
    grad_ext = jnp.where(low, zero, packed)
    pairs = (kv_ref[0], left_ref[0], right_ref[0])

    def nt(a, b):
        return lax.dot_general(a, b, (((1,), (1,)), ((), ())), preferred_element_type=f32)

    def nn(a, b):
        return lax.dot_general(a, b, (((1,), (0,)), ((), ())), preferred_element_type=f32)

    def tn(a, b):
        return lax.dot_general(a, b, (((0,), (0,)), ((), ())), preferred_element_type=f32)

    scores = [nt(query_ext, pair) * scale for pair in pairs]
    row = lax.broadcasted_iota(jnp.int32, scores[0].shape, 0)
    col = lax.broadcasted_iota(jnp.int32, scores[0].shape, 1)
    scores[0] = jnp.where(col <= row, scores[0], -jnp.inf)
    highest = jnp.max(scores[0], axis=1, keepdims=True)
    for part in scores[1:]:
        highest = jnp.maximum(highest, jnp.max(part, axis=1, keepdims=True))
    total = sum(jnp.sum(jnp.exp(part - highest), axis=1, keepdims=True) for part in scores)
    log_total = highest + jnp.log(total)
    weights = [jnp.exp(part - log_total) for part in scores]
    weights_bf = [w.astype(jnp.bfloat16) for w in weights]
    attended = sum(nn(w, pair) for w, pair in zip(weights_bf, pairs)).astype(jnp.bfloat16)
    products = jnp.where(low, 0.0, packed.astype(f32) * attended.astype(f32))
    row_delta = jnp.sum(products, axis=1, keepdims=True)
    score_grads = [
        (w * (nt(grad_ext, pair) - row_delta)).astype(jnp.bfloat16) for w, pair in zip(weights, pairs)
    ]
    query_grad = (sum(nn(d, pair) for d, pair in zip(score_grads, pairs)) * scale).astype(jnp.bfloat16)
    out_ref[0] = jnp.where(low, query_grad, attended)
    key_parts = [tn(d, packed) * scale for d in score_grads]
    value_parts = [tn(w, packed) for w in weights_bf]
    kv_parts = [jnp.where(low, k, v) for k, v in zip(key_parts, value_parts)]
    own_grad_ref[0] = kv_parts[0]
    left_pick = picks_ref[0, number]
    right_pick = picks_ref[1, number]
    left_acc[left_pick] += kv_parts[1]
    right_acc[right_pick] += kv_parts[2]

    @pl.when(number == pl.num_programs(0) - 1)
    def _():
        to_left_ref[...] = left_acc[...].astype(jnp.bfloat16)
        to_right_ref[...] = right_acc[...].astype(jnp.bfloat16)


def attention(picks, qd, kv, left, right):
    block_count, block, width = kv.shape
    left_spec = pl.BlockSpec((1, block, width), lambda n, p: (p[0, n], 0, 0))
    right_spec = pl.BlockSpec((1, block, width), lambda n, p: (p[1, n], 0, 0))
    one_spec = pl.BlockSpec((1, block, width), lambda n, p: (n, 0, 0))
    whole_spec = pl.BlockSpec((block_count, block, width), lambda n, p: (0, 0, 0))
    shape = (block_count, block, width)
    return pl.pallas_call(
        attention_kernel,
        grid_spec=pltpu.PrefetchScalarGridSpec(
            num_scalar_prefetch=1,
            grid=(block_count,),
            in_specs=[one_spec, one_spec, left_spec, right_spec],
            out_specs=[one_spec, one_spec, whole_spec, whole_spec],
            scratch_shapes=[pltpu.VMEM(shape, jnp.float32), pltpu.VMEM(shape, jnp.float32)],
        ),
        out_shape=[
            jax.ShapeDtypeStruct(shape, jnp.bfloat16),
            jax.ShapeDtypeStruct(shape, jnp.float32),
            jax.ShapeDtypeStruct(shape, jnp.bfloat16),
            jax.ShapeDtypeStruct(shape, jnp.bfloat16),
        ],
        compiler_params=pltpu.CompilerParams(dimension_semantics=("arbitrary",)),
        interpret=INTERPRET,
    )(picks, qd, kv, left, right)


def shards(query_rows, key_rows, value_rows, out_grad, neighbour_blocks):
    kv_heads = to_heads(key_rows, value_rows)
    row_count, width = kv_heads.shape
    block_count = row_count // BLOCK
    kv = kv_heads.reshape(block_count, BLOCK, width)
    left = from_behind(kv, "blk", 1)
    right = from_behind(kv, "blk", -1)
    qd = to_heads(query_rows, out_grad).reshape(block_count, BLOCK, width)
    first_row = lax.axis_index("blk") * block_count
    picks = jnp.stack(
        [lax.dynamic_slice_in_dim(neighbour_blocks[:, c], first_row, block_count, 0) for c in range(2)]
    )
    picks = jnp.clip(picks, 0, block_count - 1).astype(jnp.int32)
    out_pair, own_grads, to_left, to_right = attention(picks, qd, kv, left, right)
    from_right = from_behind(to_left, "blk", -1).astype(jnp.float32)
    from_left = from_behind(to_right, "blk", 1).astype(jnp.float32)
    query_grad, attended = to_rows(out_pair.reshape(row_count, width))
    kv_grads = (own_grads + from_right + from_left).astype(jnp.bfloat16)
    key_grad, value_grad = to_rows(kv_grads.reshape(row_count, width))
    return (attended, query_grad, key_grad, value_grad)


def solution(mesh):
    in_specs = (
        P(("blk", "head"), None),
        P(("blk", "head"), None),
        P(("blk", "head"), None),
        P(("blk", "head"), None),
        P(),
    )
    out_specs = (
        P(("blk", "head"), None),
        P(("blk", "head"), None),
        P(("blk", "head"), None),
        P(("blk", "head"), None),
    )
    return jax.shard_map(shards, mesh=mesh, in_specs=in_specs, out_specs=out_specs, check_vma=False)
```

time: 149 us -> 141 us (0.946)
  local copies, waits for them, and re-layouts: 20.8 us -> 11.9 us
  waiting for transfers between devices: 56 us -> 61.3 us
  other arithmetic: 4.68 us -> 2.44 us
    ppermute x4, waiting for transfers between devices: 32.1 us -> 36.9 us  [from_behind(): return lax.ppermute(value, axis, pairs)]
    ppermute x4 -> x0, local copies, waits for them, and re-layouts: 4.64 us -> none  [from_behind(): return lax.ppermute(value, axis, pairs)]
    another operation x3 -> x0, local copies, waits for them, and re-layouts: 3.81 us -> none  [the longest x2 3.48 us: to_rows(): stacked.reshape(parts, count, rows // count, width).transpose(1, 0, 2, 3)]
    transpose x4 -> x0, local copies, waits for them, and re-layouts: 3.59 us -> none  [the longest x2 1.91 us: to_heads(): moved.transpose(1, 0, 2, 3)]
    all_to_all x2 -> x4, local copies, waits for them, and re-layouts: 1.11 us -> 4.46 us  [the longest x2 3.17 us: to_rows(): lax.all_to_all(packed, 'head', split_axis=0, concat_axis=1, tiled=True)]
    convert_element_type x2 -> x0, other arithmetic: 2.07 us -> none  [the longest x1 1.9 us: shards(): to_left.astype(jnp.bfloat16)]
    convert_element_type x1, other arithmetic: 1.94 us -> 0.17 us  [shards(): kv_grads = (own_grads + from_right + from_left).astype(jnp.bfloat16)]
    concatenate x0 -> x2, other arithmetic: none -> 1.69 us  [to_heads(): packed = jnp.concatenate(split, axis=2)]
  transfers between devices with their start and end apart: 8 -> 8, of which waited for: 7 -> 7; matrix products, arithmetic and copies ran while one was open for 11% -> 4% of each run, Pallas kernels for 0% -> 0%
where the time goes in v4:
time: 141 us; the launch traced here: 140 us
  waiting for transfers between devices  61.3 us (43%)
  starting transfers between devices  46 us (33%)
  Pallas kernels  17.7 us (13%)
  local copies, waits for them, and re-layouts  11.9 us (8%)
  other arithmetic  2.44 us (2%)
    ppermute x4, waiting for transfers between devices, from_behind(): return lax.ppermute(value, axis, pairs)  36.9 us
    pallas_call x1, Pallas kernels, attention(): pl.pallas_call(attention_kernel, grid_spec=pltpu.PrefetchScalarGridSpec(n...  17.7 us
    ppermute x4, starting transfers between devices, from_behind(): return lax.ppermute(value, axis, pairs)  17.2 us
    all_to_all x2, starting transfers between devices, to_heads(): lax.all_to_all(packed, 'head', split_axis=1, concat_axis=0, tiled=True)  15.1 us
    all_to_all x2, waiting for transfers between devices, to_heads(): lax.all_to_all(packed, 'head', split_axis=1, concat_axis=0, tiled=True)  14.6 us
    all_to_all x2, starting transfers between devices, to_rows(): lax.all_to_all(packed, 'head', split_axis=0, concat_axis=1, tiled=True)  13.7 us
    all_to_all x2, waiting for transfers between devices, to_rows(): lax.all_to_all(packed, 'head', split_axis=0, concat_axis=1, tiled=True)  9.75 us
    unnamed x28, local copies, waits for them, and re-layouts  7.31 us
  transfers between devices with their start and end apart: 8, of which 7 were waited for; matrix products, arithmetic and copies ran while one was open for 4% of the time, Pallas kernels for 0%

profile of v4, /device:TPU:8, one launch (start us, length us, event | category | flops | bytes accessed | tf_op | source)
XLA Modules:
  0.0 140.1 jit_solution(16618741352397825804)
XLA Ops:
  0.6 0.0 copy-start.4
  0.6 1.2 copy.20
  1.8 0.0 copy-done.4
  1.8 0.2 copy.21
  2.0 0.8 pad_maximum_fusion.1
  2.8 0.0 copy-start.5
  2.8 9.5 %all-to-all-start.1 = ((bf16[128,16,128]{0,2,1:T(8,128)(2,1)}), bf16[128,16,128]{0,2,1:T(8,128)(2,1)S(1)}, u32[]{:S(2)}, u32[]{:S(2)}) async-start(bf16[128,16,128]{0,2,1:T(8,128)(2,1)} %pad_maximum_fusion.1), calls=%async_computation.1 | async-start | bytes 1048576 | tf_op jit(solution)/shard_map/all_to_all | solution.py:18
  12.3 0.0 copy-done.5
  12.3 0.0 copy-start.6
  12.4 0.2 copy.17
  12.5 0.8 copy-done.6
  13.3 0.2 copy.18
  13.5 0.8 pad_maximum_fusion
  14.3 13.1 %all-to-all-done.1 = bf16[128,16,128]{0,2,1:T(8,128)(2,1)S(1)} async-done(((bf16[128,16,128]{0,2,1:T(8,128)(2,1)}), bf16[128,16,128]{0,2,1:T(8,128)(2,1)S(1)}, u32[]{:S(2)}, u32[]{:S(2)}) %all-to-all-start.1) | async-done | bytes 524320 | tf_op jit(solution)/shard_map/all_to_all | solution.py:18
  27.4 5.6 %all-to-all-start = ((bf16[128,16,128]{0,2,1:T(8,128)(2,1)}), bf16[128,16,128]{0,2,1:T(8,128)(2,1)S(1)}, u32[]{:S(2)}, u32[]{:S(2)}) async-start(bf16[128,16,128]{0,2,1:T(8,128)(2,1)} %pad_maximum_fusion), calls=%async_computation | async-start | bytes 1048576 | tf_op jit(solution)/shard_map/all_to_all | solution.py:18
  33.0 0.3 copy.22
  33.2 0.0 copy-start
  33.3 10.9 %collective-permute-start.1 = (bf16[4,512,128]{2,1,0:T(8,128)(2,1)S(1)}, bf16[4,512,128]{2,1,0:T(8,128)(2,1)S(1)}, u32[]{:S(2)}, u32[]{:S(2)}) collective-permute-start(bf16[4,512,128]{2,1,0:T(8,128)(2,1)S(1)} %bitcast.33), channel_id=1, source_target_pairs={{0,496},{16,0},{32,16},{48,32},{64,48},{80,64},{96,80},{112,96},{1... | collective-permute-start | bytes 1572872 | tf_op jit(solution)/shard_map/ppermute | solution.py:33
  44.2 1.9 %collective-permute-start = (bf16[4,512,128]{2,1,0:T(8,128)(2,1)S(1)}, bf16[4,512,128]{2,1,0:T(8,128)(2,1)S(1)}, u32[]{:S(2)}, u32[]{:S(2)}) collective-permute-start(bf16[4,512,128]{2,1,0:T(8,128)(2,1)S(1)} %bitcast.34), channel_id=1, source_target_pairs={{0,16},{16,32},{32,48},{48,64},{64,80},{80,96},{96,112},{112,128},... | collective-permute-start | bytes 1572872 | tf_op jit(solution)/shard_map/ppermute | solution.py:33
  46.1 0.0 copy-start.7
  46.1 0.7 copy-done.7
  46.8 0.1 dynamic-slice_bitcast_fusion
  46.9 0.6 add_clamp_fusion.picks_ref
  47.5 1.5 %all-to-all-done = bf16[128,16,128]{0,2,1:T(8,128)(2,1)S(1)} async-done(((bf16[128,16,128]{0,2,1:T(8,128)(2,1)}), bf16[128,16,128]{0,2,1:T(8,128)(2,1)S(1)}, u32[]{:S(2)}, u32[]{:S(2)}) %all-to-all-start) | async-done | bytes 524320 | tf_op jit(solution)/shard_map/all_to_all | solution.py:18
  49.0 1.0 copy.19
  50.0 0.0 copy-done
  50.0 7.4 %collective-permute-done.1.right_ref = bf16[4,512,128]{2,1,0:T(8,128)(2,1)S(1)} collective-permute-done((bf16[4,512,128]{2,1,0:T(8,128)(2,1)S(1)}, bf16[4,512,128]{2,1,0:T(8,128)(2,1)S(1)}, u32[]{:S(2)}, u32[]{:S(2)}) %collective-permute-start.1) | collective-permute-done | bytes 524320 | tf_op jit(solution)/shard_map/ppermute | solution.py:33
  57.4 0.0 copy-start.2
  57.4 8.8 %collective-permute-done.left_ref = bf16[4,512,128]{2,1,0:T(8,128)(2,1)S(1)} collective-permute-done((bf16[4,512,128]{2,1,0:T(8,128)(2,1)S(1)}, bf16[4,512,128]{2,1,0:T(8,128)(2,1)S(1)}, u32[]{:S(2)}, u32[]{:S(2)}) %collective-permute-start) | collective-permute-done | bytes 524320 | tf_op jit(solution)/shard_map/ppermute | solution.py:33
  66.2 0.0 copy-start.3
  66.2 0.0 copy-done.2
  66.2 0.8 copy-done.3
  67.0 17.7 %shard_map.84 = (bf16[4,512,128]{2,1,0:T(8,128)(2,1)}, f32[4,512,128]{2,1,0:T(8,128)}, bf16[4,512,128]{2,1,0:T(8,128)(2,1)}, bf16[4,512,128]{2,1,0:T(8,128)(2,1)}) custom-call(s32[2,4]{1,0:T(2,128)} %add_clamp_fusion.picks_ref, bf16[4,512,128]{2,1,0:T(8,128)(2,1)} %bitcast.36, bf16[4,512,128]{2,1,0:T(8,128)(2,1)} %bitcast.35, ...), custom_call_target="tpu_custom_call" | custom-call | tf_op jit(solution)/shard_map/pallas_call | solution.py:107
  84.7 0.0 copy-start.1
  84.7 2.2 %copy.23 = bf16[16,128,128]{1,2,0:T(8,128)(2,1)} copy(bf16[16,128,128]{2,1,0:T(8,128)(2,1)} %bitcast.45) | data formatting | bytes 1048576 | tf_op jit(solution)/shard_map/all_to_all | solution.py:25
  86.8 0.0 copy-start.9
  86.8 0.0 copy-start.8
  86.9 6.5 %all-to-all-start.2 = ((bf16[16,128,128]{1,2,0:T(8,128)(2,1)}), bf16[16,128,128]{1,2,0:T(8,128)(2,1)S(1)}, u32[]{:S(2)}, u32[]{:S(2)}) async-start(bf16[16,128,128]{1,2,0:T(8,128)(2,1)} %copy.23), calls=%async_computation.2 | async-start | bytes 1048576 | tf_op jit(solution)/shard_map/all_to_all | solution.py:25
  93.4 0.0 copy-done.9
  93.4 1.9 %collective-permute-start.2 = (bf16[4,512,128]{2,1,0:T(8,128)(2,1)S(1)}, bf16[4,512,128]{2,1,0:T(8,128)(2,1)S(1)}, u32[]{:S(2)}, u32[]{:S(2)}) collective-permute-start(bf16[4,512,128]{2,1,0:T(8,128)(2,1)S(1)} %copy-done.9), channel_id=1, source_target_pairs={{0,496},{16,0},{32,16},{48,32},{64,48},{80,64},{96,80},{112,96},{1... | collective-permute-start | bytes 1572872 | tf_op jit(solution)/shard_map/ppermute | solution.py:33
  95.3 0.0 copy-done.8
  95.3 2.4 %collective-permute-start.3 = (bf16[4,512,128]{2,1,0:T(8,128)(2,1)S(1)}, bf16[4,512,128]{2,1,0:T(8,128)(2,1)S(1)}, u32[]{:S(2)}, u32[]{:S(2)}) collective-permute-start(bf16[4,512,128]{2,1,0:T(8,128)(2,1)S(1)} %copy-done.8), channel_id=1, source_target_pairs={{0,16},{16,32},{32,48},{48,64},{64,80},{80,96},{96,112},{112,128},... | collective-permute-start | bytes 1572872 | tf_op jit(solution)/shard_map/ppermute | solution.py:33
  97.7 10.7 %collective-permute-done.2 = bf16[4,512,128]{2,1,0:T(8,128)(2,1)S(1)} collective-permute-done((bf16[4,512,128]{2,1,0:T(8,128)(2,1)S(1)}, bf16[4,512,128]{2,1,0:T(8,128)(2,1)S(1)}, u32[]{:S(2)}, u32[]{:S(2)}) %collective-permute-start.2) | collective-permute-done | bytes 524320 | tf_op jit(solution)/shard_map/ppermute | solution.py:33
  108.4 10.0 %collective-permute-done.3 = bf16[4,512,128]{2,1,0:T(8,128)(2,1)S(1)} collective-permute-done((bf16[4,512,128]{2,1,0:T(8,128)(2,1)S(1)}, bf16[4,512,128]{2,1,0:T(8,128)(2,1)S(1)}, u32[]{:S(2)}, u32[]{:S(2)}) %collective-permute-start.3) | collective-permute-done | bytes 524320 | tf_op jit(solution)/shard_map/ppermute | solution.py:33
  118.4 0.0 copy-done.1
  118.4 0.2 add_convert_fusion
  118.6 1.0 copy.24
  119.6 0.0 all-to-all-done.2
  119.6 7.2 %all-to-all-start.3 = ((bf16[16,128,128]{1,2,0:T(8,128)(2,1)}), bf16[16,128,128]{1,2,0:T(8,128)(2,1)S(1)}, u32[]{:S(2)}, u32[]{:S(2)}) async-start(bf16[16,128,128]{1,2,0:T(8,128)(2,1)} %copy.24), calls=%async_computation.3 | async-start | bytes 1048576 | tf_op jit(solution)/shard_map/all_to_all | solution.py:25
  126.9 0.9 copy.26
  127.7 0.8 copy.25
  128.6 9.7 %all-to-all-done.3 = bf16[16,128,128]{1,2,0:T(8,128)(2,1)S(1)} async-done(((bf16[16,128,128]{1,2,0:T(8,128)(2,1)}), bf16[16,128,128]{1,2,0:T(8,128)(2,1)S(1)}, u32[]{:S(2)}, u32[]{:S(2)}) %all-to-all-start.3) | async-done | bytes 524320 | tf_op jit(solution)/shard_map/all_to_all | solution.py:25
  138.4 0.9 copy.28
  139.2 0.8 copy.27
  (3 shorter events, 0.1 us)
Async XLA Ops:
  0.6 1.2 copy-start.4
  2.8 9.5 %copy-start.5 = (bf16[128,1024]{1,0:T(8,128)(2,1)S(1)}, bf16[128,1024]{1,0:T(8,128)(2,1)}, u32[]{:S(2)}) copy-start(bf16[128,1024]{1,0:T(8,128)(2,1)} %param.5) | copy-start | bytes 786436
  2.8 24.6 %all-to-all-start.1 = ((bf16[128,16,128]{0,2,1:T(8,128)(2,1)}), bf16[128,16,128]{0,2,1:T(8,128)(2,1)S(1)}, u32[]{:S(2)}, u32[]{:S(2)}) async-start(bf16[128,16,128]{0,2,1:T(8,128)(2,1)} %pad_maximum_fusion.1), calls=%async_computation.1 | async-start | bytes 1048576 | tf_op jit(solution)/shard_map/all_to_all | solution.py:18
  12.3 1.0 copy-start.6
  27.4 21.6 %all-to-all-start = ((bf16[128,16,128]{0,2,1:T(8,128)(2,1)}), bf16[128,16,128]{0,2,1:T(8,128)(2,1)S(1)}, u32[]{:S(2)}, u32[]{:S(2)}) async-start(bf16[128,16,128]{0,2,1:T(8,128)(2,1)} %pad_maximum_fusion), calls=%async_computation | async-start | bytes 1048576 | tf_op jit(solution)/shard_map/all_to_all | solution.py:18
  33.2 16.7 %copy-start = (bf16[16,128,1,128]{3,1,0,2:T(8,128)(2,1)}, bf16[16,128,1,128]{3,1,0,2:T(8,128)(2,1)S(1)}, u32[]{:S(2)}) copy-start(bf16[16,128,1,128]{3,1,0,2:T(8,128)(2,1)S(1)} %copy.22) | copy-start | bytes 1572868
  33.3 24.1 %collective-permute-start.1 = (bf16[4,512,128]{2,1,0:T(8,128)(2,1)S(1)}, bf16[4,512,128]{2,1,0:T(8,128)(2,1)S(1)}, u32[]{:S(2)}, u32[]{:S(2)}) collective-permute-start(bf16[4,512,128]{2,1,0:T(8,128)(2,1)S(1)} %bitcast.33), channel_id=1, source_target_pairs={{0,496},{16,0},{32,16},{48,32},{64,48},{80,64},{96,80},{112,96},{1... | collective-permute-start | bytes 1572872 | tf_op jit(solution)/shard_map/ppermute | solution.py:33
  44.2 22.0 %collective-permute-start = (bf16[4,512,128]{2,1,0:T(8,128)(2,1)S(1)}, bf16[4,512,128]{2,1,0:T(8,128)(2,1)S(1)}, u32[]{:S(2)}, u32[]{:S(2)}) collective-permute-start(bf16[4,512,128]{2,1,0:T(8,128)(2,1)S(1)} %bitcast.34), channel_id=1, source_target_pairs={{0,16},{16,32},{32,48},{48,64},{64,80},{80,96},{96,112},{112,128},... | collective-permute-start | bytes 1572872 | tf_op jit(solution)/shard_map/ppermute | solution.py:33
  46.1 0.7 copy-start.7
  57.4 8.8 %copy-start.2 = (bf16[4,512,128]{2,1,0:T(8,128)(2,1)}, bf16[4,512,128]{2,1,0:T(8,128)(2,1)S(1)}, u32[]{:S(2)}) copy-start(bf16[4,512,128]{2,1,0:T(8,128)(2,1)S(1)} %collective-permute-done.1.right_ref) | copy-start | bytes 1572868
  66.2 0.8 copy-start.3
  84.7 33.7 %copy-start.1 = (f32[4,512,128]{2,1,0:T(8,128)S(1)}, f32[4,512,128]{2,1,0:T(8,128)}, u32[]{:S(2)}) copy-start(f32[4,512,128]{2,1,0:T(8,128)} %get-tuple-element.9) | copy-start | bytes 3145732
  86.8 6.5 %copy-start.9 = (bf16[4,512,128]{2,1,0:T(8,128)(2,1)S(1)}, bf16[4,512,128]{2,1,0:T(8,128)(2,1)}, u32[]{:S(2)}) copy-start(bf16[4,512,128]{2,1,0:T(8,128)(2,1)} %get-tuple-element.10) | copy-start | bytes 1572868
  86.8 8.5 %copy-start.8 = (bf16[4,512,128]{2,1,0:T(8,128)(2,1)S(1)}, bf16[4,512,128]{2,1,0:T(8,128)(2,1)}, u32[]{:S(2)}) copy-start(bf16[4,512,128]{2,1,0:T(8,128)(2,1)} %get-tuple-element.11) | copy-start | bytes 1572868
  86.9 32.8 %all-to-all-start.2 = ((bf16[16,128,128]{1,2,0:T(8,128)(2,1)}), bf16[16,128,128]{1,2,0:T(8,128)(2,1)S(1)}, u32[]{:S(2)}, u32[]{:S(2)}) async-start(bf16[16,128,128]{1,2,0:T(8,128)(2,1)} %copy.23), calls=%async_computation.2 | async-start | bytes 1048576 | tf_op jit(solution)/shard_map/all_to_all | solution.py:25
  93.4 15.0 %collective-permute-start.2 = (bf16[4,512,128]{2,1,0:T(8,128)(2,1)S(1)}, bf16[4,512,128]{2,1,0:T(8,128)(2,1)S(1)}, u32[]{:S(2)}, u32[]{:S(2)}) collective-permute-start(bf16[4,512,128]{2,1,0:T(8,128)(2,1)S(1)} %copy-done.9), channel_id=1, source_target_pairs={{0,496},{16,0},{32,16},{48,32},{64,48},{80,64},{96,80},{112,96},{1... | collective-permute-start | bytes 1572872 | tf_op jit(solution)/shard_map/ppermute | solution.py:33
  95.3 23.1 %collective-permute-start.3 = (bf16[4,512,128]{2,1,0:T(8,128)(2,1)S(1)}, bf16[4,512,128]{2,1,0:T(8,128)(2,1)S(1)}, u32[]{:S(2)}, u32[]{:S(2)}) collective-permute-start(bf16[4,512,128]{2,1,0:T(8,128)(2,1)S(1)} %copy-done.8), channel_id=1, source_target_pairs={{0,16},{16,32},{32,48},{48,64},{64,80},{80,96},{96,112},{112,128},... | collective-permute-start | bytes 1572872 | tf_op jit(solution)/shard_map/ppermute | solution.py:33
  119.6 18.7 %all-to-all-start.3 = ((bf16[16,128,128]{1,2,0:T(8,128)(2,1)}), bf16[16,128,128]{1,2,0:T(8,128)(2,1)S(1)}, u32[]{:S(2)}, u32[]{:S(2)}) async-start(bf16[16,128,128]{1,2,0:T(8,128)(2,1)} %copy.24), calls=%async_computation.3 | async-start | bytes 1048576 | tf_op jit(solution)/shard_map/all_to_all | solution.py:25

commit v5 on v4

--- a/solution.py
+++ b/solution.py
@@ -70,9 +70,10 @@
     highest = jnp.max(scores[0], axis=1, keepdims=True)
     for part in scores[1:]:
         highest = jnp.maximum(highest, jnp.max(part, axis=1, keepdims=True))
-    total = sum(jnp.sum(jnp.exp(part - highest), axis=1, keepdims=True) for part in scores)
-    log_total = highest + jnp.log(total)
-    weights = [jnp.exp(part - log_total) for part in scores]
+    shifted = [jnp.exp(part - highest) for part in scores]
+    total = sum(jnp.sum(part, axis=1, keepdims=True) for part in shifted)
+    inverse = 1.0 / total
+    weights = [part * inverse for part in shifted]
     weights_bf = [w.astype(jnp.bfloat16) for w in weights]
     attended = sum(nn(w, pair) for w, pair in zip(weights_bf, pairs)).astype(jnp.bfloat16)
     products = jnp.where(low, 0.0, packed.astype(f32) * attended.astype(f32))

time: 141 us -> 141 us (level)
  no operation moved by 1% of the time
where the time goes in v5:
time: 141 us; the launch traced here: 140 us
  waiting for transfers between devices  61.3 us (43%)
  starting transfers between devices  46 us (33%)
  Pallas kernels  17.7 us (13%)
  local copies, waits for them, and re-layouts  11.9 us (8%)
  other arithmetic  2.44 us (2%)
    ppermute x4, waiting for transfers between devices, from_behind(): return lax.ppermute(value, axis, pairs)  36.9 us
    pallas_call x1, Pallas kernels, attention(): pl.pallas_call(attention_kernel, grid_spec=pltpu.PrefetchScalarGridSpec(n...  17.7 us
    ppermute x4, starting transfers between devices, from_behind(): return lax.ppermute(value, axis, pairs)  17.2 us
    all_to_all x2, starting transfers between devices, to_heads(): lax.all_to_all(packed, 'head', split_axis=1, concat_axis=0, tiled=True)  15.1 us
    all_to_all x2, waiting for transfers between devices, to_heads(): lax.all_to_all(packed, 'head', split_axis=1, concat_axis=0, tiled=True)  14.6 us
    all_to_all x2, starting transfers between devices, to_rows(): lax.all_to_all(packed, 'head', split_axis=0, concat_axis=1, tiled=True)  13.7 us
    all_to_all x2, waiting for transfers between devices, to_rows(): lax.all_to_all(packed, 'head', split_axis=0, concat_axis=1, tiled=True)  9.75 us
    unnamed x28, local copies, waits for them, and re-layouts  7.31 us
  transfers between devices with their start and end apart: 8, of which 7 were waited for; matrix products, arithmetic and copies ran while one was open for 4% of the time, Pallas kernels for 0%

profile of v5, /device:TPU:8, one launch (start us, length us, event | category | flops | bytes accessed | tf_op | source)
XLA Modules:
  0.0 140.1 jit_solution(10821871322633654516)
XLA Ops:
  0.6 0.0 copy-start.4
  0.6 1.2 copy.20
  1.8 0.0 copy-done.4
  1.8 0.2 copy.21
  2.0 0.8 pad_maximum_fusion.1
  2.8 0.0 copy-start.5
  2.8 9.5 %all-to-all-start.1 = ((bf16[128,16,128]{0,2,1:T(8,128)(2,1)}), bf16[128,16,128]{0,2,1:T(8,128)(2,1)S(1)}, u32[]{:S(2)}, u32[]{:S(2)}) async-start(bf16[128,16,128]{0,2,1:T(8,128)(2,1)} %pad_maximum_fusion.1), calls=%async_computation.1 | async-start | bytes 1048576 | tf_op jit(solution)/shard_map/all_to_all | solution.py:18
  12.3 0.0 copy-done.5
  12.3 0.0 copy-start.6
  12.4 0.2 copy.17
  12.5 0.8 copy-done.6
  13.3 0.2 copy.18
  13.5 0.8 pad_maximum_fusion
  14.3 13.1 %all-to-all-done.1 = bf16[128,16,128]{0,2,1:T(8,128)(2,1)S(1)} async-done(((bf16[128,16,128]{0,2,1:T(8,128)(2,1)}), bf16[128,16,128]{0,2,1:T(8,128)(2,1)S(1)}, u32[]{:S(2)}, u32[]{:S(2)}) %all-to-all-start.1) | async-done | bytes 524320 | tf_op jit(solution)/shard_map/all_to_all | solution.py:18
  27.4 5.6 %all-to-all-start = ((bf16[128,16,128]{0,2,1:T(8,128)(2,1)}), bf16[128,16,128]{0,2,1:T(8,128)(2,1)S(1)}, u32[]{:S(2)}, u32[]{:S(2)}) async-start(bf16[128,16,128]{0,2,1:T(8,128)(2,1)} %pad_maximum_fusion), calls=%async_computation | async-start | bytes 1048576 | tf_op jit(solution)/shard_map/all_to_all | solution.py:18
  33.0 0.3 copy.22
  33.2 0.0 copy-start
  33.3 10.9 %collective-permute-start.1 = (bf16[4,512,128]{2,1,0:T(8,128)(2,1)S(1)}, bf16[4,512,128]{2,1,0:T(8,128)(2,1)S(1)}, u32[]{:S(2)}, u32[]{:S(2)}) collective-permute-start(bf16[4,512,128]{2,1,0:T(8,128)(2,1)S(1)} %bitcast.33), channel_id=1, source_target_pairs={{0,496},{16,0},{32,16},{48,32},{64,48},{80,64},{96,80},{112,96},{1... | collective-permute-start | bytes 1572872 | tf_op jit(solution)/shard_map/ppermute | solution.py:33
  44.2 1.9 %collective-permute-start = (bf16[4,512,128]{2,1,0:T(8,128)(2,1)S(1)}, bf16[4,512,128]{2,1,0:T(8,128)(2,1)S(1)}, u32[]{:S(2)}, u32[]{:S(2)}) collective-permute-start(bf16[4,512,128]{2,1,0:T(8,128)(2,1)S(1)} %bitcast.34), channel_id=1, source_target_pairs={{0,16},{16,32},{32,48},{48,64},{64,80},{80,96},{96,112},{112,128},... | collective-permute-start | bytes 1572872 | tf_op jit(solution)/shard_map/ppermute | solution.py:33
  46.1 0.0 copy-start.7
  46.1 0.7 copy-done.7
  46.8 0.1 dynamic-slice_bitcast_fusion
  46.9 0.6 add_clamp_fusion.picks_ref
  47.5 1.5 %all-to-all-done = bf16[128,16,128]{0,2,1:T(8,128)(2,1)S(1)} async-done(((bf16[128,16,128]{0,2,1:T(8,128)(2,1)}), bf16[128,16,128]{0,2,1:T(8,128)(2,1)S(1)}, u32[]{:S(2)}, u32[]{:S(2)}) %all-to-all-start) | async-done | bytes 524320 | tf_op jit(solution)/shard_map/all_to_all | solution.py:18
  49.0 1.0 copy.19
  50.0 0.0 copy-done
  50.0 7.4 %collective-permute-done.1.right_ref = bf16[4,512,128]{2,1,0:T(8,128)(2,1)S(1)} collective-permute-done((bf16[4,512,128]{2,1,0:T(8,128)(2,1)S(1)}, bf16[4,512,128]{2,1,0:T(8,128)(2,1)S(1)}, u32[]{:S(2)}, u32[]{:S(2)}) %collective-permute-start.1) | collective-permute-done | bytes 524320 | tf_op jit(solution)/shard_map/ppermute | solution.py:33
  57.4 0.0 copy-start.2
  57.4 8.8 %collective-permute-done.left_ref = bf16[4,512,128]{2,1,0:T(8,128)(2,1)S(1)} collective-permute-done((bf16[4,512,128]{2,1,0:T(8,128)(2,1)S(1)}, bf16[4,512,128]{2,1,0:T(8,128)(2,1)S(1)}, u32[]{:S(2)}, u32[]{:S(2)}) %collective-permute-start) | collective-permute-done | bytes 524320 | tf_op jit(solution)/shard_map/ppermute | solution.py:33
  66.2 0.0 copy-start.3
  66.2 0.0 copy-done.2
  66.2 0.8 copy-done.3
  67.0 17.7 %shard_map.84 = (bf16[4,512,128]{2,1,0:T(8,128)(2,1)}, f32[4,512,128]{2,1,0:T(8,128)}, bf16[4,512,128]{2,1,0:T(8,128)(2,1)}, bf16[4,512,128]{2,1,0:T(8,128)(2,1)}) custom-call(s32[2,4]{1,0:T(2,128)} %add_clamp_fusion.picks_ref, bf16[4,512,128]{2,1,0:T(8,128)(2,1)} %bitcast.36, bf16[4,512,128]{2,1,0:T(8,128)(2,1)} %bitcast.35, ...), custom_call_target="tpu_custom_call" | custom-call | tf_op jit(solution)/shard_map/pallas_call | solution.py:108
  84.7 0.0 copy-start.1
  84.7 2.2 %copy.23 = bf16[16,128,128]{1,2,0:T(8,128)(2,1)} copy(bf16[16,128,128]{2,1,0:T(8,128)(2,1)} %bitcast.45) | data formatting | bytes 1048576 | tf_op jit(solution)/shard_map/all_to_all | solution.py:25
  86.8 0.0 copy-start.9
  86.8 0.0 copy-start.8
  86.8 6.5 %all-to-all-start.2 = ((bf16[16,128,128]{1,2,0:T(8,128)(2,1)}), bf16[16,128,128]{1,2,0:T(8,128)(2,1)S(1)}, u32[]{:S(2)}, u32[]{:S(2)}) async-start(bf16[16,128,128]{1,2,0:T(8,128)(2,1)} %copy.23), calls=%async_computation.2 | async-start | bytes 1048576 | tf_op jit(solution)/shard_map/all_to_all | solution.py:25
  93.4 0.0 copy-done.9
  93.4 1.9 %collective-permute-start.2 = (bf16[4,512,128]{2,1,0:T(8,128)(2,1)S(1)}, bf16[4,512,128]{2,1,0:T(8,128)(2,1)S(1)}, u32[]{:S(2)}, u32[]{:S(2)}) collective-permute-start(bf16[4,512,128]{2,1,0:T(8,128)(2,1)S(1)} %copy-done.9), channel_id=1, source_target_pairs={{0,496},{16,0},{32,16},{48,32},{64,48},{80,64},{96,80},{112,96},{1... | collective-permute-start | bytes 1572872 | tf_op jit(solution)/shard_map/ppermute | solution.py:33
  95.3 0.0 copy-done.8
  95.3 2.4 %collective-permute-start.3 = (bf16[4,512,128]{2,1,0:T(8,128)(2,1)S(1)}, bf16[4,512,128]{2,1,0:T(8,128)(2,1)S(1)}, u32[]{:S(2)}, u32[]{:S(2)}) collective-permute-start(bf16[4,512,128]{2,1,0:T(8,128)(2,1)S(1)} %copy-done.8), channel_id=1, source_target_pairs={{0,16},{16,32},{32,48},{48,64},{64,80},{80,96},{96,112},{112,128},... | collective-permute-start | bytes 1572872 | tf_op jit(solution)/shard_map/ppermute | solution.py:33
  97.7 10.7 %collective-permute-done.2 = bf16[4,512,128]{2,1,0:T(8,128)(2,1)S(1)} collective-permute-done((bf16[4,512,128]{2,1,0:T(8,128)(2,1)S(1)}, bf16[4,512,128]{2,1,0:T(8,128)(2,1)S(1)}, u32[]{:S(2)}, u32[]{:S(2)}) %collective-permute-start.2) | collective-permute-done | bytes 524320 | tf_op jit(solution)/shard_map/ppermute | solution.py:33
  108.4 10.0 %collective-permute-done.3 = bf16[4,512,128]{2,1,0:T(8,128)(2,1)S(1)} collective-permute-done((bf16[4,512,128]{2,1,0:T(8,128)(2,1)S(1)}, bf16[4,512,128]{2,1,0:T(8,128)(2,1)S(1)}, u32[]{:S(2)}, u32[]{:S(2)}) %collective-permute-start.3) | collective-permute-done | bytes 524320 | tf_op jit(solution)/shard_map/ppermute | solution.py:33
  118.4 0.0 copy-done.1
  118.4 0.2 add_convert_fusion
  118.6 1.0 copy.24
  119.6 0.0 all-to-all-done.2
  119.6 7.2 %all-to-all-start.3 = ((bf16[16,128,128]{1,2,0:T(8,128)(2,1)}), bf16[16,128,128]{1,2,0:T(8,128)(2,1)S(1)}, u32[]{:S(2)}, u32[]{:S(2)}) async-start(bf16[16,128,128]{1,2,0:T(8,128)(2,1)} %copy.24), calls=%async_computation.3 | async-start | bytes 1048576 | tf_op jit(solution)/shard_map/all_to_all | solution.py:25
  126.9 0.9 copy.26
  127.7 0.8 copy.25
  128.6 9.7 %all-to-all-done.3 = bf16[16,128,128]{1,2,0:T(8,128)(2,1)S(1)} async-done(((bf16[16,128,128]{1,2,0:T(8,128)(2,1)}), bf16[16,128,128]{1,2,0:T(8,128)(2,1)S(1)}, u32[]{:S(2)}, u32[]{:S(2)}) %all-to-all-start.3) | async-done | bytes 524320 | tf_op jit(solution)/shard_map/all_to_all | solution.py:25
  138.4 0.9 copy.28
  139.2 0.8 copy.27
  (3 shorter events, 0.1 us)
Async XLA Ops:
  0.6 1.2 copy-start.4
  2.8 9.5 %copy-start.5 = (bf16[128,1024]{1,0:T(8,128)(2,1)S(1)}, bf16[128,1024]{1,0:T(8,128)(2,1)}, u32[]{:S(2)}) copy-start(bf16[128,1024]{1,0:T(8,128)(2,1)} %param.5) | copy-start | bytes 786436
  2.8 24.6 %all-to-all-start.1 = ((bf16[128,16,128]{0,2,1:T(8,128)(2,1)}), bf16[128,16,128]{0,2,1:T(8,128)(2,1)S(1)}, u32[]{:S(2)}, u32[]{:S(2)}) async-start(bf16[128,16,128]{0,2,1:T(8,128)(2,1)} %pad_maximum_fusion.1), calls=%async_computation.1 | async-start | bytes 1048576 | tf_op jit(solution)/shard_map/all_to_all | solution.py:18
  12.3 1.0 copy-start.6
  27.4 21.6 %all-to-all-start = ((bf16[128,16,128]{0,2,1:T(8,128)(2,1)}), bf16[128,16,128]{0,2,1:T(8,128)(2,1)S(1)}, u32[]{:S(2)}, u32[]{:S(2)}) async-start(bf16[128,16,128]{0,2,1:T(8,128)(2,1)} %pad_maximum_fusion), calls=%async_computation | async-start | bytes 1048576 | tf_op jit(solution)/shard_map/all_to_all | solution.py:18
  33.2 16.7 %copy-start = (bf16[16,128,1,128]{3,1,0,2:T(8,128)(2,1)}, bf16[16,128,1,128]{3,1,0,2:T(8,128)(2,1)S(1)}, u32[]{:S(2)}) copy-start(bf16[16,128,1,128]{3,1,0,2:T(8,128)(2,1)S(1)} %copy.22) | copy-start | bytes 1572868
  33.3 24.1 %collective-permute-start.1 = (bf16[4,512,128]{2,1,0:T(8,128)(2,1)S(1)}, bf16[4,512,128]{2,1,0:T(8,128)(2,1)S(1)}, u32[]{:S(2)}, u32[]{:S(2)}) collective-permute-start(bf16[4,512,128]{2,1,0:T(8,128)(2,1)S(1)} %bitcast.33), channel_id=1, source_target_pairs={{0,496},{16,0},{32,16},{48,32},{64,48},{80,64},{96,80},{112,96},{1... | collective-permute-start | bytes 1572872 | tf_op jit(solution)/shard_map/ppermute | solution.py:33
  44.2 22.0 %collective-permute-start = (bf16[4,512,128]{2,1,0:T(8,128)(2,1)S(1)}, bf16[4,512,128]{2,1,0:T(8,128)(2,1)S(1)}, u32[]{:S(2)}, u32[]{:S(2)}) collective-permute-start(bf16[4,512,128]{2,1,0:T(8,128)(2,1)S(1)} %bitcast.34), channel_id=1, source_target_pairs={{0,16},{16,32},{32,48},{48,64},{64,80},{80,96},{96,112},{112,128},... | collective-permute-start | bytes 1572872 | tf_op jit(solution)/shard_map/ppermute | solution.py:33
  46.1 0.7 copy-start.7
  57.4 8.8 %copy-start.2 = (bf16[4,512,128]{2,1,0:T(8,128)(2,1)}, bf16[4,512,128]{2,1,0:T(8,128)(2,1)S(1)}, u32[]{:S(2)}) copy-start(bf16[4,512,128]{2,1,0:T(8,128)(2,1)S(1)} %collective-permute-done.1.right_ref) | copy-start | bytes 1572868
  66.2 0.8 copy-start.3
  84.7 33.7 %copy-start.1 = (f32[4,512,128]{2,1,0:T(8,128)S(1)}, f32[4,512,128]{2,1,0:T(8,128)}, u32[]{:S(2)}) copy-start(f32[4,512,128]{2,1,0:T(8,128)} %get-tuple-element.9) | copy-start | bytes 3145732
  86.8 6.5 %copy-start.9 = (bf16[4,512,128]{2,1,0:T(8,128)(2,1)S(1)}, bf16[4,512,128]{2,1,0:T(8,128)(2,1)}, u32[]{:S(2)}) copy-start(bf16[4,512,128]{2,1,0:T(8,128)(2,1)} %get-tuple-element.10) | copy-start | bytes 1572868
  86.8 8.5 %copy-start.8 = (bf16[4,512,128]{2,1,0:T(8,128)(2,1)S(1)}, bf16[4,512,128]{2,1,0:T(8,128)(2,1)}, u32[]{:S(2)}) copy-start(bf16[4,512,128]{2,1,0:T(8,128)(2,1)} %get-tuple-element.11) | copy-start | bytes 1572868
  86.8 32.8 %all-to-all-start.2 = ((bf16[16,128,128]{1,2,0:T(8,128)(2,1)}), bf16[16,128,128]{1,2,0:T(8,128)(2,1)S(1)}, u32[]{:S(2)}, u32[]{:S(2)}) async-start(bf16[16,128,128]{1,2,0:T(8,128)(2,1)} %copy.23), calls=%async_computation.2 | async-start | bytes 1048576 | tf_op jit(solution)/shard_map/all_to_all | solution.py:25
  93.4 15.0 %collective-permute-start.2 = (bf16[4,512,128]{2,1,0:T(8,128)(2,1)S(1)}, bf16[4,512,128]{2,1,0:T(8,128)(2,1)S(1)}, u32[]{:S(2)}, u32[]{:S(2)}) collective-permute-start(bf16[4,512,128]{2,1,0:T(8,128)(2,1)S(1)} %copy-done.9), channel_id=1, source_target_pairs={{0,496},{16,0},{32,16},{48,32},{64,48},{80,64},{96,80},{112,96},{1... | collective-permute-start | bytes 1572872 | tf_op jit(solution)/shard_map/ppermute | solution.py:33
  95.3 23.1 %collective-permute-start.3 = (bf16[4,512,128]{2,1,0:T(8,128)(2,1)S(1)}, bf16[4,512,128]{2,1,0:T(8,128)(2,1)S(1)}, u32[]{:S(2)}, u32[]{:S(2)}) collective-permute-start(bf16[4,512,128]{2,1,0:T(8,128)(2,1)S(1)} %copy-done.8), channel_id=1, source_target_pairs={{0,16},{16,32},{32,48},{48,64},{64,80},{80,96},{96,112},{112,128},... | collective-permute-start | bytes 1572872 | tf_op jit(solution)/shard_map/ppermute | solution.py:33
  119.6 18.7 %all-to-all-start.3 = ((bf16[16,128,128]{1,2,0:T(8,128)(2,1)}), bf16[16,128,128]{1,2,0:T(8,128)(2,1)S(1)}, u32[]{:S(2)}, u32[]{:S(2)}) async-start(bf16[16,128,128]{1,2,0:T(8,128)(2,1)} %copy.24), calls=%async_computation.3 | async-start | bytes 1048576 | tf_op jit(solution)/shard_map/all_to_all | solution.py:25

commit v6 on v5

--- a/solution.py
+++ b/solution.py
@@ -35,7 +35,7 @@
 
 def attention_kernel(
     picks_ref, qd_ref, kv_ref, left_ref, right_ref,
-    out_ref, own_grad_ref, to_left_ref, to_right_ref, left_acc, right_acc,
+    out_ref, highest_ref, inverse_ref, delta_ref, to_left_ref, to_right_ref, left_acc, right_acc,
 ):
     number = pl.program_id(0)
     scale = HEAD_DIM ** (-0.5)
@@ -83,10 +83,13 @@
     ]
     query_grad = (sum(nn(d, pair) for d, pair in zip(score_grads, pairs)) * scale).astype(jnp.bfloat16)
     out_ref[0] = jnp.where(low, query_grad, attended)
-    key_parts = [tn(d, packed) * scale for d in score_grads]
-    value_parts = [tn(w, packed) for w in weights_bf]
-    kv_parts = [jnp.where(low, k, v) for k, v in zip(key_parts, value_parts)]
-    own_grad_ref[0] = kv_parts[0]
+    highest_ref[0] = highest
+    inverse_ref[0] = inverse
+    delta_ref[0] = row_delta
+    kv_parts = [None] + [
+        jnp.where(low, tn(d, packed) * scale, tn(w, packed))
+        for d, w in zip(score_grads[1:], weights_bf[1:])
+    ]
     left_pick = picks_ref[0, number]
     right_pick = picks_ref[1, number]
     left_acc[left_pick] += kv_parts[1]
@@ -96,6 +99,45 @@
     def _():
         to_left_ref[...] = left_acc[...].astype(jnp.bfloat16)
         to_right_ref[...] = right_acc[...].astype(jnp.bfloat16)
+
+
+def own_kernel(qd_ref, kv_ref, highest_ref, inverse_ref, delta_ref, own_grad_ref):
+    scale = HEAD_DIM ** (-0.5)
+    f32 = jnp.float32
+    packed = qd_ref[0]
+    pair = kv_ref[0]
+    lane = lax.broadcasted_iota(jnp.int32, packed.shape, 1)
+    low = lane < HEAD_DIM
+    zero = jnp.zeros_like(packed)
+    query_ext = jnp.where(low, packed, zero)
+    grad_ext = jnp.where(low, zero, packed)
+    score = lax.dot_general(query_ext, pair, (((1,), (1,)), ((), ())), preferred_element_type=f32) * scale
+    row = lax.broadcasted_iota(jnp.int32, score.shape, 0)
+    col = lax.broadcasted_iota(jnp.int32, score.shape, 1)
+    score = jnp.where(col <= row, score, -jnp.inf)
+    weight = jnp.exp(score - highest_ref[0]) * inverse_ref[0]
+    weight_grad = lax.dot_general(grad_ext, pair, (((1,), (1,)), ((), ())), preferred_element_type=f32)
+    score_grad = (weight * (weight_grad - delta_ref[0])).astype(jnp.bfloat16)
+    key_part = lax.dot_general(score_grad, packed, (((0,), (0,)), ((), ())), preferred_element_type=f32)
+    value_part = lax.dot_general(
+        weight.astype(jnp.bfloat16), packed, (((0,), (0,)), ((), ())), preferred_element_type=f32
+    )
+    own_grad_ref[0] = jnp.where(low, key_part * scale, value_part)
+
+
+def own_grads_of(qd, kv, highest, inverse, delta):
+    block_count, block, width = kv.shape
+    one_spec = pl.BlockSpec((1, block, width), lambda n: (n, 0, 0))
+    stat_spec = pl.BlockSpec((1, block, 1), lambda n: (n, 0, 0))
+    return pl.pallas_call(
+        own_kernel,
+        grid=(block_count,),
+        in_specs=[one_spec, one_spec, stat_spec, stat_spec, stat_spec],
+        out_specs=one_spec,
+        out_shape=jax.ShapeDtypeStruct((block_count, block, width), jnp.float32),
+        compiler_params=pltpu.CompilerParams(dimension_semantics=("arbitrary",)),
+        interpret=INTERPRET,
+    )(qd, kv, highest, inverse, delta)
 
 
 def attention(picks, qd, kv, left, right):
@@ -104,19 +146,23 @@
     right_spec = pl.BlockSpec((1, block, width), lambda n, p: (p[1, n], 0, 0))
     one_spec = pl.BlockSpec((1, block, width), lambda n, p: (n, 0, 0))
     whole_spec = pl.BlockSpec((block_count, block, width), lambda n, p: (0, 0, 0))
+    stat_spec = pl.BlockSpec((1, block, 1), lambda n, p: (n, 0, 0))
     shape = (block_count, block, width)
+    stat = jax.ShapeDtypeStruct((block_count, block, 1), jnp.float32)
     return pl.pallas_call(
         attention_kernel,
         grid_spec=pltpu.PrefetchScalarGridSpec(
             num_scalar_prefetch=1,
             grid=(block_count,),
             in_specs=[one_spec, one_spec, left_spec, right_spec],
-            out_specs=[one_spec, one_spec, whole_spec, whole_spec],
+            out_specs=[one_spec, stat_spec, stat_spec, stat_spec, whole_spec, whole_spec],
             scratch_shapes=[pltpu.VMEM(shape, jnp.float32), pltpu.VMEM(shape, jnp.float32)],
         ),
         out_shape=[
             jax.ShapeDtypeStruct(shape, jnp.bfloat16),
-            jax.ShapeDtypeStruct(shape, jnp.float32),
+            stat,
+            stat,
+            stat,
             jax.ShapeDtypeStruct(shape, jnp.bfloat16),
             jax.ShapeDtypeStruct(shape, jnp.bfloat16),
         ],
@@ -138,9 +184,10 @@
         [lax.dynamic_slice_in_dim(neighbour_blocks[:, c], first_row, block_count, 0) for c in range(2)]
     )
     picks = jnp.clip(picks, 0, block_count - 1).astype(jnp.int32)
-    out_pair, own_grads, to_left, to_right = attention(picks, qd, kv, left, right)
+    out_pair, highest, inverse, delta, to_left, to_right = attention(picks, qd, kv, left, right)
     from_right = from_behind(to_left, "blk", -1).astype(jnp.float32)
     from_left = from_behind(to_right, "blk", 1).astype(jnp.float32)
+    own_grads = own_grads_of(qd, kv, highest, inverse, delta)
     query_grad, attended = to_rows(out_pair.reshape(row_count, width))
     kv_grads = (own_grads + from_right + from_left).astype(jnp.bfloat16)
     key_grad, value_grad = to_rows(kv_grads.reshape(row_count, width))

time: 141 us -> 139 us (0.986)
  waiting for transfers between devices: 61.3 us -> 53.3 us
  Pallas kernels: 17.7 us -> 22.7 us
    ppermute x4, waiting for transfers between devices: 36.9 us -> 29 us  [from_behind(): return lax.ppermute(value, axis, pairs)]
    pallas_call x0 -> x1, Pallas kernels: none -> 5.88 us  [own_grads_of(): pl.pallas_call(own_kernel, grid=(block_count,), in_specs=[one_spec, one_s...]
    unnamed x28 -> x26, local copies, waits for them, and re-layouts: 7.31 us -> 7.32 us
  transfers between devices with their start and end apart: 8 -> 8, of which waited for: 7 -> 7; matrix products, arithmetic and copies ran while one was open for 4% -> 5% of each run, Pallas kernels for 0% -> 4%
where the time goes in v6:
time: 139 us; the launch traced here: 138 us
  waiting for transfers between devices  53.3 us (38%)
  starting transfers between devices  46.1 us (33%)
  Pallas kernels  22.7 us (16%)
  local copies, waits for them, and re-layouts  11.8 us (8%)
  other arithmetic  3.66 us (3%)
    ppermute x4, waiting for transfers between devices, from_behind(): return lax.ppermute(value, axis, pairs)  29 us
    ppermute x4, starting transfers between devices, from_behind(): return lax.ppermute(value, axis, pairs)  17.2 us
    pallas_call x1, Pallas kernels, attention(): pl.pallas_call(attention_kernel, grid_spec=pltpu.PrefetchScalarGridSpec(n...  16.8 us
    all_to_all x2, starting transfers between devices, to_heads(): lax.all_to_all(packed, 'head', split_axis=1, concat_axis=0, tiled=True)  15.1 us
    all_to_all x2, waiting for transfers between devices, to_heads(): lax.all_to_all(packed, 'head', split_axis=1, concat_axis=0, tiled=True)  14.6 us
    all_to_all x2, starting transfers between devices, to_rows(): lax.all_to_all(packed, 'head', split_axis=0, concat_axis=1, tiled=True)  13.8 us
    all_to_all x2, waiting for transfers between devices, to_rows(): lax.all_to_all(packed, 'head', split_axis=0, concat_axis=1, tiled=True)  9.75 us
    unnamed x26, local copies, waits for them, and re-layouts  7.32 us
  transfers between devices with their start and end apart: 8, of which 7 were waited for; matrix products, arithmetic and copies ran while one was open for 5% of the time, Pallas kernels for 4%

profile of v6, /device:TPU:8, one launch (start us, length us, event | category | flops | bytes accessed | tf_op | source)
XLA Modules:
  0.0 138.3 jit_solution(7535519194794480324)
XLA Ops:
  0.6 0.0 copy-start.3
  0.6 1.2 copy.20
  1.8 0.0 copy-done.3
  1.8 0.2 copy.21
  2.0 0.8 pad_maximum_fusion.1
  2.8 0.0 copy-start.4
  2.8 9.5 %all-to-all-start.1 = ((bf16[128,16,128]{0,2,1:T(8,128)(2,1)}), bf16[128,16,128]{0,2,1:T(8,128)(2,1)S(1)}, u32[]{:S(2)}, u32[]{:S(2)}) async-start(bf16[128,16,128]{0,2,1:T(8,128)(2,1)} %pad_maximum_fusion.1), calls=%async_computation.1 | async-start | bytes 1048576 | tf_op jit(solution)/shard_map/all_to_all | solution.py:18
  12.3 0.0 copy-done.4
  12.3 0.0 copy-start.5
  12.4 0.2 copy.17
  12.5 0.8 copy-done.5
  13.3 0.2 copy.18
  13.5 0.8 pad_maximum_fusion
  14.3 13.1 %all-to-all-done.1 = bf16[128,16,128]{0,2,1:T(8,128)(2,1)S(1)} async-done(((bf16[128,16,128]{0,2,1:T(8,128)(2,1)}), bf16[128,16,128]{0,2,1:T(8,128)(2,1)S(1)}, u32[]{:S(2)}, u32[]{:S(2)}) %all-to-all-start.1) | async-done | bytes 524320 | tf_op jit(solution)/shard_map/all_to_all | solution.py:18
  27.4 5.6 %all-to-all-start = ((bf16[128,16,128]{0,2,1:T(8,128)(2,1)}), bf16[128,16,128]{0,2,1:T(8,128)(2,1)S(1)}, u32[]{:S(2)}, u32[]{:S(2)}) async-start(bf16[128,16,128]{0,2,1:T(8,128)(2,1)} %pad_maximum_fusion), calls=%async_computation | async-start | bytes 1048576 | tf_op jit(solution)/shard_map/all_to_all | solution.py:18
  33.0 0.3 copy.22
  33.2 0.0 copy-start
  33.3 10.9 %collective-permute-start.1 = (bf16[4,512,128]{2,1,0:T(8,128)(2,1)S(1)}, bf16[4,512,128]{2,1,0:T(8,128)(2,1)S(1)}, u32[]{:S(2)}, u32[]{:S(2)}) collective-permute-start(bf16[4,512,128]{2,1,0:T(8,128)(2,1)S(1)} %bitcast.28), channel_id=1, source_target_pairs={{0,496},{16,0},{32,16},{48,32},{64,48},{80,64},{96,80},{112,96},{1... | collective-permute-start | bytes 1572872 | tf_op jit(solution)/shard_map/ppermute | solution.py:33
  44.2 1.9 %collective-permute-start = (bf16[4,512,128]{2,1,0:T(8,128)(2,1)S(1)}, bf16[4,512,128]{2,1,0:T(8,128)(2,1)S(1)}, u32[]{:S(2)}, u32[]{:S(2)}) collective-permute-start(bf16[4,512,128]{2,1,0:T(8,128)(2,1)S(1)} %bitcast.29), channel_id=1, source_target_pairs={{0,16},{16,32},{32,48},{48,64},{64,80},{80,96},{96,112},{112,128},... | collective-permute-start | bytes 1572872 | tf_op jit(solution)/shard_map/ppermute | solution.py:33
  46.1 0.0 copy-start.6
  46.1 0.7 copy-done.6
  46.8 0.1 dynamic-slice_bitcast_fusion
  46.9 0.6 add_clamp_fusion.picks_ref
  47.5 1.5 %all-to-all-done = bf16[128,16,128]{0,2,1:T(8,128)(2,1)S(1)} async-done(((bf16[128,16,128]{0,2,1:T(8,128)(2,1)}), bf16[128,16,128]{0,2,1:T(8,128)(2,1)S(1)}, u32[]{:S(2)}, u32[]{:S(2)}) %all-to-all-start) | async-done | bytes 524320 | tf_op jit(solution)/shard_map/all_to_all | solution.py:18
  49.0 1.0 copy.19
  50.0 0.0 copy-done
  50.0 7.4 %collective-permute-done.1.right_ref = bf16[4,512,128]{2,1,0:T(8,128)(2,1)S(1)} collective-permute-done((bf16[4,512,128]{2,1,0:T(8,128)(2,1)S(1)}, bf16[4,512,128]{2,1,0:T(8,128)(2,1)S(1)}, u32[]{:S(2)}, u32[]{:S(2)}) %collective-permute-start.1) | collective-permute-done | bytes 524320 | tf_op jit(solution)/shard_map/ppermute | solution.py:33
  57.4 0.0 copy-start.1
  57.4 8.8 %collective-permute-done.left_ref = bf16[4,512,128]{2,1,0:T(8,128)(2,1)S(1)} collective-permute-done((bf16[4,512,128]{2,1,0:T(8,128)(2,1)S(1)}, bf16[4,512,128]{2,1,0:T(8,128)(2,1)S(1)}, u32[]{:S(2)}, u32[]{:S(2)}) %collective-permute-start) | collective-permute-done | bytes 524320 | tf_op jit(solution)/shard_map/ppermute | solution.py:33
  66.2 0.0 copy-start.2
  66.2 0.0 copy-done.1
  66.2 0.8 copy-done.2
  67.0 16.8 %shard_map.84 = (bf16[4,512,128]{2,1,0:T(8,128)(2,1)}, f32[4,512,1]{2,1,0:T(8,128)}, f32[4,512,1]{2,1,0:T(8,128)}, f32[4,512,1]{2,1,0:T(8,128)}, bf16[4,512,128]...) custom-call(s32[2,4]{1,0:T(2,128)} %add_clamp_fusion.picks_ref, bf16[4,512,128]{2,1,0:T(8,128)(2,1)} %bitcast.32, ...), custom_call_target="tpu_custom_call" | custom-call | tf_op jit(solution)/shard_map/pallas_call | solution.py:152
  83.8 2.0 %copy.23 = bf16[16,128,128]{1,2,0:T(8,128)(2,1)} copy(bf16[16,128,128]{2,1,0:T(8,128)(2,1)} %bitcast.47) | data formatting | bytes 1048576 | tf_op jit(solution)/shard_map/all_to_all | solution.py:25
  85.9 0.0 copy-start.8
  85.9 0.0 copy-start.7
  85.9 6.5 %all-to-all-start.2 = ((bf16[16,128,128]{1,2,0:T(8,128)(2,1)}), bf16[16,128,128]{1,2,0:T(8,128)(2,1)S(1)}, u32[]{:S(2)}, u32[]{:S(2)}) async-start(bf16[16,128,128]{1,2,0:T(8,128)(2,1)} %copy.23), calls=%async_computation.2 | async-start | bytes 1048576 | tf_op jit(solution)/shard_map/all_to_all | solution.py:25
  92.4 0.0 copy-done.8
  92.4 1.9 %collective-permute-start.2 = (bf16[4,512,128]{2,1,0:T(8,128)(2,1)S(1)}, bf16[4,512,128]{2,1,0:T(8,128)(2,1)S(1)}, u32[]{:S(2)}, u32[]{:S(2)}) collective-permute-start(bf16[4,512,128]{2,1,0:T(8,128)(2,1)S(1)} %copy-done.8), channel_id=1, source_target_pairs={{0,496},{16,0},{32,16},{48,32},{64,48},{80,64},{96,80},{112,96},{1... | collective-permute-start | bytes 1572872 | tf_op jit(solution)/shard_map/ppermute | solution.py:33
  94.3 0.0 copy-done.7
  94.3 2.4 %collective-permute-start.3 = (bf16[4,512,128]{2,1,0:T(8,128)(2,1)S(1)}, bf16[4,512,128]{2,1,0:T(8,128)(2,1)S(1)}, u32[]{:S(2)}, u32[]{:S(2)}) collective-permute-start(bf16[4,512,128]{2,1,0:T(8,128)(2,1)S(1)} %copy-done.7), channel_id=1, source_target_pairs={{0,16},{16,32},{32,48},{48,64},{64,80},{80,96},{96,112},{112,128},... | collective-permute-start | bytes 1572872 | tf_op jit(solution)/shard_map/ppermute | solution.py:33
  96.7 5.9 %shard_map.85 = f32[4,512,128]{2,1,0:T(8,128)} custom-call(bf16[4,512,128]{2,1,0:T(8,128)(2,1)} %bitcast.33, bf16[4,512,128]{2,1,0:T(8,128)(2,1)} %bitcast.31, f32[4,512,1]{2,1,0:T(8,128)} %get-tuple-element.11.highest_ref, f32[4,512,1]{2,1,0:T(8,128)} %get-tuple-element.12.inverse_ref, f32[4,512,1]{2,1,0:T(8,128)} %get-tuple-element.13.delta_ref), custom_call_target="tpu_custom_call" | custom-call | tf_op jit(solution)/shard_map/pallas_call | solution.py:132
  102.6 4.8 %collective-permute-done.2 = bf16[4,512,128]{2,1,0:T(8,128)(2,1)S(1)} collective-permute-done((bf16[4,512,128]{2,1,0:T(8,128)(2,1)S(1)}, bf16[4,512,128]{2,1,0:T(8,128)(2,1)S(1)}, u32[]{:S(2)}, u32[]{:S(2)}) %collective-permute-start.2) | collective-permute-done | bytes 524320 | tf_op jit(solution)/shard_map/ppermute | solution.py:33
  107.4 8.0 %collective-permute-done.3 = bf16[4,512,128]{2,1,0:T(8,128)(2,1)S(1)} collective-permute-done((bf16[4,512,128]{2,1,0:T(8,128)(2,1)S(1)}, bf16[4,512,128]{2,1,0:T(8,128)(2,1)S(1)}, u32[]{:S(2)}, u32[]{:S(2)}) %collective-permute-start.3) | collective-permute-done | bytes 524320 | tf_op jit(solution)/shard_map/ppermute | solution.py:33
  115.4 1.4 %add_convert_fusion = bf16[4,512,128]{2,1,0:T(8,128)(2,1)S(1)} fusion(bf16[4,512,128]{2,1,0:T(8,128)(2,1)S(1)} %collective-permute-done.3, f32[4,512,128]{2,1,0:T(8,128)} %shard_map.85, bf16[4,512,128]{2,1,0:T(8,128)(2,1)S(1)} %collective-permute-done.2), kind=kLoop, calls=%fused_computation | loop fusion | flops 1310720 | bytes 2621440 | tf_op jit(solution)/shard_map/convert_element_type | solution.py:192
  116.8 1.0 copy.24
  117.8 0.0 all-to-all-done.2
  117.8 7.3 %all-to-all-start.3 = ((bf16[16,128,128]{1,2,0:T(8,128)(2,1)}), bf16[16,128,128]{1,2,0:T(8,128)(2,1)S(1)}, u32[]{:S(2)}, u32[]{:S(2)}) async-start(bf16[16,128,128]{1,2,0:T(8,128)(2,1)} %copy.24), calls=%async_computation.3 | async-start | bytes 1048576 | tf_op jit(solution)/shard_map/all_to_all | solution.py:25
  125.1 0.9 copy.26
  126.0 0.8 copy.25
  126.8 9.7 %all-to-all-done.3 = bf16[16,128,128]{1,2,0:T(8,128)(2,1)S(1)} async-done(((bf16[16,128,128]{1,2,0:T(8,128)(2,1)}), bf16[16,128,128]{1,2,0:T(8,128)(2,1)S(1)}, u32[]{:S(2)}, u32[]{:S(2)}) %all-to-all-start.3) | async-done | bytes 524320 | tf_op jit(solution)/shard_map/all_to_all | solution.py:25
  136.6 0.9 copy.28
  137.5 0.8 copy.27
  (3 shorter events, 0.1 us)
Async XLA Ops:
  0.6 1.2 copy-start.3
  2.8 9.5 %copy-start.4 = (bf16[128,1024]{1,0:T(8,128)(2,1)S(1)}, bf16[128,1024]{1,0:T(8,128)(2,1)}, u32[]{:S(2)}) copy-start(bf16[128,1024]{1,0:T(8,128)(2,1)} %param.5) | copy-start | bytes 786436
  2.8 24.6 %all-to-all-start.1 = ((bf16[128,16,128]{0,2,1:T(8,128)(2,1)}), bf16[128,16,128]{0,2,1:T(8,128)(2,1)S(1)}, u32[]{:S(2)}, u32[]{:S(2)}) async-start(bf16[128,16,128]{0,2,1:T(8,128)(2,1)} %pad_maximum_fusion.1), calls=%async_computation.1 | async-start | bytes 1048576 | tf_op jit(solution)/shard_map/all_to_all | solution.py:18
  12.3 1.0 copy-start.5
  27.4 21.6 %all-to-all-start = ((bf16[128,16,128]{0,2,1:T(8,128)(2,1)}), bf16[128,16,128]{0,2,1:T(8,128)(2,1)S(1)}, u32[]{:S(2)}, u32[]{:S(2)}) async-start(bf16[128,16,128]{0,2,1:T(8,128)(2,1)} %pad_maximum_fusion), calls=%async_computation | async-start | bytes 1048576 | tf_op jit(solution)/shard_map/all_to_all | solution.py:18
  33.2 16.7 %copy-start = (bf16[16,128,1,128]{3,1,0,2:T(8,128)(2,1)}, bf16[16,128,1,128]{3,1,0,2:T(8,128)(2,1)S(1)}, u32[]{:S(2)}) copy-start(bf16[16,128,1,128]{3,1,0,2:T(8,128)(2,1)S(1)} %copy.22) | copy-start | bytes 1572868
  33.3 24.1 %collective-permute-start.1 = (bf16[4,512,128]{2,1,0:T(8,128)(2,1)S(1)}, bf16[4,512,128]{2,1,0:T(8,128)(2,1)S(1)}, u32[]{:S(2)}, u32[]{:S(2)}) collective-permute-start(bf16[4,512,128]{2,1,0:T(8,128)(2,1)S(1)} %bitcast.28), channel_id=1, source_target_pairs={{0,496},{16,0},{32,16},{48,32},{64,48},{80,64},{96,80},{112,96},{1... | collective-permute-start | bytes 1572872 | tf_op jit(solution)/shard_map/ppermute | solution.py:33
  44.2 22.0 %collective-permute-start = (bf16[4,512,128]{2,1,0:T(8,128)(2,1)S(1)}, bf16[4,512,128]{2,1,0:T(8,128)(2,1)S(1)}, u32[]{:S(2)}, u32[]{:S(2)}) collective-permute-start(bf16[4,512,128]{2,1,0:T(8,128)(2,1)S(1)} %bitcast.29), channel_id=1, source_target_pairs={{0,16},{16,32},{32,48},{48,64},{64,80},{80,96},{96,112},{112,128},... | collective-permute-start | bytes 1572872 | tf_op jit(solution)/shard_map/ppermute | solution.py:33
  46.1 0.7 copy-start.6
  57.4 8.8 %copy-start.1 = (bf16[4,512,128]{2,1,0:T(8,128)(2,1)}, bf16[4,512,128]{2,1,0:T(8,128)(2,1)S(1)}, u32[]{:S(2)}) copy-start(bf16[4,512,128]{2,1,0:T(8,128)(2,1)S(1)} %collective-permute-done.1.right_ref) | copy-start | bytes 1572868
  66.2 0.8 copy-start.2
  85.9 6.5 %copy-start.8 = (bf16[4,512,128]{2,1,0:T(8,128)(2,1)S(1)}, bf16[4,512,128]{2,1,0:T(8,128)(2,1)}, u32[]{:S(2)}) copy-start(bf16[4,512,128]{2,1,0:T(8,128)(2,1)} %get-tuple-element.14) | copy-start | bytes 1572868
  85.9 8.5 %copy-start.7 = (bf16[4,512,128]{2,1,0:T(8,128)(2,1)S(1)}, bf16[4,512,128]{2,1,0:T(8,128)(2,1)}, u32[]{:S(2)}) copy-start(bf16[4,512,128]{2,1,0:T(8,128)(2,1)} %get-tuple-element.15) | copy-start | bytes 1572868
  85.9 31.9 %all-to-all-start.2 = ((bf16[16,128,128]{1,2,0:T(8,128)(2,1)}), bf16[16,128,128]{1,2,0:T(8,128)(2,1)S(1)}, u32[]{:S(2)}, u32[]{:S(2)}) async-start(bf16[16,128,128]{1,2,0:T(8,128)(2,1)} %copy.23), calls=%async_computation.2 | async-start | bytes 1048576 | tf_op jit(solution)/shard_map/all_to_all | solution.py:25
  92.4 15.0 %collective-permute-start.2 = (bf16[4,512,128]{2,1,0:T(8,128)(2,1)S(1)}, bf16[4,512,128]{2,1,0:T(8,128)(2,1)S(1)}, u32[]{:S(2)}, u32[]{:S(2)}) collective-permute-start(bf16[4,512,128]{2,1,0:T(8,128)(2,1)S(1)} %copy-done.8), channel_id=1, source_target_pairs={{0,496},{16,0},{32,16},{48,32},{64,48},{80,64},{96,80},{112,96},{1... | collective-permute-start | bytes 1572872 | tf_op jit(solution)/shard_map/ppermute | solution.py:33
  94.3 21.0 %collective-permute-start.3 = (bf16[4,512,128]{2,1,0:T(8,128)(2,1)S(1)}, bf16[4,512,128]{2,1,0:T(8,128)(2,1)S(1)}, u32[]{:S(2)}, u32[]{:S(2)}) collective-permute-start(bf16[4,512,128]{2,1,0:T(8,128)(2,1)S(1)} %copy-done.7), channel_id=1, source_target_pairs={{0,16},{16,32},{32,48},{48,64},{64,80},{80,96},{96,112},{112,128},... | collective-permute-start | bytes 1572872 | tf_op jit(solution)/shard_map/ppermute | solution.py:33
  117.8 18.8 %all-to-all-start.3 = ((bf16[16,128,128]{1,2,0:T(8,128)(2,1)}), bf16[16,128,128]{1,2,0:T(8,128)(2,1)S(1)}, u32[]{:S(2)}, u32[]{:S(2)}) async-start(bf16[16,128,128]{1,2,0:T(8,128)(2,1)} %copy.24), calls=%async_computation.3 | async-start | bytes 1048576 | tf_op jit(solution)/shard_map/all_to_all | solution.py:25

commit v7 on v6

--- a/solution.py
+++ b/solution.py
@@ -176,20 +176,24 @@
     row_count, width = kv_heads.shape
     block_count = row_count // BLOCK
     kv = kv_heads.reshape(block_count, BLOCK, width)
-    left = from_behind(kv, "blk", 1)
-    right = from_behind(kv, "blk", -1)
+    count = lax.axis_size("blk")
+    near_pairs = [(i, i ^ 1) for i in range(count)]
+    far_pairs = [(i, (i + 1 if i % 2 else i - 1) % count) for i in range(count)]
+    near = lax.ppermute(kv, "blk", near_pairs)
+    far = lax.ppermute(kv, "blk", far_pairs)
     qd = to_heads(query_rows, out_grad).reshape(block_count, BLOCK, width)
-    first_row = lax.axis_index("blk") * block_count
-    picks = jnp.stack(
-        [lax.dynamic_slice_in_dim(neighbour_blocks[:, c], first_row, block_count, 0) for c in range(2)]
-    )
+    place = lax.axis_index("blk")
+    first_row = place * block_count
+    picks = [lax.dynamic_slice_in_dim(neighbour_blocks[:, c], first_row, block_count, 0) for c in range(2)]
+    even = place % 2 == 0
+    picks = jnp.stack([jnp.where(even, picks[1], picks[0]), jnp.where(even, picks[0], picks[1])])
     picks = jnp.clip(picks, 0, block_count - 1).astype(jnp.int32)
-    out_pair, highest, inverse, delta, to_left, to_right = attention(picks, qd, kv, left, right)
-    from_right = from_behind(to_left, "blk", -1).astype(jnp.float32)
-    from_left = from_behind(to_right, "blk", 1).astype(jnp.float32)
+    out_pair, highest, inverse, delta, to_near, to_far = attention(picks, qd, kv, near, far)
+    from_near = lax.ppermute(to_near, "blk", near_pairs).astype(jnp.float32)
+    from_far = lax.ppermute(to_far, "blk", far_pairs).astype(jnp.float32)
     own_grads = own_grads_of(qd, kv, highest, inverse, delta)
     query_grad, attended = to_rows(out_pair.reshape(row_count, width))
-    kv_grads = (own_grads + from_right + from_left).astype(jnp.bfloat16)
+    kv_grads = (own_grads + from_near + from_far).astype(jnp.bfloat16)
     key_grad, value_grad = to_rows(kv_grads.reshape(row_count, width))
     return (attended, query_grad, key_grad, value_grad)
 

time: 139 us -> 135 us (0.971)
  waiting for transfers between devices: 53.3 us -> 47.8 us
  starting transfers between devices: 46.1 us -> 47.5 us
    ppermute x4, waiting for transfers between devices: 29 us -> 23.5 us  [the longest x1 12.2 us: shards(): from_far = lax.ppermute(to_far, 'blk', far_pairs).astype(jnp.float32)]
  transfers between devices with their start and end apart: 8 -> 8, of which waited for: 7 -> 5; matrix products, arithmetic and copies ran while one was open for 5% -> 5% of each run, Pallas kernels for 4% -> 4%
where the time goes in v7:
time: 135 us; the launch traced here: 134 us
  waiting for transfers between devices  47.8 us (35%)
  starting transfers between devices  47.5 us (35%)
  Pallas kernels  22.7 us (17%)
  local copies, waits for them, and re-layouts  11.9 us (9%)
  other arithmetic  3.74 us (3%)
    pallas_call x1, Pallas kernels, attention(): pl.pallas_call(attention_kernel, grid_spec=pltpu.PrefetchScalarGridSpec(n...  16.8 us
    all_to_all x2, starting transfers between devices, to_heads(): lax.all_to_all(packed, 'head', split_axis=1, concat_axis=0, tiled=True)  15.1 us
    all_to_all x2, waiting for transfers between devices, to_heads(): lax.all_to_all(packed, 'head', split_axis=1, concat_axis=0, tiled=True)  14.6 us
    all_to_all x2, starting transfers between devices, to_rows(): lax.all_to_all(packed, 'head', split_axis=0, concat_axis=1, tiled=True)  14.3 us
    ppermute x1, waiting for transfers between devices, shards(): from_far = lax.ppermute(to_far, 'blk', far_pairs).astype(jnp.float32)  12.2 us
    ppermute x1, waiting for transfers between devices, shards(): far = lax.ppermute(kv, 'blk', far_pairs)  11.3 us
    ppermute x1, starting transfers between devices, shards(): far = lax.ppermute(kv, 'blk', far_pairs)  10.9 us
    all_to_all x2, waiting for transfers between devices, to_rows(): lax.all_to_all(packed, 'head', split_axis=0, concat_axis=1, tiled=True)  9.75 us
  transfers between devices with their start and end apart: 8, of which 5 were waited for; matrix products, arithmetic and copies ran while one was open for 5% of the time, Pallas kernels for 4%

profile of v7, /device:TPU:8, one launch (start us, length us, event | category | flops | bytes accessed | tf_op | source)
XLA Modules:
  0.0 134.4 jit_solution(5907676747299374783)
XLA Ops:
  0.6 0.0 copy-start.3
  0.6 1.2 copy.20
  1.8 0.0 copy-done.3
  1.8 0.2 copy.21
  2.0 0.8 pad_maximum_fusion.1
  2.8 0.0 copy-start.4
  2.8 9.5 %all-to-all-start.1 = ((bf16[128,16,128]{0,2,1:T(8,128)(2,1)}), bf16[128,16,128]{0,2,1:T(8,128)(2,1)S(1)}, u32[]{:S(2)}, u32[]{:S(2)}) async-start(bf16[128,16,128]{0,2,1:T(8,128)(2,1)} %pad_maximum_fusion.1), calls=%async_computation.1 | async-start | bytes 1048576 | tf_op jit(solution)/shard_map/all_to_all | solution.py:18
  12.3 0.0 copy-done.4
  12.3 0.0 copy-start.5
  12.4 0.2 copy.17
  12.5 0.8 copy-done.5
  13.3 0.2 copy.18
  13.5 0.8 pad_maximum_fusion
  14.3 13.1 %all-to-all-done.1 = bf16[128,16,128]{0,2,1:T(8,128)(2,1)S(1)} async-done(((bf16[128,16,128]{0,2,1:T(8,128)(2,1)}), bf16[128,16,128]{0,2,1:T(8,128)(2,1)S(1)}, u32[]{:S(2)}, u32[]{:S(2)}) %all-to-all-start.1) | async-done | bytes 524320 | tf_op jit(solution)/shard_map/all_to_all | solution.py:18
  27.4 5.6 %all-to-all-start = ((bf16[128,16,128]{0,2,1:T(8,128)(2,1)}), bf16[128,16,128]{0,2,1:T(8,128)(2,1)S(1)}, u32[]{:S(2)}, u32[]{:S(2)}) async-start(bf16[128,16,128]{0,2,1:T(8,128)(2,1)} %pad_maximum_fusion), calls=%async_computation | async-start | bytes 1048576 | tf_op jit(solution)/shard_map/all_to_all | solution.py:18
  33.0 0.3 copy.22
  33.2 0.0 copy-start
  33.3 10.9 %collective-permute-start.1 = (bf16[4,512,128]{2,1,0:T(8,128)(2,1)S(1)}, bf16[4,512,128]{2,1,0:T(8,128)(2,1)S(1)}, u32[]{:S(2)}, u32[]{:S(2)}) collective-permute-start(bf16[4,512,128]{2,1,0:T(8,128)(2,1)S(1)} %bitcast.28), channel_id=1, source_target_pairs={{0,496},{16,32},{32,16},{48,64},{64,48},{80,96},{96,80},{112,128},... | collective-permute-start | bytes 1572872 | tf_op jit(solution)/shard_map/ppermute | solution.py:183
  44.2 1.9 %collective-permute-start = (bf16[4,512,128]{2,1,0:T(8,128)(2,1)S(1)}, bf16[4,512,128]{2,1,0:T(8,128)(2,1)S(1)}, u32[]{:S(2)}, u32[]{:S(2)}) collective-permute-start(bf16[4,512,128]{2,1,0:T(8,128)(2,1)S(1)} %bitcast.29), channel_id=1, source_target_pairs={{0,16},{16,0},{32,48},{48,32},{64,80},{80,64},{96,112},{112,96},{1... | collective-permute-start | bytes 1572872 | tf_op jit(solution)/shard_map/ppermute | solution.py:182
  46.1 0.0 copy-start.6
  46.1 0.7 copy-done.6
  46.8 0.1 fusion
  46.9 0.6 add_clamp_fusion.picks_ref
  47.5 1.5 %all-to-all-done = bf16[128,16,128]{0,2,1:T(8,128)(2,1)S(1)} async-done(((bf16[128,16,128]{0,2,1:T(8,128)(2,1)}), bf16[128,16,128]{0,2,1:T(8,128)(2,1)S(1)}, u32[]{:S(2)}, u32[]{:S(2)}) %all-to-all-start) | async-done | bytes 524320 | tf_op jit(solution)/shard_map/all_to_all | solution.py:18
  49.0 1.0 copy.19
  50.0 0.0 copy-done
  50.0 11.3 %collective-permute-done.1.right_ref = bf16[4,512,128]{2,1,0:T(8,128)(2,1)S(1)} collective-permute-done((bf16[4,512,128]{2,1,0:T(8,128)(2,1)S(1)}, bf16[4,512,128]{2,1,0:T(8,128)(2,1)S(1)}, u32[]{:S(2)}, u32[]{:S(2)}) %collective-permute-start.1) | collective-permute-done | bytes 524320 | tf_op jit(solution)/shard_map/ppermute | solution.py:183
  61.3 0.0 copy-start.1
  61.3 0.0 collective-permute-done.left_ref
  61.3 0.0 copy-start.2
  61.3 0.8 copy-done.1
  62.1 0.2 copy-done.2
  62.2 16.8 %shard_map.84 = (bf16[4,512,128]{2,1,0:T(8,128)(2,1)}, f32[4,512,1]{2,1,0:T(8,128)}, f32[4,512,1]{2,1,0:T(8,128)}, f32[4,512,1]{2,1,0:T(8,128)}, bf16[4,512,128]...) custom-call(s32[2,4]{1,0:T(2,128)} %add_clamp_fusion.picks_ref, bf16[4,512,128]{2,1,0:T(8,128)(2,1)} %bitcast.32, ...), custom_call_target="tpu_custom_call" | custom-call | tf_op jit(solution)/shard_map/pallas_call | solution.py:152
  79.1 2.0 %copy.23 = bf16[16,128,128]{1,2,0:T(8,128)(2,1)} copy(bf16[16,128,128]{2,1,0:T(8,128)(2,1)} %bitcast.47) | data formatting | bytes 1048576 | tf_op jit(solution)/shard_map/all_to_all | solution.py:25
  81.1 0.0 copy-start.8
  81.1 0.0 copy-start.7
  81.1 7.6 %all-to-all-start.2 = ((bf16[16,128,128]{1,2,0:T(8,128)(2,1)}), bf16[16,128,128]{1,2,0:T(8,128)(2,1)S(1)}, u32[]{:S(2)}, u32[]{:S(2)}) async-start(bf16[16,128,128]{1,2,0:T(8,128)(2,1)} %copy.23), calls=%async_computation.2 | async-start | bytes 1048576 | tf_op jit(solution)/shard_map/all_to_all | solution.py:25
  88.7 0.0 copy-done.8
  88.7 1.9 %collective-permute-start.2 = (bf16[4,512,128]{2,1,0:T(8,128)(2,1)S(1)}, bf16[4,512,128]{2,1,0:T(8,128)(2,1)S(1)}, u32[]{:S(2)}, u32[]{:S(2)}) collective-permute-start(bf16[4,512,128]{2,1,0:T(8,128)(2,1)S(1)} %copy-done.8), channel_id=1, source_target_pairs={{0,16},{16,0},{32,48},{48,32},{64,80},{80,64},{96,112},{112,96},{1... | collective-permute-start | bytes 1572872 | tf_op jit(solution)/shard_map/ppermute | solution.py:192
  90.6 0.0 copy-done.7
  90.6 3.3 %collective-permute-start.3 = (bf16[4,512,128]{2,1,0:T(8,128)(2,1)S(1)}, bf16[4,512,128]{2,1,0:T(8,128)(2,1)S(1)}, u32[]{:S(2)}, u32[]{:S(2)}) collective-permute-start(bf16[4,512,128]{2,1,0:T(8,128)(2,1)S(1)} %copy-done.7), channel_id=1, source_target_pairs={{0,496},{16,32},{32,16},{48,64},{64,48},{80,96},{96,80},{112,128},... | collective-permute-start | bytes 1572872 | tf_op jit(solution)/shard_map/ppermute | solution.py:193
  93.9 5.9 %shard_map.85 = f32[4,512,128]{2,1,0:T(8,128)} custom-call(bf16[4,512,128]{2,1,0:T(8,128)(2,1)} %bitcast.33, bf16[4,512,128]{2,1,0:T(8,128)(2,1)} %bitcast.31, f32[4,512,1]{2,1,0:T(8,128)} %get-tuple-element.11.highest_ref, f32[4,512,1]{2,1,0:T(8,128)} %get-tuple-element.12.inverse_ref, f32[4,512,1]{2,1,0:T(8,128)} %get-tuple-element.13.delta_ref), custom_call_target="tpu_custom_call" | custom-call | tf_op jit(solution)/shard_map/pallas_call | solution.py:132
  99.8 0.0 collective-permute-done.2
  99.8 12.2 %collective-permute-done.3 = bf16[4,512,128]{2,1,0:T(8,128)(2,1)S(1)} collective-permute-done((bf16[4,512,128]{2,1,0:T(8,128)(2,1)S(1)}, bf16[4,512,128]{2,1,0:T(8,128)(2,1)S(1)}, u32[]{:S(2)}, u32[]{:S(2)}) %collective-permute-start.3) | collective-permute-done | bytes 524320 | tf_op jit(solution)/shard_map/ppermute | solution.py:193
  112.0 1.4 %add_convert_fusion = bf16[4,512,128]{2,1,0:T(8,128)(2,1)S(1)} fusion(bf16[4,512,128]{2,1,0:T(8,128)(2,1)S(1)} %collective-permute-done.3, f32[4,512,128]{2,1,0:T(8,128)} %shard_map.85, bf16[4,512,128]{2,1,0:T(8,128)(2,1)S(1)} %collective-permute-done.2), kind=kLoop, calls=%fused_computation | loop fusion | flops 1310720 | bytes 2621440 | tf_op jit(solution)/shard_map/convert_element_type | solution.py:196
  113.4 1.0 copy.24
  114.4 0.0 all-to-all-done.2
  114.4 6.7 %all-to-all-start.3 = ((bf16[16,128,128]{1,2,0:T(8,128)(2,1)}), bf16[16,128,128]{1,2,0:T(8,128)(2,1)S(1)}, u32[]{:S(2)}, u32[]{:S(2)}) async-start(bf16[16,128,128]{1,2,0:T(8,128)(2,1)} %copy.24), calls=%async_computation.3 | async-start | bytes 1048576 | tf_op jit(solution)/shard_map/all_to_all | solution.py:25
  121.2 0.9 copy.26
  122.1 0.8 copy.25
  122.9 9.7 %all-to-all-done.3 = bf16[16,128,128]{1,2,0:T(8,128)(2,1)S(1)} async-done(((bf16[16,128,128]{1,2,0:T(8,128)(2,1)}), bf16[16,128,128]{1,2,0:T(8,128)(2,1)S(1)}, u32[]{:S(2)}, u32[]{:S(2)}) %all-to-all-start.3) | async-done | bytes 524320 | tf_op jit(solution)/shard_map/all_to_all | solution.py:25
  132.7 0.9 copy.28
  133.5 0.8 copy.27
  (3 shorter events, 0.1 us)
Async XLA Ops:
  0.6 1.2 copy-start.3
  2.8 9.5 %copy-start.4 = (bf16[128,1024]{1,0:T(8,128)(2,1)S(1)}, bf16[128,1024]{1,0:T(8,128)(2,1)}, u32[]{:S(2)}) copy-start(bf16[128,1024]{1,0:T(8,128)(2,1)} %param.5) | copy-start | bytes 786436
  2.8 24.6 %all-to-all-start.1 = ((bf16[128,16,128]{0,2,1:T(8,128)(2,1)}), bf16[128,16,128]{0,2,1:T(8,128)(2,1)S(1)}, u32[]{:S(2)}, u32[]{:S(2)}) async-start(bf16[128,16,128]{0,2,1:T(8,128)(2,1)} %pad_maximum_fusion.1), calls=%async_computation.1 | async-start | bytes 1048576 | tf_op jit(solution)/shard_map/all_to_all | solution.py:18
  12.3 1.0 copy-start.5
  27.4 21.6 %all-to-all-start = ((bf16[128,16,128]{0,2,1:T(8,128)(2,1)}), bf16[128,16,128]{0,2,1:T(8,128)(2,1)S(1)}, u32[]{:S(2)}, u32[]{:S(2)}) async-start(bf16[128,16,128]{0,2,1:T(8,128)(2,1)} %pad_maximum_fusion), calls=%async_computation | async-start | bytes 1048576 | tf_op jit(solution)/shard_map/all_to_all | solution.py:18
  33.2 16.7 %copy-start = (bf16[16,128,1,128]{3,1,0,2:T(8,128)(2,1)}, bf16[16,128,1,128]{3,1,0,2:T(8,128)(2,1)S(1)}, u32[]{:S(2)}) copy-start(bf16[16,128,1,128]{3,1,0,2:T(8,128)(2,1)S(1)} %copy.22) | copy-start | bytes 1572868
  33.3 28.0 %collective-permute-start.1 = (bf16[4,512,128]{2,1,0:T(8,128)(2,1)S(1)}, bf16[4,512,128]{2,1,0:T(8,128)(2,1)S(1)}, u32[]{:S(2)}, u32[]{:S(2)}) collective-permute-start(bf16[4,512,128]{2,1,0:T(8,128)(2,1)S(1)} %bitcast.28), channel_id=1, source_target_pairs={{0,496},{16,32},{32,16},{48,64},{64,48},{80,96},{96,80},{112,128},... | collective-permute-start | bytes 1572872 | tf_op jit(solution)/shard_map/ppermute | solution.py:183
  44.2 17.1 %collective-permute-start = (bf16[4,512,128]{2,1,0:T(8,128)(2,1)S(1)}, bf16[4,512,128]{2,1,0:T(8,128)(2,1)S(1)}, u32[]{:S(2)}, u32[]{:S(2)}) collective-permute-start(bf16[4,512,128]{2,1,0:T(8,128)(2,1)S(1)} %bitcast.29), channel_id=1, source_target_pairs={{0,16},{16,0},{32,48},{48,32},{64,80},{80,64},{96,112},{112,96},{1... | collective-permute-start | bytes 1572872 | tf_op jit(solution)/shard_map/ppermute | solution.py:182
  46.1 0.7 copy-start.6
  61.3 0.8 copy-start.1
  61.3 1.0 copy-start.2
  81.1 7.6 %copy-start.8 = (bf16[4,512,128]{2,1,0:T(8,128)(2,1)S(1)}, bf16[4,512,128]{2,1,0:T(8,128)(2,1)}, u32[]{:S(2)}) copy-start(bf16[4,512,128]{2,1,0:T(8,128)(2,1)} %get-tuple-element.14) | copy-start | bytes 1572868
  81.1 9.5 %copy-start.7 = (bf16[4,512,128]{2,1,0:T(8,128)(2,1)S(1)}, bf16[4,512,128]{2,1,0:T(8,128)(2,1)}, u32[]{:S(2)}) copy-start(bf16[4,512,128]{2,1,0:T(8,128)(2,1)} %get-tuple-element.15) | copy-start | bytes 1572868
  81.1 33.4 %all-to-all-start.2 = ((bf16[16,128,128]{1,2,0:T(8,128)(2,1)}), bf16[16,128,128]{1,2,0:T(8,128)(2,1)S(1)}, u32[]{:S(2)}, u32[]{:S(2)}) async-start(bf16[16,128,128]{1,2,0:T(8,128)(2,1)} %copy.23), calls=%async_computation.2 | async-start | bytes 1048576 | tf_op jit(solution)/shard_map/all_to_all | solution.py:25
  88.7 11.1 %collective-permute-start.2 = (bf16[4,512,128]{2,1,0:T(8,128)(2,1)S(1)}, bf16[4,512,128]{2,1,0:T(8,128)(2,1)S(1)}, u32[]{:S(2)}, u32[]{:S(2)}) collective-permute-start(bf16[4,512,128]{2,1,0:T(8,128)(2,1)S(1)} %copy-done.8), channel_id=1, source_target_pairs={{0,16},{16,0},{32,48},{48,32},{64,80},{80,64},{96,112},{112,96},{1... | collective-permute-start | bytes 1572872 | tf_op jit(solution)/shard_map/ppermute | solution.py:192
  90.6 21.4 %collective-permute-start.3 = (bf16[4,512,128]{2,1,0:T(8,128)(2,1)S(1)}, bf16[4,512,128]{2,1,0:T(8,128)(2,1)S(1)}, u32[]{:S(2)}, u32[]{:S(2)}) collective-permute-start(bf16[4,512,128]{2,1,0:T(8,128)(2,1)S(1)} %copy-done.7), channel_id=1, source_target_pairs={{0,496},{16,32},{32,16},{48,64},{64,48},{80,96},{96,80},{112,128},... | collective-permute-start | bytes 1572872 | tf_op jit(solution)/shard_map/ppermute | solution.py:193
  114.4 18.2 %all-to-all-start.3 = ((bf16[16,128,128]{1,2,0:T(8,128)(2,1)}), bf16[16,128,128]{1,2,0:T(8,128)(2,1)S(1)}, u32[]{:S(2)}, u32[]{:S(2)}) async-start(bf16[16,128,128]{1,2,0:T(8,128)(2,1)} %copy.24), calls=%async_computation.3 | async-start | bytes 1048576 | tf_op jit(solution)/shard_map/all_to_all | solution.py:25

commit v8 on v7

--- a/solution.py
+++ b/solution.py
@@ -38,10 +38,11 @@
     out_ref, highest_ref, inverse_ref, delta_ref, to_left_ref, to_right_ref, left_acc, right_acc,
 ):
     number = pl.program_id(0)
+    half = pl.program_id(1)
     scale = HEAD_DIM ** (-0.5)
     f32 = jnp.float32
 
-    @pl.when(number == 0)
+    @pl.when((number == 0) & (half == 0))
     def _():
         left_acc[...] = jnp.zeros(left_acc.shape, f32)
         right_acc[...] = jnp.zeros(right_acc.shape, f32)
@@ -64,7 +65,7 @@
         return lax.dot_general(a, b, (((0,), (0,)), ((), ())), preferred_element_type=f32)
 
     scores = [nt(query_ext, pair) * scale for pair in pairs]
-    row = lax.broadcasted_iota(jnp.int32, scores[0].shape, 0)
+    row = lax.broadcasted_iota(jnp.int32, scores[0].shape, 0) + half * packed.shape[0]
     col = lax.broadcasted_iota(jnp.int32, scores[0].shape, 1)
     scores[0] = jnp.where(col <= row, scores[0], -jnp.inf)
     highest = jnp.max(scores[0], axis=1, keepdims=True)
@@ -86,8 +87,9 @@
     highest_ref[0] = highest
     inverse_ref[0] = inverse
     delta_ref[0] = row_delta
+    key_low = lax.broadcasted_iota(jnp.int32, pairs[0].shape, 1) < HEAD_DIM
     kv_parts = [None] + [
-        jnp.where(low, tn(d, packed) * scale, tn(w, packed))
+        jnp.where(key_low, tn(d, packed) * scale, tn(w, packed))
         for d, w in zip(score_grads[1:], weights_bf[1:])
     ]
     left_pick = picks_ref[0, number]
@@ -95,7 +97,7 @@
     left_acc[left_pick] += kv_parts[1]
     right_acc[right_pick] += kv_parts[2]
 
-    @pl.when(number == pl.num_programs(0) - 1)
+    @pl.when((number == pl.num_programs(0) - 1) & (half == pl.num_programs(1) - 1))
     def _():
         to_left_ref[...] = left_acc[...].astype(jnp.bfloat16)
         to_right_ref[...] = right_acc[...].astype(jnp.bfloat16)
@@ -142,20 +144,22 @@
 
 def attention(picks, qd, kv, left, right):
     block_count, block, width = kv.shape
-    left_spec = pl.BlockSpec((1, block, width), lambda n, p: (p[0, n], 0, 0))
-    right_spec = pl.BlockSpec((1, block, width), lambda n, p: (p[1, n], 0, 0))
-    one_spec = pl.BlockSpec((1, block, width), lambda n, p: (n, 0, 0))
-    whole_spec = pl.BlockSpec((block_count, block, width), lambda n, p: (0, 0, 0))
-    stat_spec = pl.BlockSpec((1, block, 1), lambda n, p: (n, 0, 0))
+    tile = block // 2
+    left_spec = pl.BlockSpec((1, block, width), lambda n, h, p: (p[0, n], 0, 0))
+    right_spec = pl.BlockSpec((1, block, width), lambda n, h, p: (p[1, n], 0, 0))
+    kv_spec = pl.BlockSpec((1, block, width), lambda n, h, p: (n, 0, 0))
+    tile_spec = pl.BlockSpec((1, tile, width), lambda n, h, p: (n, h, 0))
+    whole_spec = pl.BlockSpec((block_count, block, width), lambda n, h, p: (0, 0, 0))
+    stat_spec = pl.BlockSpec((1, tile, 1), lambda n, h, p: (n, h, 0))
     shape = (block_count, block, width)
     stat = jax.ShapeDtypeStruct((block_count, block, 1), jnp.float32)
     return pl.pallas_call(
         attention_kernel,
         grid_spec=pltpu.PrefetchScalarGridSpec(
             num_scalar_prefetch=1,
-            grid=(block_count,),
-            in_specs=[one_spec, one_spec, left_spec, right_spec],
-            out_specs=[one_spec, stat_spec, stat_spec, stat_spec, whole_spec, whole_spec],
+            grid=(block_count, 2),
+            in_specs=[tile_spec, kv_spec, left_spec, right_spec],
+            out_specs=[tile_spec, stat_spec, stat_spec, stat_spec, whole_spec, whole_spec],
             scratch_shapes=[pltpu.VMEM(shape, jnp.float32), pltpu.VMEM(shape, jnp.float32)],
         ),
         out_shape=[
@@ -166,7 +170,7 @@
             jax.ShapeDtypeStruct(shape, jnp.bfloat16),
             jax.ShapeDtypeStruct(shape, jnp.bfloat16),
         ],
-        compiler_params=pltpu.CompilerParams(dimension_semantics=("arbitrary",)),
+        compiler_params=pltpu.CompilerParams(dimension_semantics=("arbitrary", "arbitrary")),
         interpret=INTERPRET,
     )(picks, qd, kv, left, right)
 

time: 135 us -> 136 us (level)
  no operation moved by 1% of the time
where the time goes in v8:
time: 136 us; the launch traced here: 135 us
  waiting for transfers between devices  47.8 us (35%)
  starting transfers between devices  47.4 us (35%)
  Pallas kernels  23.2 us (17%)
  local copies, waits for them, and re-layouts  11.9 us (9%)
  other arithmetic  3.74 us (3%)
    pallas_call x1, Pallas kernels, attention(): pl.pallas_call(attention_kernel, grid_spec=pltpu.PrefetchScalarGridSpec(n...  17.3 us
    all_to_all x2, starting transfers between devices, to_heads(): lax.all_to_all(packed, 'head', split_axis=1, concat_axis=0, tiled=True)  15.1 us
    all_to_all x2, waiting for transfers between devices, to_heads(): lax.all_to_all(packed, 'head', split_axis=1, concat_axis=0, tiled=True)  14.6 us
    all_to_all x2, starting transfers between devices, to_rows(): lax.all_to_all(packed, 'head', split_axis=0, concat_axis=1, tiled=True)  14.3 us
    ppermute x1, waiting for transfers between devices, shards(): from_far = lax.ppermute(to_far, 'blk', far_pairs).astype(jnp.float32)  12.2 us
    ppermute x1, waiting for transfers between devices, shards(): far = lax.ppermute(kv, 'blk', far_pairs)  11.3 us
    ppermute x1, starting transfers between devices, shards(): far = lax.ppermute(kv, 'blk', far_pairs)  10.9 us
    all_to_all x2, waiting for transfers between devices, to_rows(): lax.all_to_all(packed, 'head', split_axis=0, concat_axis=1, tiled=True)  9.75 us
  transfers between devices with their start and end apart: 8, of which 5 were waited for; matrix products, arithmetic and copies ran while one was open for 5% of the time, Pallas kernels for 4%

profile of v8, /device:TPU:8, one launch (start us, length us, event | category | flops | bytes accessed | tf_op | source)
XLA Modules:
  0.0 134.9 jit_solution(14892241743048254683)
XLA Ops:
  0.6 0.0 copy-start.3
  0.6 1.2 copy.20
  1.8 0.0 copy-done.3
  1.8 0.2 copy.21
  2.0 0.8 pad_maximum_fusion.1
  2.8 0.0 copy-start.4
  2.8 9.5 %all-to-all-start.1 = ((bf16[128,16,128]{0,2,1:T(8,128)(2,1)}), bf16[128,16,128]{0,2,1:T(8,128)(2,1)S(1)}, u32[]{:S(2)}, u32[]{:S(2)}) async-start(bf16[128,16,128]{0,2,1:T(8,128)(2,1)} %pad_maximum_fusion.1), calls=%async_computation.1 | async-start | bytes 1048576 | tf_op jit(solution)/shard_map/all_to_all | solution.py:18
  12.3 0.0 copy-done.4
  12.3 0.0 copy-start.5
  12.4 0.2 copy.17
  12.5 0.8 copy-done.5
  13.3 0.2 copy.18
  13.5 0.8 pad_maximum_fusion
  14.3 13.1 %all-to-all-done.1 = bf16[128,16,128]{0,2,1:T(8,128)(2,1)S(1)} async-done(((bf16[128,16,128]{0,2,1:T(8,128)(2,1)}), bf16[128,16,128]{0,2,1:T(8,128)(2,1)S(1)}, u32[]{:S(2)}, u32[]{:S(2)}) %all-to-all-start.1) | async-done | bytes 524320 | tf_op jit(solution)/shard_map/all_to_all | solution.py:18
  27.4 5.6 %all-to-all-start = ((bf16[128,16,128]{0,2,1:T(8,128)(2,1)}), bf16[128,16,128]{0,2,1:T(8,128)(2,1)S(1)}, u32[]{:S(2)}, u32[]{:S(2)}) async-start(bf16[128,16,128]{0,2,1:T(8,128)(2,1)} %pad_maximum_fusion), calls=%async_computation | async-start | bytes 1048576 | tf_op jit(solution)/shard_map/all_to_all | solution.py:18
  33.0 0.3 copy.22
  33.2 0.0 copy-start
  33.3 10.9 %collective-permute-start.1 = (bf16[4,512,128]{2,1,0:T(8,128)(2,1)S(1)}, bf16[4,512,128]{2,1,0:T(8,128)(2,1)S(1)}, u32[]{:S(2)}, u32[]{:S(2)}) collective-permute-start(bf16[4,512,128]{2,1,0:T(8,128)(2,1)S(1)} %bitcast.28), channel_id=1, source_target_pairs={{0,496},{16,32},{32,16},{48,64},{64,48},{80,96},{96,80},{112,128},... | collective-permute-start | bytes 1572872 | tf_op jit(solution)/shard_map/ppermute | solution.py:187
  44.2 1.9 %collective-permute-start = (bf16[4,512,128]{2,1,0:T(8,128)(2,1)S(1)}, bf16[4,512,128]{2,1,0:T(8,128)(2,1)S(1)}, u32[]{:S(2)}, u32[]{:S(2)}) collective-permute-start(bf16[4,512,128]{2,1,0:T(8,128)(2,1)S(1)} %bitcast.29), channel_id=1, source_target_pairs={{0,16},{16,0},{32,48},{48,32},{64,80},{80,64},{96,112},{112,96},{1... | collective-permute-start | bytes 1572872 | tf_op jit(solution)/shard_map/ppermute | solution.py:186
  46.1 0.0 copy-start.6
  46.1 0.7 copy-done.6
  46.8 0.1 fusion
  46.9 0.6 add_clamp_fusion.picks_ref
  47.5 1.5 %all-to-all-done = bf16[128,16,128]{0,2,1:T(8,128)(2,1)S(1)} async-done(((bf16[128,16,128]{0,2,1:T(8,128)(2,1)}), bf16[128,16,128]{0,2,1:T(8,128)(2,1)S(1)}, u32[]{:S(2)}, u32[]{:S(2)}) %all-to-all-start) | async-done | bytes 524320 | tf_op jit(solution)/shard_map/all_to_all | solution.py:18
  49.0 1.0 copy.19
  50.0 0.0 copy-done
  50.0 11.3 %collective-permute-done.1.right_ref = bf16[4,512,128]{2,1,0:T(8,128)(2,1)S(1)} collective-permute-done((bf16[4,512,128]{2,1,0:T(8,128)(2,1)S(1)}, bf16[4,512,128]{2,1,0:T(8,128)(2,1)S(1)}, u32[]{:S(2)}, u32[]{:S(2)}) %collective-permute-start.1) | collective-permute-done | bytes 524320 | tf_op jit(solution)/shard_map/ppermute | solution.py:187
  61.3 0.0 copy-start.1
  61.3 0.0 collective-permute-done.left_ref
  61.3 0.0 copy-start.2
  61.3 0.8 copy-done.1
  62.1 0.2 copy-done.2
  62.2 17.3 %shard_map.84 = (bf16[4,512,128]{2,1,0:T(8,128)(2,1)}, f32[4,512,1]{2,1,0:T(8,128)}, f32[4,512,1]{2,1,0:T(8,128)}, f32[4,512,1]{2,1,0:T(8,128)}, bf16[4,512,128]...) custom-call(s32[2,4]{1,0:T(2,128)} %add_clamp_fusion.picks_ref, bf16[4,512,128]{2,1,0:T(8,128)(2,1)} %bitcast.32, ...), custom_call_target="tpu_custom_call" | custom-call | tf_op jit(solution)/shard_map/pallas_call | solution.py:156
  79.6 2.0 %copy.23 = bf16[16,128,128]{1,2,0:T(8,128)(2,1)} copy(bf16[16,128,128]{2,1,0:T(8,128)(2,1)} %bitcast.47) | data formatting | bytes 1048576 | tf_op jit(solution)/shard_map/all_to_all | solution.py:25
  81.6 0.0 copy-start.8
  81.6 0.0 copy-start.7
  81.6 7.6 %all-to-all-start.2 = ((bf16[16,128,128]{1,2,0:T(8,128)(2,1)}), bf16[16,128,128]{1,2,0:T(8,128)(2,1)S(1)}, u32[]{:S(2)}, u32[]{:S(2)}) async-start(bf16[16,128,128]{1,2,0:T(8,128)(2,1)} %copy.23), calls=%async_computation.2 | async-start | bytes 1048576 | tf_op jit(solution)/shard_map/all_to_all | solution.py:25
  89.2 0.0 copy-done.8
  89.2 1.9 %collective-permute-start.2 = (bf16[4,512,128]{2,1,0:T(8,128)(2,1)S(1)}, bf16[4,512,128]{2,1,0:T(8,128)(2,1)S(1)}, u32[]{:S(2)}, u32[]{:S(2)}) collective-permute-start(bf16[4,512,128]{2,1,0:T(8,128)(2,1)S(1)} %copy-done.8), channel_id=1, source_target_pairs={{0,16},{16,0},{32,48},{48,32},{64,80},{80,64},{96,112},{112,96},{1... | collective-permute-start | bytes 1572872 | tf_op jit(solution)/shard_map/ppermute | solution.py:196
  91.2 0.0 copy-done.7
  91.2 3.3 %collective-permute-start.3 = (bf16[4,512,128]{2,1,0:T(8,128)(2,1)S(1)}, bf16[4,512,128]{2,1,0:T(8,128)(2,1)S(1)}, u32[]{:S(2)}, u32[]{:S(2)}) collective-permute-start(bf16[4,512,128]{2,1,0:T(8,128)(2,1)S(1)} %copy-done.7), channel_id=1, source_target_pairs={{0,496},{16,32},{32,16},{48,64},{64,48},{80,96},{96,80},{112,128},... | collective-permute-start | bytes 1572872 | tf_op jit(solution)/shard_map/ppermute | solution.py:197
  94.5 5.9 %shard_map.85 = f32[4,512,128]{2,1,0:T(8,128)} custom-call(bf16[4,512,128]{2,1,0:T(8,128)(2,1)} %bitcast.33, bf16[4,512,128]{2,1,0:T(8,128)(2,1)} %bitcast.31, f32[4,512,1]{2,1,0:T(8,128)} %get-tuple-element.11.highest_ref, f32[4,512,1]{2,1,0:T(8,128)} %get-tuple-element.12.inverse_ref, f32[4,512,1]{2,1,0:T(8,128)} %get-tuple-element.13.delta_ref), custom_call_target="tpu_custom_call" | custom-call | tf_op jit(solution)/shard_map/pallas_call | solution.py:134
  100.3 0.0 collective-permute-done.2
  100.4 12.2 %collective-permute-done.3 = bf16[4,512,128]{2,1,0:T(8,128)(2,1)S(1)} collective-permute-done((bf16[4,512,128]{2,1,0:T(8,128)(2,1)S(1)}, bf16[4,512,128]{2,1,0:T(8,128)(2,1)S(1)}, u32[]{:S(2)}, u32[]{:S(2)}) %collective-permute-start.3) | collective-permute-done | bytes 524320 | tf_op jit(solution)/shard_map/ppermute | solution.py:197
  112.6 1.4 %add_convert_fusion = bf16[4,512,128]{2,1,0:T(8,128)(2,1)S(1)} fusion(bf16[4,512,128]{2,1,0:T(8,128)(2,1)S(1)} %collective-permute-done.3, f32[4,512,128]{2,1,0:T(8,128)} %shard_map.85, bf16[4,512,128]{2,1,0:T(8,128)(2,1)S(1)} %collective-permute-done.2), kind=kLoop, calls=%fused_computation | loop fusion | flops 1310720 | bytes 2621440 | tf_op jit(solution)/shard_map/convert_element_type | solution.py:200
  114.0 1.0 copy.24
  115.0 0.0 all-to-all-done.2
  115.0 6.7 %all-to-all-start.3 = ((bf16[16,128,128]{1,2,0:T(8,128)(2,1)}), bf16[16,128,128]{1,2,0:T(8,128)(2,1)S(1)}, u32[]{:S(2)}, u32[]{:S(2)}) async-start(bf16[16,128,128]{1,2,0:T(8,128)(2,1)} %copy.24), calls=%async_computation.3 | async-start | bytes 1048576 | tf_op jit(solution)/shard_map/all_to_all | solution.py:25
  121.7 0.9 copy.26
  122.6 0.8 copy.25
  123.4 9.7 %all-to-all-done.3 = bf16[16,128,128]{1,2,0:T(8,128)(2,1)S(1)} async-done(((bf16[16,128,128]{1,2,0:T(8,128)(2,1)}), bf16[16,128,128]{1,2,0:T(8,128)(2,1)S(1)}, u32[]{:S(2)}, u32[]{:S(2)}) %all-to-all-start.3) | async-done | bytes 524320 | tf_op jit(solution)/shard_map/all_to_all | solution.py:25
  133.2 0.9 copy.28
  134.1 0.8 copy.27
  (3 shorter events, 0.1 us)
Async XLA Ops:
  0.6 1.2 copy-start.3
  2.8 9.5 %copy-start.4 = (bf16[128,1024]{1,0:T(8,128)(2,1)S(1)}, bf16[128,1024]{1,0:T(8,128)(2,1)}, u32[]{:S(2)}) copy-start(bf16[128,1024]{1,0:T(8,128)(2,1)} %param.5) | copy-start | bytes 786436
  2.8 24.6 %all-to-all-start.1 = ((bf16[128,16,128]{0,2,1:T(8,128)(2,1)}), bf16[128,16,128]{0,2,1:T(8,128)(2,1)S(1)}, u32[]{:S(2)}, u32[]{:S(2)}) async-start(bf16[128,16,128]{0,2,1:T(8,128)(2,1)} %pad_maximum_fusion.1), calls=%async_computation.1 | async-start | bytes 1048576 | tf_op jit(solution)/shard_map/all_to_all | solution.py:18
  12.3 1.0 copy-start.5
  27.4 21.6 %all-to-all-start = ((bf16[128,16,128]{0,2,1:T(8,128)(2,1)}), bf16[128,16,128]{0,2,1:T(8,128)(2,1)S(1)}, u32[]{:S(2)}, u32[]{:S(2)}) async-start(bf16[128,16,128]{0,2,1:T(8,128)(2,1)} %pad_maximum_fusion), calls=%async_computation | async-start | bytes 1048576 | tf_op jit(solution)/shard_map/all_to_all | solution.py:18
  33.2 16.7 %copy-start = (bf16[16,128,1,128]{3,1,0,2:T(8,128)(2,1)}, bf16[16,128,1,128]{3,1,0,2:T(8,128)(2,1)S(1)}, u32[]{:S(2)}) copy-start(bf16[16,128,1,128]{3,1,0,2:T(8,128)(2,1)S(1)} %copy.22) | copy-start | bytes 1572868
  33.3 28.0 %collective-permute-start.1 = (bf16[4,512,128]{2,1,0:T(8,128)(2,1)S(1)}, bf16[4,512,128]{2,1,0:T(8,128)(2,1)S(1)}, u32[]{:S(2)}, u32[]{:S(2)}) collective-permute-start(bf16[4,512,128]{2,1,0:T(8,128)(2,1)S(1)} %bitcast.28), channel_id=1, source_target_pairs={{0,496},{16,32},{32,16},{48,64},{64,48},{80,96},{96,80},{112,128},... | collective-permute-start | bytes 1572872 | tf_op jit(solution)/shard_map/ppermute | solution.py:187
  44.2 17.1 %collective-permute-start = (bf16[4,512,128]{2,1,0:T(8,128)(2,1)S(1)}, bf16[4,512,128]{2,1,0:T(8,128)(2,1)S(1)}, u32[]{:S(2)}, u32[]{:S(2)}) collective-permute-start(bf16[4,512,128]{2,1,0:T(8,128)(2,1)S(1)} %bitcast.29), channel_id=1, source_target_pairs={{0,16},{16,0},{32,48},{48,32},{64,80},{80,64},{96,112},{112,96},{1... | collective-permute-start | bytes 1572872 | tf_op jit(solution)/shard_map/ppermute | solution.py:186
  46.1 0.7 copy-start.6
  61.3 0.8 copy-start.1
  61.3 1.0 copy-start.2
  81.6 7.6 %copy-start.8 = (bf16[4,512,128]{2,1,0:T(8,128)(2,1)S(1)}, bf16[4,512,128]{2,1,0:T(8,128)(2,1)}, u32[]{:S(2)}) copy-start(bf16[4,512,128]{2,1,0:T(8,128)(2,1)} %get-tuple-element.14) | copy-start | bytes 1572868
  81.6 9.5 %copy-start.7 = (bf16[4,512,128]{2,1,0:T(8,128)(2,1)S(1)}, bf16[4,512,128]{2,1,0:T(8,128)(2,1)}, u32[]{:S(2)}) copy-start(bf16[4,512,128]{2,1,0:T(8,128)(2,1)} %get-tuple-element.15) | copy-start | bytes 1572868
  81.6 33.4 %all-to-all-start.2 = ((bf16[16,128,128]{1,2,0:T(8,128)(2,1)}), bf16[16,128,128]{1,2,0:T(8,128)(2,1)S(1)}, u32[]{:S(2)}, u32[]{:S(2)}) async-start(bf16[16,128,128]{1,2,0:T(8,128)(2,1)} %copy.23), calls=%async_computation.2 | async-start | bytes 1048576 | tf_op jit(solution)/shard_map/all_to_all | solution.py:25
  89.2 11.1 %collective-permute-start.2 = (bf16[4,512,128]{2,1,0:T(8,128)(2,1)S(1)}, bf16[4,512,128]{2,1,0:T(8,128)(2,1)S(1)}, u32[]{:S(2)}, u32[]{:S(2)}) collective-permute-start(bf16[4,512,128]{2,1,0:T(8,128)(2,1)S(1)} %copy-done.8), channel_id=1, source_target_pairs={{0,16},{16,0},{32,48},{48,32},{64,80},{80,64},{96,112},{112,96},{1... | collective-permute-start | bytes 1572872 | tf_op jit(solution)/shard_map/ppermute | solution.py:196
  91.2 21.4 %collective-permute-start.3 = (bf16[4,512,128]{2,1,0:T(8,128)(2,1)S(1)}, bf16[4,512,128]{2,1,0:T(8,128)(2,1)S(1)}, u32[]{:S(2)}, u32[]{:S(2)}) collective-permute-start(bf16[4,512,128]{2,1,0:T(8,128)(2,1)S(1)} %copy-done.7), channel_id=1, source_target_pairs={{0,496},{16,32},{32,16},{48,64},{64,48},{80,96},{96,80},{112,128},... | collective-permute-start | bytes 1572872 | tf_op jit(solution)/shard_map/ppermute | solution.py:197
  115.0 18.2 %all-to-all-start.3 = ((bf16[16,128,128]{1,2,0:T(8,128)(2,1)}), bf16[16,128,128]{1,2,0:T(8,128)(2,1)S(1)}, u32[]{:S(2)}, u32[]{:S(2)}) async-start(bf16[16,128,128]{1,2,0:T(8,128)(2,1)} %copy.24), calls=%async_computation.3 | async-start | bytes 1048576 | tf_op jit(solution)/shard_map/all_to_all | solution.py:25

commit v9 on v7

--- a/solution.py
+++ b/solution.py
@@ -82,7 +82,10 @@
         (w * (nt(grad_ext, pair) - row_delta)).astype(jnp.bfloat16) for w, pair in zip(weights, pairs)
     ]
     query_grad = (sum(nn(d, pair) for d, pair in zip(score_grads, pairs)) * scale).astype(jnp.bfloat16)
-    out_ref[0] = jnp.where(low, query_grad, attended)
+    out_rows = jnp.where(low, query_grad.astype(f32), attended.astype(f32))
+    chunk = out_ref.shape[1]
+    for j in range(out_ref.shape[0]):
+        out_ref[j] = jnp.transpose(out_rows[j * chunk : (j + 1) * chunk]).astype(jnp.bfloat16)
     highest_ref[0] = highest
     inverse_ref[0] = inverse
     delta_ref[0] = row_delta
@@ -147,6 +150,8 @@
     one_spec = pl.BlockSpec((1, block, width), lambda n, p: (n, 0, 0))
     whole_spec = pl.BlockSpec((block_count, block, width), lambda n, p: (0, 0, 0))
     stat_spec = pl.BlockSpec((1, block, 1), lambda n, p: (n, 0, 0))
+    chunks = block // width
+    chunk_spec = pl.BlockSpec((chunks, width, width), lambda n, p: (n, 0, 0))
     shape = (block_count, block, width)
     stat = jax.ShapeDtypeStruct((block_count, block, 1), jnp.float32)
     return pl.pallas_call(
@@ -155,11 +160,11 @@
             num_scalar_prefetch=1,
             grid=(block_count,),
             in_specs=[one_spec, one_spec, left_spec, right_spec],
-            out_specs=[one_spec, stat_spec, stat_spec, stat_spec, whole_spec, whole_spec],
+            out_specs=[chunk_spec, stat_spec, stat_spec, stat_spec, whole_spec, whole_spec],
             scratch_shapes=[pltpu.VMEM(shape, jnp.float32), pltpu.VMEM(shape, jnp.float32)],
         ),
         out_shape=[
-            jax.ShapeDtypeStruct(shape, jnp.bfloat16),
+            jax.ShapeDtypeStruct((block_count * chunks, width, width), jnp.bfloat16),
             stat,
             stat,
             stat,
@@ -192,7 +197,7 @@
     from_near = lax.ppermute(to_near, "blk", near_pairs).astype(jnp.float32)
     from_far = lax.ppermute(to_far, "blk", far_pairs).astype(jnp.float32)
     own_grads = own_grads_of(qd, kv, highest, inverse, delta)
-    query_grad, attended = to_rows(out_pair.reshape(row_count, width))
+    query_grad, attended = to_rows(out_pair.transpose(0, 2, 1).reshape(row_count, width))
     kv_grads = (own_grads + from_near + from_far).astype(jnp.bfloat16)
     key_grad, value_grad = to_rows(kv_grads.reshape(row_count, width))
     return (attended, query_grad, key_grad, value_grad)

time: 135 us -> 133 us (0.985)
  local copies, waits for them, and re-layouts: 11.9 us -> 9.87 us
    all_to_all x2 -> x1, local copies, waits for them, and re-layouts: 3.06 us -> 1.02 us  [to_rows(): lax.all_to_all(packed, 'head', split_axis=0, concat_axis=1, tiled=True)]
  transfers between devices with their start and end apart: 8 -> 8, of which waited for: 5 -> 5; matrix products, arithmetic and copies ran while one was open for 5% -> 6% of each run, Pallas kernels for 4% -> 4%
where the time goes in v9:
time: 133 us; the launch traced here: 132 us
  waiting for transfers between devices  47.8 us (36%)
  starting transfers between devices  47.5 us (36%)
  Pallas kernels  22.7 us (17%)
  local copies, waits for them, and re-layouts  9.87 us (7%)
  other arithmetic  3.74 us (3%)
    pallas_call x1, Pallas kernels, attention(): pl.pallas_call(attention_kernel, grid_spec=pltpu.PrefetchScalarGridSpec(n...  16.8 us
    all_to_all x2, starting transfers between devices, to_heads(): lax.all_to_all(packed, 'head', split_axis=1, concat_axis=0, tiled=True)  15.1 us
    all_to_all x2, waiting for transfers between devices, to_heads(): lax.all_to_all(packed, 'head', split_axis=1, concat_axis=0, tiled=True)  14.6 us
    all_to_all x2, starting transfers between devices, to_rows(): lax.all_to_all(packed, 'head', split_axis=0, concat_axis=1, tiled=True)  14.3 us
    ppermute x1, waiting for transfers between devices, shards(): from_far = lax.ppermute(to_far, 'blk', far_pairs).astype(jnp.float32)  12.2 us
    ppermute x1, waiting for transfers between devices, shards(): far = lax.ppermute(kv, 'blk', far_pairs)  11.3 us
    ppermute x1, starting transfers between devices, shards(): far = lax.ppermute(kv, 'blk', far_pairs)  10.9 us
    all_to_all x2, waiting for transfers between devices, to_rows(): lax.all_to_all(packed, 'head', split_axis=0, concat_axis=1, tiled=True)  9.75 us
  transfers between devices with their start and end apart: 8, of which 5 were waited for; matrix products, arithmetic and copies ran while one was open for 6% of the time, Pallas kernels for 4%

profile of v9, /device:TPU:8, one launch (start us, length us, event | category | flops | bytes accessed | tf_op | source)
XLA Modules:
  0.0 132.4 jit_solution(4388427812833520326)
XLA Ops:
  0.6 0.0 copy-start.3
  0.6 1.2 copy.20
  1.8 0.0 copy-done.3
  1.8 0.2 copy.21
  2.0 0.8 pad_maximum_fusion.1
  2.8 0.0 copy-start.4
  2.8 9.5 %all-to-all-start.1 = ((bf16[128,16,128]{0,2,1:T(8,128)(2,1)}), bf16[128,16,128]{0,2,1:T(8,128)(2,1)S(1)}, u32[]{:S(2)}, u32[]{:S(2)}) async-start(bf16[128,16,128]{0,2,1:T(8,128)(2,1)} %pad_maximum_fusion.1), calls=%async_computation.1 | async-start | bytes 1048576 | tf_op jit(solution)/shard_map/all_to_all | solution.py:18
  12.3 0.0 copy-done.4
  12.3 0.0 copy-start.5
  12.4 0.2 copy.17
  12.5 0.8 copy-done.5
  13.3 0.2 copy.18
  13.5 0.8 pad_maximum_fusion
  14.3 13.1 %all-to-all-done.1 = bf16[128,16,128]{0,2,1:T(8,128)(2,1)S(1)} async-done(((bf16[128,16,128]{0,2,1:T(8,128)(2,1)}), bf16[128,16,128]{0,2,1:T(8,128)(2,1)S(1)}, u32[]{:S(2)}, u32[]{:S(2)}) %all-to-all-start.1) | async-done | bytes 524320 | tf_op jit(solution)/shard_map/all_to_all | solution.py:18
  27.4 5.6 %all-to-all-start = ((bf16[128,16,128]{0,2,1:T(8,128)(2,1)}), bf16[128,16,128]{0,2,1:T(8,128)(2,1)S(1)}, u32[]{:S(2)}, u32[]{:S(2)}) async-start(bf16[128,16,128]{0,2,1:T(8,128)(2,1)} %pad_maximum_fusion), calls=%async_computation | async-start | bytes 1048576 | tf_op jit(solution)/shard_map/all_to_all | solution.py:18
  33.0 0.3 copy.22
  33.2 0.0 copy-start
  33.3 10.9 %collective-permute-start.1 = (bf16[4,512,128]{2,1,0:T(8,128)(2,1)S(1)}, bf16[4,512,128]{2,1,0:T(8,128)(2,1)S(1)}, u32[]{:S(2)}, u32[]{:S(2)}) collective-permute-start(bf16[4,512,128]{2,1,0:T(8,128)(2,1)S(1)} %bitcast.32), channel_id=1, source_target_pairs={{0,496},{16,32},{32,16},{48,64},{64,48},{80,96},{96,80},{112,128},... | collective-permute-start | bytes 1572872 | tf_op jit(solution)/shard_map/ppermute | solution.py:188
  44.2 1.9 %collective-permute-start = (bf16[4,512,128]{2,1,0:T(8,128)(2,1)S(1)}, bf16[4,512,128]{2,1,0:T(8,128)(2,1)S(1)}, u32[]{:S(2)}, u32[]{:S(2)}) collective-permute-start(bf16[4,512,128]{2,1,0:T(8,128)(2,1)S(1)} %bitcast.33), channel_id=1, source_target_pairs={{0,16},{16,0},{32,48},{48,32},{64,80},{80,64},{96,112},{112,96},{1... | collective-permute-start | bytes 1572872 | tf_op jit(solution)/shard_map/ppermute | solution.py:187
  46.1 0.0 copy-start.6
  46.1 0.7 copy-done.6
  46.8 0.1 fusion
  46.9 0.6 add_clamp_fusion.picks_ref
  47.5 1.5 %all-to-all-done = bf16[128,16,128]{0,2,1:T(8,128)(2,1)S(1)} async-done(((bf16[128,16,128]{0,2,1:T(8,128)(2,1)}), bf16[128,16,128]{0,2,1:T(8,128)(2,1)S(1)}, u32[]{:S(2)}, u32[]{:S(2)}) %all-to-all-start) | async-done | bytes 524320 | tf_op jit(solution)/shard_map/all_to_all | solution.py:18
  49.0 1.0 copy.19
  50.0 0.0 copy-done
  50.0 11.3 %collective-permute-done.1.right_ref = bf16[4,512,128]{2,1,0:T(8,128)(2,1)S(1)} collective-permute-done((bf16[4,512,128]{2,1,0:T(8,128)(2,1)S(1)}, bf16[4,512,128]{2,1,0:T(8,128)(2,1)S(1)}, u32[]{:S(2)}, u32[]{:S(2)}) %collective-permute-start.1) | collective-permute-done | bytes 524320 | tf_op jit(solution)/shard_map/ppermute | solution.py:188
  61.3 0.0 copy-start.1
  61.3 0.0 collective-permute-done.left_ref
  61.3 0.0 copy-start.2
  61.3 0.8 copy-done.1
  62.0 0.2 copy-done.2
  62.2 16.8 %shard_map.84 = (bf16[16,128,128]{2,1,0:T(8,128)(2,1)}, f32[4,512,1]{2,1,0:T(8,128)}, f32[4,512,1]{2,1,0:T(8,128)}, f32[4,512,1]{2,1,0:T(8,128)}, bf16[4,512,128...) custom-call(s32[2,4]{1,0:T(2,128)} %add_clamp_fusion.picks_ref, bf16[4,512,128]{2,1,0:T(8,128)(2,1)} %bitcast.36, ...), custom_call_target="tpu_custom_call" | custom-call | tf_op jit(solution)/shard_map/pallas_call | solution.py:157
  79.1 0.0 copy-start.8
  79.1 0.0 copy-start.7
  79.1 7.6 %all-to-all-start.2 = ((bf16[16,128,128]{1,2,0:T(8,128)(2,1)}), bf16[16,128,128]{1,2,0:T(8,128)(2,1)S(1)}, u32[]{:S(2)}, u32[]{:S(2)}) async-start(bf16[16,128,128]{1,2,0:T(8,128)(2,1)} %bitcast.51), calls=%async_computation.2 | async-start | bytes 1048576 | tf_op jit(solution)/shard_map/all_to_all | solution.py:25
  86.7 0.0 copy-done.8
  86.7 1.9 %collective-permute-start.2 = (bf16[4,512,128]{2,1,0:T(8,128)(2,1)S(1)}, bf16[4,512,128]{2,1,0:T(8,128)(2,1)S(1)}, u32[]{:S(2)}, u32[]{:S(2)}) collective-permute-start(bf16[4,512,128]{2,1,0:T(8,128)(2,1)S(1)} %copy-done.8), channel_id=1, source_target_pairs={{0,16},{16,0},{32,48},{48,32},{64,80},{80,64},{96,112},{112,96},{1... | collective-permute-start | bytes 1572872 | tf_op jit(solution)/shard_map/ppermute | solution.py:197
  88.6 0.0 copy-done.7
  88.6 3.3 %collective-permute-start.3 = (bf16[4,512,128]{2,1,0:T(8,128)(2,1)S(1)}, bf16[4,512,128]{2,1,0:T(8,128)(2,1)S(1)}, u32[]{:S(2)}, u32[]{:S(2)}) collective-permute-start(bf16[4,512,128]{2,1,0:T(8,128)(2,1)S(1)} %copy-done.7), channel_id=1, source_target_pairs={{0,496},{16,32},{32,16},{48,64},{64,48},{80,96},{96,80},{112,128},... | collective-permute-start | bytes 1572872 | tf_op jit(solution)/shard_map/ppermute | solution.py:198
  91.9 5.9 %shard_map.85 = f32[4,512,128]{2,1,0:T(8,128)} custom-call(bf16[4,512,128]{2,1,0:T(8,128)(2,1)} %bitcast.37, bf16[4,512,128]{2,1,0:T(8,128)(2,1)} %bitcast.35, f32[4,512,1]{2,1,0:T(8,128)} %get-tuple-element.11.highest_ref, f32[4,512,1]{2,1,0:T(8,128)} %get-tuple-element.12.inverse_ref, f32[4,512,1]{2,1,0:T(8,128)} %get-tuple-element.13.delta_ref), custom_call_target="tpu_custom_call" | custom-call | tf_op jit(solution)/shard_map/pallas_call | solution.py:135
  97.8 0.0 collective-permute-done.2
  97.8 12.2 %collective-permute-done.3 = bf16[4,512,128]{2,1,0:T(8,128)(2,1)S(1)} collective-permute-done((bf16[4,512,128]{2,1,0:T(8,128)(2,1)S(1)}, bf16[4,512,128]{2,1,0:T(8,128)(2,1)S(1)}, u32[]{:S(2)}, u32[]{:S(2)}) %collective-permute-start.3) | collective-permute-done | bytes 524320 | tf_op jit(solution)/shard_map/ppermute | solution.py:198
  110.0 1.4 %add_convert_fusion = bf16[4,512,128]{2,1,0:T(8,128)(2,1)S(1)} fusion(bf16[4,512,128]{2,1,0:T(8,128)(2,1)S(1)} %collective-permute-done.3, f32[4,512,128]{2,1,0:T(8,128)} %shard_map.85, bf16[4,512,128]{2,1,0:T(8,128)(2,1)S(1)} %collective-permute-done.2), kind=kLoop, calls=%fused_computation | loop fusion | flops 1310720 | bytes 2621440 | tf_op jit(solution)/shard_map/convert_element_type | solution.py:201
  111.4 1.0 copy.25
  112.4 0.0 all-to-all-done.2
  112.5 6.7 %all-to-all-start.3 = ((bf16[16,128,128]{1,2,0:T(8,128)(2,1)}), bf16[16,128,128]{1,2,0:T(8,128)(2,1)S(1)}, u32[]{:S(2)}, u32[]{:S(2)}) async-start(bf16[16,128,128]{1,2,0:T(8,128)(2,1)} %copy.25), calls=%async_computation.3 | async-start | bytes 1048576 | tf_op jit(solution)/shard_map/all_to_all | solution.py:25
  119.2 0.9 copy.27
  120.1 0.8 copy.26
  120.9 9.7 %all-to-all-done.3 = bf16[16,128,128]{1,2,0:T(8,128)(2,1)S(1)} async-done(((bf16[16,128,128]{1,2,0:T(8,128)(2,1)}), bf16[16,128,128]{1,2,0:T(8,128)(2,1)S(1)}, u32[]{:S(2)}, u32[]{:S(2)}) %all-to-all-start.3) | async-done | bytes 524320 | tf_op jit(solution)/shard_map/all_to_all | solution.py:25
  130.7 0.9 copy.29
  131.5 0.8 copy.28
  (3 shorter events, 0.1 us)
Async XLA Ops:
  0.6 1.2 copy-start.3
  2.8 9.5 %copy-start.4 = (bf16[128,1024]{1,0:T(8,128)(2,1)S(1)}, bf16[128,1024]{1,0:T(8,128)(2,1)}, u32[]{:S(2)}) copy-start(bf16[128,1024]{1,0:T(8,128)(2,1)} %param.5) | copy-start | bytes 786436
  2.8 24.6 %all-to-all-start.1 = ((bf16[128,16,128]{0,2,1:T(8,128)(2,1)}), bf16[128,16,128]{0,2,1:T(8,128)(2,1)S(1)}, u32[]{:S(2)}, u32[]{:S(2)}) async-start(bf16[128,16,128]{0,2,1:T(8,128)(2,1)} %pad_maximum_fusion.1), calls=%async_computation.1 | async-start | bytes 1048576 | tf_op jit(solution)/shard_map/all_to_all | solution.py:18
  12.3 1.0 copy-start.5
  27.4 21.6 %all-to-all-start = ((bf16[128,16,128]{0,2,1:T(8,128)(2,1)}), bf16[128,16,128]{0,2,1:T(8,128)(2,1)S(1)}, u32[]{:S(2)}, u32[]{:S(2)}) async-start(bf16[128,16,128]{0,2,1:T(8,128)(2,1)} %pad_maximum_fusion), calls=%async_computation | async-start | bytes 1048576 | tf_op jit(solution)/shard_map/all_to_all | solution.py:18
  33.2 16.7 %copy-start = (bf16[16,128,1,128]{3,1,0,2:T(8,128)(2,1)}, bf16[16,128,1,128]{3,1,0,2:T(8,128)(2,1)S(1)}, u32[]{:S(2)}) copy-start(bf16[16,128,1,128]{3,1,0,2:T(8,128)(2,1)S(1)} %copy.22) | copy-start | bytes 1572868
  33.3 28.0 %collective-permute-start.1 = (bf16[4,512,128]{2,1,0:T(8,128)(2,1)S(1)}, bf16[4,512,128]{2,1,0:T(8,128)(2,1)S(1)}, u32[]{:S(2)}, u32[]{:S(2)}) collective-permute-start(bf16[4,512,128]{2,1,0:T(8,128)(2,1)S(1)} %bitcast.32), channel_id=1, source_target_pairs={{0,496},{16,32},{32,16},{48,64},{64,48},{80,96},{96,80},{112,128},... | collective-permute-start | bytes 1572872 | tf_op jit(solution)/shard_map/ppermute | solution.py:188
  44.2 17.1 %collective-permute-start = (bf16[4,512,128]{2,1,0:T(8,128)(2,1)S(1)}, bf16[4,512,128]{2,1,0:T(8,128)(2,1)S(1)}, u32[]{:S(2)}, u32[]{:S(2)}) collective-permute-start(bf16[4,512,128]{2,1,0:T(8,128)(2,1)S(1)} %bitcast.33), channel_id=1, source_target_pairs={{0,16},{16,0},{32,48},{48,32},{64,80},{80,64},{96,112},{112,96},{1... | collective-permute-start | bytes 1572872 | tf_op jit(solution)/shard_map/ppermute | solution.py:187
  46.1 0.7 copy-start.6
  61.3 0.8 copy-start.1
  61.3 1.0 copy-start.2
  79.1 7.6 %copy-start.8 = (bf16[4,512,128]{2,1,0:T(8,128)(2,1)S(1)}, bf16[4,512,128]{2,1,0:T(8,128)(2,1)}, u32[]{:S(2)}) copy-start(bf16[4,512,128]{2,1,0:T(8,128)(2,1)} %get-tuple-element.14) | copy-start | bytes 1572868
  79.1 9.6 %copy-start.7 = (bf16[4,512,128]{2,1,0:T(8,128)(2,1)S(1)}, bf16[4,512,128]{2,1,0:T(8,128)(2,1)}, u32[]{:S(2)}) copy-start(bf16[4,512,128]{2,1,0:T(8,128)(2,1)} %get-tuple-element.15) | copy-start | bytes 1572868
  79.1 33.4 %all-to-all-start.2 = ((bf16[16,128,128]{1,2,0:T(8,128)(2,1)}), bf16[16,128,128]{1,2,0:T(8,128)(2,1)S(1)}, u32[]{:S(2)}, u32[]{:S(2)}) async-start(bf16[16,128,128]{1,2,0:T(8,128)(2,1)} %bitcast.51), calls=%async_computation.2 | async-start | bytes 1048576 | tf_op jit(solution)/shard_map/all_to_all | solution.py:25
  86.7 11.1 %collective-permute-start.2 = (bf16[4,512,128]{2,1,0:T(8,128)(2,1)S(1)}, bf16[4,512,128]{2,1,0:T(8,128)(2,1)S(1)}, u32[]{:S(2)}, u32[]{:S(2)}) collective-permute-start(bf16[4,512,128]{2,1,0:T(8,128)(2,1)S(1)} %copy-done.8), channel_id=1, source_target_pairs={{0,16},{16,0},{32,48},{48,32},{64,80},{80,64},{96,112},{112,96},{1... | collective-permute-start | bytes 1572872 | tf_op jit(solution)/shard_map/ppermute | solution.py:197
  88.6 21.4 %collective-permute-start.3 = (bf16[4,512,128]{2,1,0:T(8,128)(2,1)S(1)}, bf16[4,512,128]{2,1,0:T(8,128)(2,1)S(1)}, u32[]{:S(2)}, u32[]{:S(2)}) collective-permute-start(bf16[4,512,128]{2,1,0:T(8,128)(2,1)S(1)} %copy-done.7), channel_id=1, source_target_pairs={{0,496},{16,32},{32,16},{48,64},{64,48},{80,96},{96,80},{112,128},... | collective-permute-start | bytes 1572872 | tf_op jit(solution)/shard_map/ppermute | solution.py:198
  112.5 18.2 %all-to-all-start.3 = ((bf16[16,128,128]{1,2,0:T(8,128)(2,1)}), bf16[16,128,128]{1,2,0:T(8,128)(2,1)S(1)}, u32[]{:S(2)}, u32[]{:S(2)}) async-start(bf16[16,128,128]{1,2,0:T(8,128)(2,1)} %copy.25), calls=%async_computation.3 | async-start | bytes 1048576 | tf_op jit(solution)/shard_map/all_to_all | solution.py:25

commit v10 on v9

--- a/solution.py
+++ b/solution.py
@@ -143,6 +143,28 @@
     )(qd, kv, highest, inverse, delta)
 
 
+def sum_kernel(own_ref, near_ref, far_ref, out_ref):
+    total = own_ref[0] + near_ref[0].astype(jnp.float32) + far_ref[0].astype(jnp.float32)
+    chunk = out_ref.shape[1]
+    for j in range(out_ref.shape[0]):
+        out_ref[j] = jnp.transpose(total[j * chunk : (j + 1) * chunk]).astype(jnp.bfloat16)
+
+
+def summed(own, near, far):
+    block_count, block, width = own.shape
+    chunks = block // width
+    one_spec = pl.BlockSpec((1, block, width), lambda n: (n, 0, 0))
+    return pl.pallas_call(
+        sum_kernel,
+        grid=(block_count,),
+        in_specs=[one_spec, one_spec, one_spec],
+        out_specs=pl.BlockSpec((chunks, width, width), lambda n: (n, 0, 0)),
+        out_shape=jax.ShapeDtypeStruct((block_count * chunks, width, width), jnp.bfloat16),
+        compiler_params=pltpu.CompilerParams(dimension_semantics=("arbitrary",)),
+        interpret=INTERPRET,
+    )(own, near, far)
+
+
 def attention(picks, qd, kv, left, right):
     block_count, block, width = kv.shape
     left_spec = pl.BlockSpec((1, block, width), lambda n, p: (p[0, n], 0, 0))
@@ -194,12 +216,12 @@
     picks = jnp.stack([jnp.where(even, picks[1], picks[0]), jnp.where(even, picks[0], picks[1])])
     picks = jnp.clip(picks, 0, block_count - 1).astype(jnp.int32)
     out_pair, highest, inverse, delta, to_near, to_far = attention(picks, qd, kv, near, far)
-    from_near = lax.ppermute(to_near, "blk", near_pairs).astype(jnp.float32)
-    from_far = lax.ppermute(to_far, "blk", far_pairs).astype(jnp.float32)
+    from_near = lax.ppermute(to_near, "blk", near_pairs)
+    from_far = lax.ppermute(to_far, "blk", far_pairs)
     own_grads = own_grads_of(qd, kv, highest, inverse, delta)
     query_grad, attended = to_rows(out_pair.transpose(0, 2, 1).reshape(row_count, width))
-    kv_grads = (own_grads + from_near + from_far).astype(jnp.bfloat16)
-    key_grad, value_grad = to_rows(kv_grads.reshape(row_count, width))
+    kv_grads = summed(own_grads, from_near, from_far)
+    key_grad, value_grad = to_rows(kv_grads.transpose(0, 2, 1).reshape(row_count, width))
     return (attended, query_grad, key_grad, value_grad)
 
 

time: 133 us -> 135 us (1.015)
  Pallas kernels: 22.7 us -> 26.4 us
  other arithmetic: 3.74 us -> 2.36 us
    pallas_call x0 -> x1, Pallas kernels: none -> 3.63 us  [summed(): pl.pallas_call(sum_kernel, grid=(block_count,), in_specs=[one_spec, one_s...]
    convert_element_type x1 -> x0, other arithmetic: 1.4 us -> none  [shards(): kv_grads = (own_grads + from_near + from_far).astype(jnp.bfloat16)]
    unnamed x26 -> x30, local copies, waits for them, and re-layouts: 7.48 us -> 8.29 us
  transfers between devices with their start and end apart: 8 -> 8, of which waited for: 5 -> 5; matrix products, arithmetic and copies ran while one was open for 6% -> 4% of each run, Pallas kernels for 4% -> 7%
where the time goes in v10:
time: 135 us; the launch traced here: 134 us
  waiting for transfers between devices  47.8 us (35%)
  starting transfers between devices  47.5 us (35%)
  Pallas kernels  26.4 us (20%)
  local copies, waits for them, and re-layouts  9.66 us (7%)
  other arithmetic  2.36 us (2%)
    pallas_call x1, Pallas kernels, attention(): pl.pallas_call(attention_kernel, grid_spec=pltpu.PrefetchScalarGridSpec(n...  16.9 us
    all_to_all x2, starting transfers between devices, to_heads(): lax.all_to_all(packed, 'head', split_axis=1, concat_axis=0, tiled=True)  15.1 us
    all_to_all x2, waiting for transfers between devices, to_heads(): lax.all_to_all(packed, 'head', split_axis=1, concat_axis=0, tiled=True)  14.5 us
    all_to_all x2, starting transfers between devices, to_rows(): lax.all_to_all(packed, 'head', split_axis=0, concat_axis=1, tiled=True)  14.3 us
    ppermute x1, waiting for transfers between devices, shards(): from_far = lax.ppermute(to_far, 'blk', far_pairs)  12.2 us
    ppermute x1, waiting for transfers between devices, shards(): far = lax.ppermute(kv, 'blk', far_pairs)  11.3 us
    ppermute x1, starting transfers between devices, shards(): far = lax.ppermute(kv, 'blk', far_pairs)  10.9 us
    all_to_all x2, waiting for transfers between devices, to_rows(): lax.all_to_all(packed, 'head', split_axis=0, concat_axis=1, tiled=True)  9.75 us
  transfers between devices with their start and end apart: 8, of which 5 were waited for; matrix products, arithmetic and copies ran while one was open for 4% of the time, Pallas kernels for 7%

profile of v10, /device:TPU:8, one launch (start us, length us, event | category | flops | bytes accessed | tf_op | source)
XLA Modules:
  0.0 134.4 jit_solution(1887689015381355935)
XLA Ops:
  0.6 0.0 copy-start.5
  0.6 1.2 copy.20
  1.8 0.0 copy-done.5
  1.8 0.2 copy.21
  2.0 0.8 pad_maximum_fusion.1
  2.8 0.0 copy-start.6
  2.8 9.5 %all-to-all-start.1 = ((bf16[128,16,128]{0,2,1:T(8,128)(2,1)}), bf16[128,16,128]{0,2,1:T(8,128)(2,1)S(1)}, u32[]{:S(2)}, u32[]{:S(2)}) async-start(bf16[128,16,128]{0,2,1:T(8,128)(2,1)} %pad_maximum_fusion.1), calls=%async_computation.1 | async-start | bytes 1048576 | tf_op jit(solution)/shard_map/all_to_all | solution.py:18
  12.3 0.0 copy-done.6
  12.4 0.0 copy-start.7
  12.4 0.2 copy.17
  12.5 0.8 copy-done.7
  13.3 0.2 copy.18
  13.5 0.9 pad_maximum_fusion
  14.3 13.1 %all-to-all-done.1 = bf16[128,16,128]{0,2,1:T(8,128)(2,1)S(1)} async-done(((bf16[128,16,128]{0,2,1:T(8,128)(2,1)}), bf16[128,16,128]{0,2,1:T(8,128)(2,1)S(1)}, u32[]{:S(2)}, u32[]{:S(2)}) %all-to-all-start.1) | async-done | bytes 524320 | tf_op jit(solution)/shard_map/all_to_all | solution.py:18
  27.4 5.6 %all-to-all-start = ((bf16[128,16,128]{0,2,1:T(8,128)(2,1)}), bf16[128,16,128]{0,2,1:T(8,128)(2,1)S(1)}, u32[]{:S(2)}, u32[]{:S(2)}) async-start(bf16[128,16,128]{0,2,1:T(8,128)(2,1)} %pad_maximum_fusion), calls=%async_computation | async-start | bytes 1048576 | tf_op jit(solution)/shard_map/all_to_all | solution.py:18
  33.0 0.3 copy.22
  33.3 0.0 copy-start
  33.3 10.9 %collective-permute-start.1 = (bf16[4,512,128]{2,1,0:T(8,128)(2,1)S(1)}, bf16[4,512,128]{2,1,0:T(8,128)(2,1)S(1)}, u32[]{:S(2)}, u32[]{:S(2)}) collective-permute-start(bf16[4,512,128]{2,1,0:T(8,128)(2,1)S(1)} %bitcast.36), channel_id=1, source_target_pairs={{0,496},{16,32},{32,16},{48,64},{64,48},{80,96},{96,80},{112,128},... | collective-permute-start | bytes 1572872 | tf_op jit(solution)/shard_map/ppermute | solution.py:210
  44.2 1.9 %collective-permute-start = (bf16[4,512,128]{2,1,0:T(8,128)(2,1)S(1)}, bf16[4,512,128]{2,1,0:T(8,128)(2,1)S(1)}, u32[]{:S(2)}, u32[]{:S(2)}) collective-permute-start(bf16[4,512,128]{2,1,0:T(8,128)(2,1)S(1)} %bitcast.37), channel_id=1, source_target_pairs={{0,16},{16,0},{32,48},{48,32},{64,80},{80,64},{96,112},{112,96},{1... | collective-permute-start | bytes 1572872 | tf_op jit(solution)/shard_map/ppermute | solution.py:209
  46.1 0.0 copy-start.8
  46.1 0.7 copy-done.8
  46.8 0.1 fusion
  46.9 0.6 add_clamp_fusion.picks_ref
  47.5 1.5 %all-to-all-done = bf16[128,16,128]{0,2,1:T(8,128)(2,1)S(1)} async-done(((bf16[128,16,128]{0,2,1:T(8,128)(2,1)}), bf16[128,16,128]{0,2,1:T(8,128)(2,1)S(1)}, u32[]{:S(2)}, u32[]{:S(2)}) %all-to-all-start) | async-done | bytes 524320 | tf_op jit(solution)/shard_map/all_to_all | solution.py:18
  49.0 1.0 copy.19
  50.0 0.0 copy-done
  50.0 11.3 %collective-permute-done.1.right_ref = bf16[4,512,128]{2,1,0:T(8,128)(2,1)S(1)} collective-permute-done((bf16[4,512,128]{2,1,0:T(8,128)(2,1)S(1)}, bf16[4,512,128]{2,1,0:T(8,128)(2,1)S(1)}, u32[]{:S(2)}, u32[]{:S(2)}) %collective-permute-start.1) | collective-permute-done | bytes 524320 | tf_op jit(solution)/shard_map/ppermute | solution.py:210
  61.3 0.0 copy-start.3
  61.3 0.0 collective-permute-done.left_ref
  61.3 0.0 copy-start.4
  61.3 0.8 copy-done.3
  62.1 0.2 copy-done.4
  62.2 16.9 %shard_map.84 = (bf16[16,128,128]{2,1,0:T(8,128)(2,1)}, f32[4,512,1]{2,1,0:T(8,128)}, f32[4,512,1]{2,1,0:T(8,128)}, f32[4,512,1]{2,1,0:T(8,128)}, bf16[4,512,128...) custom-call(s32[2,4]{1,0:T(2,128)} %add_clamp_fusion.picks_ref, bf16[4,512,128]{2,1,0:T(8,128)(2,1)} %bitcast.40, ...), custom_call_target="tpu_custom_call" | custom-call | tf_op jit(solution)/shard_map/pallas_call | solution.py:179
  79.1 0.0 copy-start.10
  79.1 0.0 copy-start.9
  79.1 7.6 %all-to-all-start.2 = ((bf16[16,128,128]{1,2,0:T(8,128)(2,1)}), bf16[16,128,128]{1,2,0:T(8,128)(2,1)S(1)}, u32[]{:S(2)}, u32[]{:S(2)}) async-start(bf16[16,128,128]{1,2,0:T(8,128)(2,1)} %bitcast.55), calls=%async_computation.2 | async-start | bytes 1048576 | tf_op jit(solution)/shard_map/all_to_all | solution.py:25
  86.7 0.0 copy-done.10
  86.7 1.9 %collective-permute-start.2 = (bf16[4,512,128]{2,1,0:T(8,128)(2,1)S(1)}, bf16[4,512,128]{2,1,0:T(8,128)(2,1)S(1)}, u32[]{:S(2)}, u32[]{:S(2)}) collective-permute-start(bf16[4,512,128]{2,1,0:T(8,128)(2,1)S(1)} %copy-done.10), channel_id=1, source_target_pairs={{0,16},{16,0},{32,48},{48,32},{64,80},{80,64},{96,112},{112,96},{1... | collective-permute-start | bytes 1572872 | tf_op jit(solution)/shard_map/ppermute | solution.py:219
  88.7 0.0 copy-done.9
  88.7 3.3 %collective-permute-start.3 = (bf16[4,512,128]{2,1,0:T(8,128)(2,1)S(1)}, bf16[4,512,128]{2,1,0:T(8,128)(2,1)S(1)}, u32[]{:S(2)}, u32[]{:S(2)}) collective-permute-start(bf16[4,512,128]{2,1,0:T(8,128)(2,1)S(1)} %copy-done.9), channel_id=1, source_target_pairs={{0,496},{16,32},{32,16},{48,64},{64,48},{80,96},{96,80},{112,128},... | collective-permute-start | bytes 1572872 | tf_op jit(solution)/shard_map/ppermute | solution.py:220
  92.0 5.9 %shard_map.85.own_ref = f32[4,512,128]{2,1,0:T(8,128)} custom-call(bf16[4,512,128]{2,1,0:T(8,128)(2,1)} %bitcast.41, bf16[4,512,128]{2,1,0:T(8,128)(2,1)} %bitcast.39, f32[4,512,1]{2,1,0:T(8,128)} %get-tuple-element.11.highest_ref, f32[4,512,1]{2,1,0:T(8,128)} %get-tuple-element.12.inverse_ref, f32[4,512,1]{2,1,0:T(8,128)} %get-tuple-element.13.delta_ref), custom_call_target="tpu_custom_call" | custom-call | tf_op jit(solution)/shard_map/pallas_call | solution.py:135
  97.9 0.0 collective-permute-done.2.near_ref
  97.9 0.0 copy-start.1
  97.9 12.2 %collective-permute-done.3.far_ref = bf16[4,512,128]{2,1,0:T(8,128)(2,1)S(1)} collective-permute-done((bf16[4,512,128]{2,1,0:T(8,128)(2,1)S(1)}, bf16[4,512,128]{2,1,0:T(8,128)(2,1)S(1)}, u32[]{:S(2)}, u32[]{:S(2)}) %collective-permute-start.3) | collective-permute-done | bytes 524320 | tf_op jit(solution)/shard_map/ppermute | solution.py:220
  110.1 0.0 copy-done.1
  110.1 0.0 copy-start.2
  110.1 0.8 copy-done.2
  110.9 3.6 %shard_map.86 = bf16[16,128,128]{2,1,0:T(8,128)(2,1)} custom-call(f32[4,512,128]{2,1,0:T(8,128)} %shard_map.85.own_ref, bf16[4,512,128]{2,1,0:T(8,128)(2,1)} %copy-done.1, bf16[4,512,128]{2,1,0:T(8,128)(2,1)} %copy-done.2), custom_call_target="tpu_custom_call" | custom-call | tf_op jit(solution)/shard_map/pallas_call | solution.py:157
  114.5 0.0 all-to-all-done.2
  114.5 6.7 %all-to-all-start.3 = ((bf16[16,128,128]{1,2,0:T(8,128)(2,1)}), bf16[16,128,128]{1,2,0:T(8,128)(2,1)S(1)}, u32[]{:S(2)}, u32[]{:S(2)}) async-start(bf16[16,128,128]{1,2,0:T(8,128)(2,1)} %bitcast.42), calls=%async_computation.3 | async-start | bytes 1048576 | tf_op jit(solution)/shard_map/all_to_all | solution.py:25
  121.2 0.9 copy.28
  122.1 0.8 copy.27
  122.9 9.7 %all-to-all-done.3 = bf16[16,128,128]{1,2,0:T(8,128)(2,1)S(1)} async-done(((bf16[16,128,128]{1,2,0:T(8,128)(2,1)}), bf16[16,128,128]{1,2,0:T(8,128)(2,1)S(1)}, u32[]{:S(2)}, u32[]{:S(2)}) %all-to-all-start.3) | async-done | bytes 524320 | tf_op jit(solution)/shard_map/all_to_all | solution.py:25
  132.7 0.9 copy.30
  133.6 0.8 copy.29
  (3 shorter events, 0.1 us)
Async XLA Ops:
  0.6 1.2 copy-start.5
  2.8 9.5 %copy-start.6 = (bf16[128,1024]{1,0:T(8,128)(2,1)S(1)}, bf16[128,1024]{1,0:T(8,128)(2,1)}, u32[]{:S(2)}) copy-start(bf16[128,1024]{1,0:T(8,128)(2,1)} %param.5) | copy-start | bytes 786436
  2.8 24.6 %all-to-all-start.1 = ((bf16[128,16,128]{0,2,1:T(8,128)(2,1)}), bf16[128,16,128]{0,2,1:T(8,128)(2,1)S(1)}, u32[]{:S(2)}, u32[]{:S(2)}) async-start(bf16[128,16,128]{0,2,1:T(8,128)(2,1)} %pad_maximum_fusion.1), calls=%async_computation.1 | async-start | bytes 1048576 | tf_op jit(solution)/shard_map/all_to_all | solution.py:18
  12.4 1.0 copy-start.7
  27.4 21.6 %all-to-all-start = ((bf16[128,16,128]{0,2,1:T(8,128)(2,1)}), bf16[128,16,128]{0,2,1:T(8,128)(2,1)S(1)}, u32[]{:S(2)}, u32[]{:S(2)}) async-start(bf16[128,16,128]{0,2,1:T(8,128)(2,1)} %pad_maximum_fusion), calls=%async_computation | async-start | bytes 1048576 | tf_op jit(solution)/shard_map/all_to_all | solution.py:18
  33.3 16.7 %copy-start = (bf16[16,128,1,128]{3,1,0,2:T(8,128)(2,1)}, bf16[16,128,1,128]{3,1,0,2:T(8,128)(2,1)S(1)}, u32[]{:S(2)}) copy-start(bf16[16,128,1,128]{3,1,0,2:T(8,128)(2,1)S(1)} %copy.22) | copy-start | bytes 1572868
  33.3 28.0 %collective-permute-start.1 = (bf16[4,512,128]{2,1,0:T(8,128)(2,1)S(1)}, bf16[4,512,128]{2,1,0:T(8,128)(2,1)S(1)}, u32[]{:S(2)}, u32[]{:S(2)}) collective-permute-start(bf16[4,512,128]{2,1,0:T(8,128)(2,1)S(1)} %bitcast.36), channel_id=1, source_target_pairs={{0,496},{16,32},{32,16},{48,64},{64,48},{80,96},{96,80},{112,128},... | collective-permute-start | bytes 1572872 | tf_op jit(solution)/shard_map/ppermute | solution.py:210
  44.2 17.1 %collective-permute-start = (bf16[4,512,128]{2,1,0:T(8,128)(2,1)S(1)}, bf16[4,512,128]{2,1,0:T(8,128)(2,1)S(1)}, u32[]{:S(2)}, u32[]{:S(2)}) collective-permute-start(bf16[4,512,128]{2,1,0:T(8,128)(2,1)S(1)} %bitcast.37), channel_id=1, source_target_pairs={{0,16},{16,0},{32,48},{48,32},{64,80},{80,64},{96,112},{112,96},{1... | collective-permute-start | bytes 1572872 | tf_op jit(solution)/shard_map/ppermute | solution.py:209
  46.1 0.7 copy-start.8
  61.3 0.8 copy-start.3
  61.3 1.0 copy-start.4
  79.1 7.6 %copy-start.10 = (bf16[4,512,128]{2,1,0:T(8,128)(2,1)S(1)}, bf16[4,512,128]{2,1,0:T(8,128)(2,1)}, u32[]{:S(2)}) copy-start(bf16[4,512,128]{2,1,0:T(8,128)(2,1)} %get-tuple-element.14) | copy-start | bytes 1572868
  79.1 9.6 %copy-start.9 = (bf16[4,512,128]{2,1,0:T(8,128)(2,1)S(1)}, bf16[4,512,128]{2,1,0:T(8,128)(2,1)}, u32[]{:S(2)}) copy-start(bf16[4,512,128]{2,1,0:T(8,128)(2,1)} %get-tuple-element.15) | copy-start | bytes 1572868
  79.1 35.4 %all-to-all-start.2 = ((bf16[16,128,128]{1,2,0:T(8,128)(2,1)}), bf16[16,128,128]{1,2,0:T(8,128)(2,1)S(1)}, u32[]{:S(2)}, u32[]{:S(2)}) async-start(bf16[16,128,128]{1,2,0:T(8,128)(2,1)} %bitcast.55), calls=%async_computation.2 | async-start | bytes 1048576 | tf_op jit(solution)/shard_map/all_to_all | solution.py:25
  86.7 11.1 %collective-permute-start.2 = (bf16[4,512,128]{2,1,0:T(8,128)(2,1)S(1)}, bf16[4,512,128]{2,1,0:T(8,128)(2,1)S(1)}, u32[]{:S(2)}, u32[]{:S(2)}) collective-permute-start(bf16[4,512,128]{2,1,0:T(8,128)(2,1)S(1)} %copy-done.10), channel_id=1, source_target_pairs={{0,16},{16,0},{32,48},{48,32},{64,80},{80,64},{96,112},{112,96},{1... | collective-permute-start | bytes 1572872 | tf_op jit(solution)/shard_map/ppermute | solution.py:219
  88.7 21.4 %collective-permute-start.3 = (bf16[4,512,128]{2,1,0:T(8,128)(2,1)S(1)}, bf16[4,512,128]{2,1,0:T(8,128)(2,1)S(1)}, u32[]{:S(2)}, u32[]{:S(2)}) collective-permute-start(bf16[4,512,128]{2,1,0:T(8,128)(2,1)S(1)} %copy-done.9), channel_id=1, source_target_pairs={{0,496},{16,32},{32,16},{48,64},{64,48},{80,96},{96,80},{112,128},... | collective-permute-start | bytes 1572872 | tf_op jit(solution)/shard_map/ppermute | solution.py:220
  97.9 12.2 %copy-start.1 = (bf16[4,512,128]{2,1,0:T(8,128)(2,1)}, bf16[4,512,128]{2,1,0:T(8,128)(2,1)S(1)}, u32[]{:S(2)}) copy-start(bf16[4,512,128]{2,1,0:T(8,128)(2,1)S(1)} %collective-permute-done.2.near_ref) | copy-start | bytes 1572868
  110.1 0.8 copy-start.2
  114.5 18.2 %all-to-all-start.3 = ((bf16[16,128,128]{1,2,0:T(8,128)(2,1)}), bf16[16,128,128]{1,2,0:T(8,128)(2,1)S(1)}, u32[]{:S(2)}, u32[]{:S(2)}) async-start(bf16[16,128,128]{1,2,0:T(8,128)(2,1)} %bitcast.42), calls=%async_computation.3 | async-start | bytes 1048576 | tf_op jit(solution)/shard_map/all_to_all | solution.py:25

commit v11 on v9

--- a/solution.py
+++ b/solution.py
@@ -35,7 +35,7 @@
 
 def attention_kernel(
     picks_ref, qd_ref, kv_ref, left_ref, right_ref,
-    out_ref, highest_ref, inverse_ref, delta_ref, to_left_ref, to_right_ref, left_acc, right_acc,
+    out_ref, stats_ref, to_left_ref, to_right_ref, left_acc, right_acc,
 ):
     number = pl.program_id(0)
     scale = HEAD_DIM ** (-0.5)
@@ -86,9 +86,7 @@
     chunk = out_ref.shape[1]
     for j in range(out_ref.shape[0]):
         out_ref[j] = jnp.transpose(out_rows[j * chunk : (j + 1) * chunk]).astype(jnp.bfloat16)
-    highest_ref[0] = highest
-    inverse_ref[0] = inverse
-    delta_ref[0] = row_delta
+    stats_ref[0] = jnp.where(lane == 0, highest, jnp.where(lane == 1, inverse, row_delta))
     kv_parts = [None] + [
         jnp.where(low, tn(d, packed) * scale, tn(w, packed))
         for d, w in zip(score_grads[1:], weights_bf[1:])
@@ -104,7 +102,7 @@
         to_right_ref[...] = right_acc[...].astype(jnp.bfloat16)
 
 
-def own_kernel(qd_ref, kv_ref, highest_ref, inverse_ref, delta_ref, own_grad_ref):
+def own_kernel(qd_ref, kv_ref, stats_ref, own_grad_ref):
     scale = HEAD_DIM ** (-0.5)
     f32 = jnp.float32
     packed = qd_ref[0]
@@ -118,9 +116,10 @@
     row = lax.broadcasted_iota(jnp.int32, score.shape, 0)
     col = lax.broadcasted_iota(jnp.int32, score.shape, 1)
     score = jnp.where(col <= row, score, -jnp.inf)
-    weight = jnp.exp(score - highest_ref[0]) * inverse_ref[0]
+    stats = stats_ref[0]
+    weight = jnp.exp(score - stats[:, 0:1]) * stats[:, 1:2]
     weight_grad = lax.dot_general(grad_ext, pair, (((1,), (1,)), ((), ())), preferred_element_type=f32)
-    score_grad = (weight * (weight_grad - delta_ref[0])).astype(jnp.bfloat16)
+    score_grad = (weight * (weight_grad - stats[:, 2:3])).astype(jnp.bfloat16)
     key_part = lax.dot_general(score_grad, packed, (((0,), (0,)), ((), ())), preferred_element_type=f32)
     value_part = lax.dot_general(
         weight.astype(jnp.bfloat16), packed, (((0,), (0,)), ((), ())), preferred_element_type=f32
@@ -128,19 +127,18 @@
     own_grad_ref[0] = jnp.where(low, key_part * scale, value_part)
 
 
-def own_grads_of(qd, kv, highest, inverse, delta):
+def own_grads_of(qd, kv, stats):
     block_count, block, width = kv.shape
     one_spec = pl.BlockSpec((1, block, width), lambda n: (n, 0, 0))
-    stat_spec = pl.BlockSpec((1, block, 1), lambda n: (n, 0, 0))
     return pl.pallas_call(
         own_kernel,
         grid=(block_count,),
-        in_specs=[one_spec, one_spec, stat_spec, stat_spec, stat_spec],
+        in_specs=[one_spec, one_spec, one_spec],
         out_specs=one_spec,
         out_shape=jax.ShapeDtypeStruct((block_count, block, width), jnp.float32),
         compiler_params=pltpu.CompilerParams(dimension_semantics=("arbitrary",)),
         interpret=INTERPRET,
-    )(qd, kv, highest, inverse, delta)
+    )(qd, kv, stats)
 
 
 def attention(picks, qd, kv, left, right):
@@ -149,25 +147,21 @@
     right_spec = pl.BlockSpec((1, block, width), lambda n, p: (p[1, n], 0, 0))
     one_spec = pl.BlockSpec((1, block, width), lambda n, p: (n, 0, 0))
     whole_spec = pl.BlockSpec((block_count, block, width), lambda n, p: (0, 0, 0))
-    stat_spec = pl.BlockSpec((1, block, 1), lambda n, p: (n, 0, 0))
     chunks = block // width
     chunk_spec = pl.BlockSpec((chunks, width, width), lambda n, p: (n, 0, 0))
     shape = (block_count, block, width)
-    stat = jax.ShapeDtypeStruct((block_count, block, 1), jnp.float32)
     return pl.pallas_call(
         attention_kernel,
         grid_spec=pltpu.PrefetchScalarGridSpec(
             num_scalar_prefetch=1,
             grid=(block_count,),
             in_specs=[one_spec, one_spec, left_spec, right_spec],
-            out_specs=[chunk_spec, stat_spec, stat_spec, stat_spec, whole_spec, whole_spec],
+            out_specs=[chunk_spec, one_spec, whole_spec, whole_spec],
             scratch_shapes=[pltpu.VMEM(shape, jnp.float32), pltpu.VMEM(shape, jnp.float32)],
         ),
         out_shape=[
             jax.ShapeDtypeStruct((block_count * chunks, width, width), jnp.bfloat16),
-            stat,
-            stat,
-            stat,
+            jax.ShapeDtypeStruct(shape, jnp.float32),
             jax.ShapeDtypeStruct(shape, jnp.bfloat16),
             jax.ShapeDtypeStruct(shape, jnp.bfloat16),
         ],
@@ -193,10 +187,10 @@
     even = place % 2 == 0
     picks = jnp.stack([jnp.where(even, picks[1], picks[0]), jnp.where(even, picks[0], picks[1])])
     picks = jnp.clip(picks, 0, block_count - 1).astype(jnp.int32)
-    out_pair, highest, inverse, delta, to_near, to_far = attention(picks, qd, kv, near, far)
+    out_pair, stats, to_near, to_far = attention(picks, qd, kv, near, far)
     from_near = lax.ppermute(to_near, "blk", near_pairs).astype(jnp.float32)
     from_far = lax.ppermute(to_far, "blk", far_pairs).astype(jnp.float32)
-    own_grads = own_grads_of(qd, kv, highest, inverse, delta)
+    own_grads = own_grads_of(qd, kv, stats)
     query_grad, attended = to_rows(out_pair.transpose(0, 2, 1).reshape(row_count, width))
     kv_grads = (own_grads + from_near + from_far).astype(jnp.bfloat16)
     key_grad, value_grad = to_rows(kv_grads.reshape(row_count, width))

time: 133 us -> 133 us (level)
  transfers between devices with their start and end apart: 8 -> 8, of which waited for: 5 -> 5; matrix products, arithmetic and copies ran while one was open for 6% -> 5% of each run, Pallas kernels for 4% -> 4%
where the time goes in v11:
time: 133 us; the launch traced here: 132 us
  waiting for transfers between devices  48.1 us (36%)
  starting transfers between devices  47.5 us (36%)
  Pallas kernels  22.3 us (17%)
  local copies, waits for them, and re-layouts  9.89 us (7%)
  other arithmetic  3.74 us (3%)
    pallas_call x1, Pallas kernels, attention(): pl.pallas_call(attention_kernel, grid_spec=pltpu.PrefetchScalarGridSpec(n...  16.7 us
    all_to_all x2, starting transfers between devices, to_heads(): lax.all_to_all(packed, 'head', split_axis=1, concat_axis=0, tiled=True)  15.1 us
    all_to_all x2, waiting for transfers between devices, to_heads(): lax.all_to_all(packed, 'head', split_axis=1, concat_axis=0, tiled=True)  14.6 us
    all_to_all x2, starting transfers between devices, to_rows(): lax.all_to_all(packed, 'head', split_axis=0, concat_axis=1, tiled=True)  14.3 us
    ppermute x1, waiting for transfers between devices, shards(): from_far = lax.ppermute(to_far, 'blk', far_pairs).astype(jnp.float32)  12.5 us
    ppermute x1, waiting for transfers between devices, shards(): far = lax.ppermute(kv, 'blk', far_pairs)  11.3 us
    ppermute x1, starting transfers between devices, shards(): far = lax.ppermute(kv, 'blk', far_pairs)  10.9 us
    all_to_all x2, waiting for transfers between devices, to_rows(): lax.all_to_all(packed, 'head', split_axis=0, concat_axis=1, tiled=True)  9.75 us
  transfers between devices with their start and end apart: 8, of which 5 were waited for; matrix products, arithmetic and copies ran while one was open for 5% of the time, Pallas kernels for 4%

profile of v11, /device:TPU:8, one launch (start us, length us, event | category | flops | bytes accessed | tf_op | source)
XLA Modules:
  0.0 132.3 jit_solution(10742334258881504092)
XLA Ops:
  0.6 0.0 copy-start.3
  0.6 1.2 copy.20
  1.8 0.0 copy-done.3
  1.8 0.2 copy.21
  2.0 0.8 pad_maximum_fusion.1
  2.8 0.0 copy-start.4
  2.8 9.5 %all-to-all-start.1 = ((bf16[128,16,128]{0,2,1:T(8,128)(2,1)}), bf16[128,16,128]{0,2,1:T(8,128)(2,1)S(1)}, u32[]{:S(2)}, u32[]{:S(2)}) async-start(bf16[128,16,128]{0,2,1:T(8,128)(2,1)} %pad_maximum_fusion.1), calls=%async_computation.1 | async-start | bytes 1048576 | tf_op jit(solution)/shard_map/all_to_all | solution.py:18
  12.3 0.0 copy-done.4
  12.3 0.0 copy-start.5
  12.4 0.2 copy.17
  12.5 0.8 copy-done.5
  13.3 0.2 copy.18
  13.5 0.8 pad_maximum_fusion
  14.3 13.1 %all-to-all-done.1 = bf16[128,16,128]{0,2,1:T(8,128)(2,1)S(1)} async-done(((bf16[128,16,128]{0,2,1:T(8,128)(2,1)}), bf16[128,16,128]{0,2,1:T(8,128)(2,1)S(1)}, u32[]{:S(2)}, u32[]{:S(2)}) %all-to-all-start.1) | async-done | bytes 524320 | tf_op jit(solution)/shard_map/all_to_all | solution.py:18
  27.4 5.6 %all-to-all-start = ((bf16[128,16,128]{0,2,1:T(8,128)(2,1)}), bf16[128,16,128]{0,2,1:T(8,128)(2,1)S(1)}, u32[]{:S(2)}, u32[]{:S(2)}) async-start(bf16[128,16,128]{0,2,1:T(8,128)(2,1)} %pad_maximum_fusion), calls=%async_computation | async-start | bytes 1048576 | tf_op jit(solution)/shard_map/all_to_all | solution.py:18
  33.0 0.3 copy.22
  33.2 0.0 copy-start
  33.3 10.9 %collective-permute-start.1 = (bf16[4,512,128]{2,1,0:T(8,128)(2,1)S(1)}, bf16[4,512,128]{2,1,0:T(8,128)(2,1)S(1)}, u32[]{:S(2)}, u32[]{:S(2)}) collective-permute-start(bf16[4,512,128]{2,1,0:T(8,128)(2,1)S(1)} %bitcast.32), channel_id=1, source_target_pairs={{0,496},{16,32},{32,16},{48,64},{64,48},{80,96},{96,80},{112,128},... | collective-permute-start | bytes 1572872 | tf_op jit(solution)/shard_map/ppermute | solution.py:182
  44.2 1.9 %collective-permute-start = (bf16[4,512,128]{2,1,0:T(8,128)(2,1)S(1)}, bf16[4,512,128]{2,1,0:T(8,128)(2,1)S(1)}, u32[]{:S(2)}, u32[]{:S(2)}) collective-permute-start(bf16[4,512,128]{2,1,0:T(8,128)(2,1)S(1)} %bitcast.33), channel_id=1, source_target_pairs={{0,16},{16,0},{32,48},{48,32},{64,80},{80,64},{96,112},{112,96},{1... | collective-permute-start | bytes 1572872 | tf_op jit(solution)/shard_map/ppermute | solution.py:181
  46.1 0.0 copy-start.6
  46.1 0.7 copy-done.6
  46.8 0.1 fusion
  46.9 0.6 add_clamp_fusion.picks_ref
  47.5 1.5 %all-to-all-done = bf16[128,16,128]{0,2,1:T(8,128)(2,1)S(1)} async-done(((bf16[128,16,128]{0,2,1:T(8,128)(2,1)}), bf16[128,16,128]{0,2,1:T(8,128)(2,1)S(1)}, u32[]{:S(2)}, u32[]{:S(2)}) %all-to-all-start) | async-done | bytes 524320 | tf_op jit(solution)/shard_map/all_to_all | solution.py:18
  49.0 1.0 copy.19
  50.0 0.0 copy-done
  50.0 11.3 %collective-permute-done.1.right_ref = bf16[4,512,128]{2,1,0:T(8,128)(2,1)S(1)} collective-permute-done((bf16[4,512,128]{2,1,0:T(8,128)(2,1)S(1)}, bf16[4,512,128]{2,1,0:T(8,128)(2,1)S(1)}, u32[]{:S(2)}, u32[]{:S(2)}) %collective-permute-start.1) | collective-permute-done | bytes 524320 | tf_op jit(solution)/shard_map/ppermute | solution.py:182
  61.3 0.0 copy-start.1
  61.3 0.0 collective-permute-done.left_ref
  61.3 0.0 copy-start.2
  61.3 0.8 copy-done.1
  62.1 0.2 copy-done.2
  62.2 16.7 %shard_map.84 = (bf16[16,128,128]{2,1,0:T(8,128)(2,1)}, f32[4,512,128]{2,1,0:T(8,128)}, bf16[4,512,128]{2,1,0:T(8,128)(2,1)}, bf16[4,512,128]{2,1,0:T(8,128)(2,1)}) custom-call(s32[2,4]{1,0:T(2,128)} %add_clamp_fusion.picks_ref, bf16[4,512,128]{2,1,0:T(8,128)(2,1)} %bitcast.36, bf16[4,512,128]{2,1,0:T(8,128)(2,1)} %bitcast.34, ...), custom_call_target="tpu_custom_call" | custom-call | tf_op jit(solution)/shard_map/pallas_call | solution.py:153
  79.0 0.0 copy-start.8
  79.0 0.0 copy-start.7
  79.0 7.6 %all-to-all-start.2 = ((bf16[16,128,128]{1,2,0:T(8,128)(2,1)}), bf16[16,128,128]{1,2,0:T(8,128)(2,1)S(1)}, u32[]{:S(2)}, u32[]{:S(2)}) async-start(bf16[16,128,128]{1,2,0:T(8,128)(2,1)} %bitcast.51), calls=%async_computation.2 | async-start | bytes 1048576 | tf_op jit(solution)/shard_map/all_to_all | solution.py:25
  86.6 0.0 copy-done.8
  86.6 1.9 %collective-permute-start.2 = (bf16[4,512,128]{2,1,0:T(8,128)(2,1)S(1)}, bf16[4,512,128]{2,1,0:T(8,128)(2,1)S(1)}, u32[]{:S(2)}, u32[]{:S(2)}) collective-permute-start(bf16[4,512,128]{2,1,0:T(8,128)(2,1)S(1)} %copy-done.8), channel_id=1, source_target_pairs={{0,16},{16,0},{32,48},{48,32},{64,80},{80,64},{96,112},{112,96},{1... | collective-permute-start | bytes 1572872 | tf_op jit(solution)/shard_map/ppermute | solution.py:191
  88.5 0.0 copy-done.7
  88.5 3.3 %collective-permute-start.3 = (bf16[4,512,128]{2,1,0:T(8,128)(2,1)S(1)}, bf16[4,512,128]{2,1,0:T(8,128)(2,1)S(1)}, u32[]{:S(2)}, u32[]{:S(2)}) collective-permute-start(bf16[4,512,128]{2,1,0:T(8,128)(2,1)S(1)} %copy-done.7), channel_id=1, source_target_pairs={{0,496},{16,32},{32,16},{48,64},{64,48},{80,96},{96,80},{112,128},... | collective-permute-start | bytes 1572872 | tf_op jit(solution)/shard_map/ppermute | solution.py:192
  91.8 5.6 %shard_map.85 = f32[4,512,128]{2,1,0:T(8,128)} custom-call(bf16[4,512,128]{2,1,0:T(8,128)(2,1)} %bitcast.37, bf16[4,512,128]{2,1,0:T(8,128)(2,1)} %bitcast.35, f32[4,512,128]{2,1,0:T(8,128)} %get-tuple-element.9.stats_ref), custom_call_target="tpu_custom_call" | custom-call | tf_op jit(solution)/shard_map/pallas_call | solution.py:133
  97.4 0.0 collective-permute-done.2
  97.4 12.5 %collective-permute-done.3 = bf16[4,512,128]{2,1,0:T(8,128)(2,1)S(1)} collective-permute-done((bf16[4,512,128]{2,1,0:T(8,128)(2,1)S(1)}, bf16[4,512,128]{2,1,0:T(8,128)(2,1)S(1)}, u32[]{:S(2)}, u32[]{:S(2)}) %collective-permute-start.3) | collective-permute-done | bytes 524320 | tf_op jit(solution)/shard_map/ppermute | solution.py:192
  109.9 1.4 %add_convert_fusion = bf16[4,512,128]{2,1,0:T(8,128)(2,1)S(1)} fusion(bf16[4,512,128]{2,1,0:T(8,128)(2,1)S(1)} %collective-permute-done.3, f32[4,512,128]{2,1,0:T(8,128)} %shard_map.85, bf16[4,512,128]{2,1,0:T(8,128)(2,1)S(1)} %collective-permute-done.2), kind=kLoop, calls=%fused_computation | loop fusion | flops 1310720 | bytes 2621440 | tf_op jit(solution)/shard_map/convert_element_type | solution.py:195
  111.3 1.0 copy.25
  112.3 0.0 all-to-all-done.2
  112.3 6.7 %all-to-all-start.3 = ((bf16[16,128,128]{1,2,0:T(8,128)(2,1)}), bf16[16,128,128]{1,2,0:T(8,128)(2,1)S(1)}, u32[]{:S(2)}, u32[]{:S(2)}) async-start(bf16[16,128,128]{1,2,0:T(8,128)(2,1)} %copy.25), calls=%async_computation.3 | async-start | bytes 1048576 | tf_op jit(solution)/shard_map/all_to_all | solution.py:25
  119.1 0.9 copy.27
  120.0 0.8 copy.26
  120.8 9.7 %all-to-all-done.3 = bf16[16,128,128]{1,2,0:T(8,128)(2,1)S(1)} async-done(((bf16[16,128,128]{1,2,0:T(8,128)(2,1)}), bf16[16,128,128]{1,2,0:T(8,128)(2,1)S(1)}, u32[]{:S(2)}, u32[]{:S(2)}) %all-to-all-start.3) | async-done | bytes 524320 | tf_op jit(solution)/shard_map/all_to_all | solution.py:25
  130.6 0.9 copy.29
  131.4 0.8 copy.28
  (3 shorter events, 0.1 us)
Async XLA Ops:
  0.6 1.2 copy-start.3
  2.8 9.5 %copy-start.4 = (bf16[128,1024]{1,0:T(8,128)(2,1)S(1)}, bf16[128,1024]{1,0:T(8,128)(2,1)}, u32[]{:S(2)}) copy-start(bf16[128,1024]{1,0:T(8,128)(2,1)} %param.5) | copy-start | bytes 786436
  2.8 24.6 %all-to-all-start.1 = ((bf16[128,16,128]{0,2,1:T(8,128)(2,1)}), bf16[128,16,128]{0,2,1:T(8,128)(2,1)S(1)}, u32[]{:S(2)}, u32[]{:S(2)}) async-start(bf16[128,16,128]{0,2,1:T(8,128)(2,1)} %pad_maximum_fusion.1), calls=%async_computation.1 | async-start | bytes 1048576 | tf_op jit(solution)/shard_map/all_to_all | solution.py:18
  12.3 1.0 copy-start.5
  27.4 21.6 %all-to-all-start = ((bf16[128,16,128]{0,2,1:T(8,128)(2,1)}), bf16[128,16,128]{0,2,1:T(8,128)(2,1)S(1)}, u32[]{:S(2)}, u32[]{:S(2)}) async-start(bf16[128,16,128]{0,2,1:T(8,128)(2,1)} %pad_maximum_fusion), calls=%async_computation | async-start | bytes 1048576 | tf_op jit(solution)/shard_map/all_to_all | solution.py:18
  33.2 16.7 %copy-start = (bf16[16,128,1,128]{3,1,0,2:T(8,128)(2,1)}, bf16[16,128,1,128]{3,1,0,2:T(8,128)(2,1)S(1)}, u32[]{:S(2)}) copy-start(bf16[16,128,1,128]{3,1,0,2:T(8,128)(2,1)S(1)} %copy.22) | copy-start | bytes 1572868
  33.3 28.0 %collective-permute-start.1 = (bf16[4,512,128]{2,1,0:T(8,128)(2,1)S(1)}, bf16[4,512,128]{2,1,0:T(8,128)(2,1)S(1)}, u32[]{:S(2)}, u32[]{:S(2)}) collective-permute-start(bf16[4,512,128]{2,1,0:T(8,128)(2,1)S(1)} %bitcast.32), channel_id=1, source_target_pairs={{0,496},{16,32},{32,16},{48,64},{64,48},{80,96},{96,80},{112,128},... | collective-permute-start | bytes 1572872 | tf_op jit(solution)/shard_map/ppermute | solution.py:182
  44.2 17.1 %collective-permute-start = (bf16[4,512,128]{2,1,0:T(8,128)(2,1)S(1)}, bf16[4,512,128]{2,1,0:T(8,128)(2,1)S(1)}, u32[]{:S(2)}, u32[]{:S(2)}) collective-permute-start(bf16[4,512,128]{2,1,0:T(8,128)(2,1)S(1)} %bitcast.33), channel_id=1, source_target_pairs={{0,16},{16,0},{32,48},{48,32},{64,80},{80,64},{96,112},{112,96},{1... | collective-permute-start | bytes 1572872 | tf_op jit(solution)/shard_map/ppermute | solution.py:181
  46.1 0.7 copy-start.6
  61.3 0.8 copy-start.1
  61.3 1.0 copy-start.2
  79.0 7.6 %copy-start.8 = (bf16[4,512,128]{2,1,0:T(8,128)(2,1)S(1)}, bf16[4,512,128]{2,1,0:T(8,128)(2,1)}, u32[]{:S(2)}) copy-start(bf16[4,512,128]{2,1,0:T(8,128)(2,1)} %get-tuple-element.10) | copy-start | bytes 1572868
  79.0 9.5 %copy-start.7 = (bf16[4,512,128]{2,1,0:T(8,128)(2,1)S(1)}, bf16[4,512,128]{2,1,0:T(8,128)(2,1)}, u32[]{:S(2)}) copy-start(bf16[4,512,128]{2,1,0:T(8,128)(2,1)} %get-tuple-element.11) | copy-start | bytes 1572868
  79.0 33.4 %all-to-all-start.2 = ((bf16[16,128,128]{1,2,0:T(8,128)(2,1)}), bf16[16,128,128]{1,2,0:T(8,128)(2,1)S(1)}, u32[]{:S(2)}, u32[]{:S(2)}) async-start(bf16[16,128,128]{1,2,0:T(8,128)(2,1)} %bitcast.51), calls=%async_computation.2 | async-start | bytes 1048576 | tf_op jit(solution)/shard_map/all_to_all | solution.py:25
  86.6 10.8 %collective-permute-start.2 = (bf16[4,512,128]{2,1,0:T(8,128)(2,1)S(1)}, bf16[4,512,128]{2,1,0:T(8,128)(2,1)S(1)}, u32[]{:S(2)}, u32[]{:S(2)}) collective-permute-start(bf16[4,512,128]{2,1,0:T(8,128)(2,1)S(1)} %copy-done.8), channel_id=1, source_target_pairs={{0,16},{16,0},{32,48},{48,32},{64,80},{80,64},{96,112},{112,96},{1... | collective-permute-start | bytes 1572872 | tf_op jit(solution)/shard_map/ppermute | solution.py:191
  88.5 21.4 %collective-permute-start.3 = (bf16[4,512,128]{2,1,0:T(8,128)(2,1)S(1)}, bf16[4,512,128]{2,1,0:T(8,128)(2,1)S(1)}, u32[]{:S(2)}, u32[]{:S(2)}) collective-permute-start(bf16[4,512,128]{2,1,0:T(8,128)(2,1)S(1)} %copy-done.7), channel_id=1, source_target_pairs={{0,496},{16,32},{32,16},{48,64},{64,48},{80,96},{96,80},{112,128},... | collective-permute-start | bytes 1572872 | tf_op jit(solution)/shard_map/ppermute | solution.py:192
  112.3 18.2 %all-to-all-start.3 = ((bf16[16,128,128]{1,2,0:T(8,128)(2,1)}), bf16[16,128,128]{1,2,0:T(8,128)(2,1)S(1)}, u32[]{:S(2)}, u32[]{:S(2)}) async-start(bf16[16,128,128]{1,2,0:T(8,128)(2,1)} %copy.25), calls=%async_computation.3 | async-start | bytes 1048576 | tf_op jit(solution)/shard_map/all_to_all | solution.py:25
